TPU v7x, 256 devices: a whole 4x4x8 slice. The times are simulated.
256 devices in a mesh: dict: 16 (over x, z_hi, core), tensor: 16 (over z_lo, y).
Axes of the slice: x: 4, y: 4, z: 8 (z_hi: 2, z_lo: 4; z = z_hi * 4 + z_lo), core: 2. Of those that a mesh axis runs over, the one named last changes fastest.
Arguments:
- residual: bfloat16 [4096, 8192], P('dict', 'tensor'), may hold values from -10 to 10
- norm_gain: float32 [8192], replicated, may hold values from 0.1 to 1.9
- w_query: bfloat16 [8192, 8192], P('dict', 'tensor'), may hold values from -2 to 2
- w_key: bfloat16 [8192, 1024], P('dict'), may hold values from -2 to 2
- value_weight: bfloat16 [8192, 1024], P('dict'), may hold values from -0.0625 to 0.0625
- w_out: bfloat16 [8192, 8192], P('tensor', 'dict'), may hold values from -0.0625 to 0.0625
- decoder: bfloat16 [131072, 8192], P('dict', 'tensor'), may hold values from -0.5 to 0.5
- block_ids: int32 [2], replicated, may hold values from 0 to 1023, as said below
- latent_ids: int32 [4096, 64], P('dict'), may hold values from 0 to 131071, as said below
- latent_vals: float32 [4096, 64], P('dict'), may hold values from 0.5 to 4
- prompt_lens: int32 [16], P('dict'), may hold values from 32 to 256, as said below
Outputs:
- ablations: bfloat16 [2, 4096, 8192], P(None, 'dict', 'tensor')
Inputs may be any that keep to these rules, and one draw needn't show every extreme that they name: `block_ids`: 2 distinct blocks, one of them the last block; block b covers latents b * 128 to b * 128 + 127. `latent_ids`: about half of a row's entries name latents of the swept blocks; a row may name a latent more than once. Prompt p uses its first prompt_lens[p] rows; some prompt uses all 256 and some only 32.
All inputs are finite; a program needn't handle non-finite values.
Results may differ from a plain program's by a relative error of at most 0.009.
Values may be sent and summed in bfloat16 or wider, within the bound.
No kernel may reach another device: no remote copies, remote signals or barrier semaphores. Data moves between devices by JAX's collectives and lax.ppermute only.
A program may use at most 192 MiB of HBM per device.

v0:
```python
import math

import jax
import jax.numpy as jnp
from jax import lax
from jax.sharding import PartitionSpec as P

QUERY_HEADS = 64
KEY_VALUE_HEADS = 8
HEAD_SIZE = 128
BLOCK = 128
PROMPT_ROWS = 256
ABLATION_STEPS = 2


ROPE_BASE = 1000000.0
EPSILON = 1e-06
MASKED = -1e30


def spread(block, axis, source):
    block = jnp.where(lax.axis_index(axis) == source, block, jnp.zeros_like(block))
    return lax.psum(block, axis)


def rope_tables(length, head_dim):
    frequency = ROPE_BASE ** (-(jnp.arange(head_dim // 2, dtype=jnp.float32) * 2.0) / head_dim)
    angles = jnp.arange(length, dtype=jnp.float32)[:, None] * frequency[None, :]
    angles = jnp.concatenate([angles, angles], axis=-1)
    return (jnp.cos(angles), jnp.sin(angles))


def apply_rotary(feature_map, cosine_table, sine_table):
    half_width = feature_map.shape[-1] // 2
    first_half = feature_map[..., :half_width]
    second_half = feature_map[..., half_width:]
    turned = jnp.concatenate([-second_half, first_half], axis=-1)
    return feature_map * cosine_table + turned * sine_table


def dense_codes(latent_ids, latent_vals, first_latent):
    offsets = latent_ids - first_latent
    columns = jnp.arange(BLOCK, dtype=jnp.int32)
    matched = offsets[:, :, None] == columns[None, None, :]
    picked = jnp.where(matched, latent_vals[:, :, None], jnp.zeros((), jnp.float32))
    return jnp.sum(picked, axis=1).astype(jnp.bfloat16)


def owner_rows(decoder, block_num):
    lat_count = decoder.shape[0]
    first_latent = block_num * BLOCK
    owner_dict = first_latent // lat_count
    row_offset = first_latent - owner_dict * lat_count
    return (lax.dynamic_slice_in_dim(decoder, row_offset, BLOCK, 0), owner_dict)


def fetch_slice(decoder, block_num):
    dec_rows, owner_dict = owner_rows(decoder, block_num)
    return spread(dec_rows, "dict", owner_dict)


def body(
    residual,
    norm_gain,
    w_query,
    w_key,
    value_weight,
    w_out,
    decoder,
    block_ids,
    latent_ids,
    latent_vals,
    prompt_lens,
):
    row_count = residual.shape[0]
    col_count = residual.shape[1]
    tensor_pos = lax.axis_index("tensor")
    tensor_count = lax.axis_size("tensor")
    full_width = col_count * tensor_count
    coef_list = [
        dense_codes(latent_ids, latent_vals, block_ids[number] * BLOCK)
        for number in range(ABLATION_STEPS)
    ]
    col_list = []
    for number in range(ABLATION_STEPS):
        dec_slice = fetch_slice(decoder, block_ids[number])
        removed = jnp.dot(coef_list[number], dec_slice, preferred_element_type=jnp.float32)
        col_list.append((residual.astype(jnp.float32) - removed).astype(jnp.bfloat16))
    own_cols = jnp.stack(col_list)
    ablated = lax.all_gather(own_cols, "tensor", axis=2, tiled=True)
    widened = ablated.astype(jnp.float32)
    mean_sq = jnp.mean(widened * widened, axis=-1, keepdims=True)
    normed = (widened * lax.rsqrt(mean_sq + EPSILON) * norm_gain).astype(jnp.bfloat16)
    normed = normed.reshape(ABLATION_STEPS * row_count, full_width)
    head_cols = w_query.shape[1]
    heads_dev = head_cols // HEAD_SIZE
    query_group_size = QUERY_HEADS // KEY_VALUE_HEADS
    kv_index = tensor_pos * heads_dev // query_group_size
    key_cols = lax.dynamic_slice_in_dim(w_key, kv_index * HEAD_SIZE, HEAD_SIZE, 1)
    value_cols = lax.dynamic_slice_in_dim(value_weight, kv_index * HEAD_SIZE, HEAD_SIZE, 1)
    pieces = (
        lax.all_gather(w_query, "dict", axis=0, tiled=True),
        lax.all_gather(key_cols, "dict", axis=0, tiled=True),
        lax.all_gather(value_cols, "dict", axis=0, tiled=True),
    )
    query_vec, key_vector, value_vector = tuple(
        (jnp.dot(normed, w_part, preferred_element_type=jnp.float32) for w_part in pieces)
    )
    prompt_count = row_count // PROMPT_ROWS
    cosine_table, sine_table = rope_tables(PROMPT_ROWS, HEAD_SIZE)
    query_vec = apply_rotary(
        query_vec.reshape(ABLATION_STEPS, prompt_count, PROMPT_ROWS, heads_dev, HEAD_SIZE),
        cosine_table[:, None, :],
        sine_table[:, None, :],
    ).astype(jnp.bfloat16)
    key_vector = apply_rotary(
        key_vector.reshape(ABLATION_STEPS, prompt_count, PROMPT_ROWS, HEAD_SIZE),
        cosine_table,
        sine_table,
    ).astype(jnp.bfloat16)
    value_vector = value_vector.reshape(
        ABLATION_STEPS, prompt_count, PROMPT_ROWS, HEAD_SIZE
    ).astype(jnp.bfloat16)
    positions = jnp.arange(PROMPT_ROWS, dtype=jnp.int32)
    scores = jnp.einsum(
        "spqhd,spkd->sphqk", query_vec, key_vector, preferred_element_type=jnp.float32
    ) / math.sqrt(HEAD_SIZE)
    allowed = (positions[None, None, :] <= positions[None, :, None]) & (
        positions[None, None, :] < prompt_lens[:, None, None]
    )
    scores = jnp.where(allowed[None, :, None, :, :], scores, MASKED)
    weights = jax.nn.softmax(scores, axis=-1).astype(jnp.bfloat16)
    context = jnp.einsum(
        "sphqk,spkd->spqhd", weights, value_vector, preferred_element_type=jnp.float32
    )
    context = context.astype(jnp.bfloat16).reshape(ABLATION_STEPS * row_count, head_cols)
    partial_value = jnp.dot(
        context,
        lax.all_gather(w_out, "dict", axis=1, tiled=True),
        preferred_element_type=jnp.float32,
    ).astype(jnp.bfloat16)
    summed = lax.psum_scatter(
        partial_value.astype(jnp.float32).astype(jnp.bfloat16),
        "tensor",
        scatter_dimension=1,
        tiled=True,
    ).astype(jnp.float32)
    result = own_cols.reshape(ABLATION_STEPS * row_count, col_count).astype(jnp.float32) + summed
    return result.astype(jnp.bfloat16).reshape(ABLATION_STEPS, row_count, col_count)


def solution(mesh):
    in_specs = (
        P("dict", "tensor"),
        P(),
        P("dict", "tensor"),
        P("dict", None),
        P("dict", None),
        P("tensor", "dict"),
        P("dict", "tensor"),
        P(),
        P("dict", None),
        P("dict", None),
        P("dict"),
    )
    out_specs = P(None, "dict", "tensor")
    return jax.shard_map(body, mesh=mesh, in_specs=in_specs, out_specs=out_specs, check_vma=False)
```

profile of v0, /device:TPU:6, one launch (start us, length us, event | category | flops | bytes accessed | tf_op | source)
XLA Modules:
  0.0 760.2 jit_solution(15523512650847887386)
XLA Ops:
  6.5 1.4 fusion.43
  9.3 1.7 dynamic-slice_select_fusion.1
  11.0 0.9 broadcast_subtract_fusion
  12.1 0.9 copy.28
  13.0 7.8 %select_reduce_fusion.1 = (bf16[256,128]{1,0:T(8,128)(2,1)S(1)}, bf16[256,128]{1,0:T(8,128)(2,1)S(1)}) fusion(f32[256,64]{1,0:T(8,128)S(1)} %copy.28, s32[256,64]{1,0:T(8,128)S(1)} %copy.27, s32[256,64]{1,0:T(8,128)S(1)} %copy.29), kind=kLoop, calls=%fused_computation.8 | loop fusion | flops 12517376 | bytes 327680 | tf_op jit(solution)/shard_map/reduce_sum | solution.py:46
  20.9 161.9 %all-reduce.3.cloned.1.call-done = (bf16[128,512]{1,0:T(8,128)(2,1)}, bf16[128,512]{1,0:T(8,128)(2,1)}) async-done(((bf16[128,512]{1,0:T(8,128)(2,1)}, bf16[128,512]{1,0:T(8,128)(2,1)}), (bf16[128,512]{1,0:T(8,128)(2,1)}, bf16[128,512]{1,0:T(8,128)(2,1)})) %all-reduce.3.cloned.1.call-update) | async-done | bytes 262160 | tf_op jit(solution)/shard_map/psum | solution.py:23
  182.8 1.2 fusion.10
  184.1 1.2 fusion.9
  185.3 0.8 pad_maximum_fusion
  186.2 0.7 all-gather.12.cloned.1.call-update
  187.0 0.7 constant_dynamic-slice_fusion
  187.7 1.6 constant_dynamic-slice_fusion.1
  189.4 0.5 all-gather.14.cloned.1.call-update
  190.7 0.5 fusion.38
  191.3 107.4 %all-gather.6.cloned.1.call-done = bf16[2,256,8192]{2,1,0:T(8,128)(2,1)} async-done(((bf16[2,256,512]{2,1,0:T(8,128)(2,1)}), bf16[2,256,8192]{2,1,0:T(8,128)(2,1)}) %all-gather.6.cloned.1.call-update) | async-done | bytes 8388624 | tf_op jit(solution)/shard_map/all_gather | solution.py:90
  298.7 5.1 fusion
  303.8 9.9 %fusion.2 = bf16[2,256,8192]{2,1,0:T(8,128)(2,1)} fusion(bf16[2,256,8192]{2,1,0:T(8,128)(2,1)} %all-gather.6.cloned.1.call-done, f32[8192]{0:T(1024)S(1)} %copy-done.4, f32[2,256]{1,0:T(2,128)S(1)} %add_rsqrt_fusion), kind=kLoop, calls=%fused_computation.4 | loop fusion | flops 16777216 | bytes 16812032 | tf_op jit(solution)/shard_map/convert_element_type | solution.py:93
  313.7 91.1 %all-gather.12.cloned.1.call-done = bf16[8192,512]{1,0:T(8,128)(2,1)} async-done(((bf16[512,512]{1,0:T(8,128)(2,1)}), bf16[8192,512]{1,0:T(8,128)(2,1)}) %all-gather.12.cloned.1.call-update) | async-done | bytes 8388624 | tf_op jit(solution)/shard_map/all_gather | solution.py:102
  404.7 9.4 %fusion.46 = f32[512,512]{1,0:T(8,128)S(1)} fusion(bf16[512,8192]{1,0:T(8,128)(2,1)} %bitcast.72, bf16[8192,512]{1,0:T(8,128)(2,1)} %all-gather.12.cloned.1.call-done), kind=kOutput, calls=%fused_computation.72 | convolution fusion | flops 4294967296 | bytes 17825792 | tf_op jit(solution)/shard_map/dot_general | solution.py:107
  414.2 0.4 reshape.250
  414.6 1.4 reshape.249
  416.0 50.0 %all-gather.10.cloned.1.call-done = bf16[8192,128]{1,0:T(8,128)(2,1)} async-done(((bf16[512,128]{1,0:T(8,128)(2,1)}), bf16[8192,128]{1,0:T(8,128)(2,1)}) %all-gather.10.cloned.1.call-update) | async-done | bytes 2097168 | tf_op jit(solution)/shard_map/all_gather | solution.py:103
  466.0 6.4 fusion.45
  472.5 0.6 fusion.42
  473.4 0.9 fusion.44
  474.3 0.3 fusion.5
  474.6 52.3 %all-gather.8.cloned.1.call-done = bf16[8192,128]{1,0:T(8,128)(2,1)} async-done(((bf16[512,128]{1,0:T(8,128)(2,1)}), bf16[8192,128]{1,0:T(8,128)(2,1)}) %all-gather.8.cloned.1.call-update) | async-done | bytes 2097168 | tf_op jit(solution)/shard_map/all_gather | solution.py:104
  526.9 6.8 fusion.6
  534.0 103.3 %all-gather.14.cloned.1.call-done = bf16[512,8192]{1,0:T(8,128)(2,1)} async-done(((bf16[512,512]{1,0:T(8,128)(2,1)}), bf16[512,8192]{1,0:T(8,128)(2,1)}) %all-gather.14.cloned.1.call-update) | async-done | bytes 8388624 | tf_op jit(solution)/shard_map/all_gather | solution.py:139
  637.2 10.1 %convolution_convert_fusion = bf16[512,8192]{1,0:T(8,128)(2,1)} fusion(bf16[512,8192]{1,0:T(8,128)(2,1)} %all-gather.14.cloned.1.call-done, bf16[64,8,4,128]{3,2,1,0:T(4,128)(2,1)S(1)} %bitcast.76), kind=kOutput, calls=%fused_computation.5 | convolution fusion | flops 4299161600 | bytes 17301504 | tf_op jit(solution)/shard_map/dot_general | solution.py:137
  647.4 104.0 %reduce-scatter.2.cloned.1.call-done = bf16[512,512]{1,0:T(8,128)(2,1)} async-done(((bf16[512,8192]{1,0:T(8,128)(2,1)}), bf16[512,512]{1,0:T(8,128)(2,1)}) %reduce-scatter.2.cloned.1.call-update) | async-done | bytes 524304 | tf_op jit(solution)/shard_map/reduce_scatter | solution.py:142
  751.3 2.0 fusion.20
  (32 shorter events, 1.3 us)
Async XLA Ops:
  6.5 180.4 %copy-start = (bf16[512,1024]{1,0:T(8,128)(2,1)S(1)}, bf16[512,1024]{1,0:T(8,128)(2,1)}, u32[]{:S(2)}) copy-start(bf16[512,1024]{1,0:T(8,128)(2,1)} %param.14) | copy-start | bytes 3145732
  6.5 297.3 %copy-start.4 = (f32[8192]{0:T(1024)S(1)}, f32[8192]{0:T(1024)}, u32[]{:S(2)}) copy-start(f32[8192]{0:T(1024)} %param.12) | copy-start | bytes 98308
  6.5 176.3 %all-reduce.3.cloned.1.call-start = ((), (), s32[]{:S(2)}) async-start(), calls=%async_computation.7 | async-start | bytes 524288 | tf_op jit(solution)/shard_map/psum | solution.py:23
  11.0 287.7 %all-gather.6.cloned.1.call-start = ((), (), s32[]{:S(2)}) async-start(), calls=%async_computation.1 | async-start | bytes 8912896 | tf_op jit(solution)/shard_map/all_gather | solution.py:90
  186.2 218.6 %all-gather.12.cloned.1.call-start = ((), (), s32[]{:S(2)}) async-start(), calls=%async_computation.4 | async-start | bytes 8912896 | tf_op jit(solution)/shard_map/all_gather | solution.py:102
  186.9 279.1 %all-gather.10.cloned.1.call-start = ((), (), s32[]{:S(2)}) async-start(), calls=%async_computation.3 | async-start | bytes 2228224 | tf_op jit(solution)/shard_map/all_gather | solution.py:103
  187.7 339.2 %all-gather.8.cloned.1.call-start = ((), (), s32[]{:S(2)}) async-start(), calls=%async_computation.2 | async-start | bytes 2228224 | tf_op jit(solution)/shard_map/all_gather | solution.py:104
  189.3 447.9 %all-gather.14.cloned.1.call-start = ((), (), s32[]{:S(2)}) async-start(), calls=%async_computation.5 | async-start | bytes 8912896 | tf_op jit(solution)/shard_map/all_gather | solution.py:139
  189.9 561.4 %reduce-scatter.2.cloned.1.call-start = ((), (), s32[]{:S(2)}) async-start(), calls=%async_computation.6 | async-start | bytes 8912896 | tf_op jit(solution)/shard_map/reduce_scatter | solution.py:142
  466.0 7.4 copy-start.3
  637.2 116.1 %copy-start.1 = (bf16[512,1024]{1,0:T(8,128)(2,1)S(1)}, bf16[512,1024]{1,0:T(8,128)(2,1)}, u32[]{:S(2)}) copy-start(bf16[512,1024]{1,0:T(8,128)(2,1)} %param.14) | copy-start | bytes 3145732
  647.4 104.0 %copy-start.2 = (bf16[2,256,512]{2,1,0:T(8,128)(2,1)S(1)}, bf16[2,256,512]{2,1,0:T(8,128)(2,1)}, u32[]{:S(2)}) copy-start(bf16[2,256,512]{2,1,0:T(8,128)(2,1)} %pad_maximum_fusion) | copy-start | bytes 1572868
Sparse Core Ops, SparseCore 0:
  11.1 171.6 all-reduce.2
  186.3 112.3 all-gather.5
  301.4 103.2 all-gather.11
  407.3 58.6 all-gather.9
  468.5 58.3 all-gather.7
  529.3 107.8 all-gather.13
  647.5 103.7 reduce-scatter.1
where the time goes:
time: 761 us; the launch traced here: 760 us
  waiting for transfers between devices  671 us (88%)
  matrix products  36.2 us (5%)
  other arithmetic  29.6 us (4%)
  between operations  15.7 us (2%)
    psum x1, waiting for transfers between devices, spread(): return lax.psum(block, axis)  162 us
    all_gather x1, waiting for transfers between devices, body(): ablated = lax.all_gather(own_cols, 'tensor', axis=2, tiled=True)  107 us
    reduce_scatter x1, waiting for transfers between devices, body(): lax.psum_scatter(partial_value.astype(jnp.float32).astype(jnp.bfloat16),...  104 us
    all_gather x1, waiting for transfers between devices, body(): lax.all_gather(w_out, 'dict', axis=1, tiled=True)  103 us
    all_gather x1, waiting for transfers between devices, body(): lax.all_gather(w_query, 'dict', axis=0, tiled=True)  91.1 us
    all_gather x1, waiting for transfers between devices, body(): lax.all_gather(value_cols, 'dict', axis=0, tiled=True)  52.3 us
    all_gather x1, waiting for transfers between devices, body(): lax.all_gather(key_cols, 'dict', axis=0, tiled=True)  50 us
    dot_general x2, matrix products, body(): jnp.dot(normed, w_part, preferred_element_type=jnp.float32)  15.8 us
  transfers between devices with their start and end apart: 7, of which 7 were waited for; matrix products, arithmetic and copies ran while one was open for 7% of the time, Pallas kernels for 0%

commit v1 on v0

--- a/solution.py
+++ b/solution.py
@@ -16,11 +16,6 @@
 ROPE_BASE = 1000000.0
 EPSILON = 1e-06
 MASKED = -1e30
-
-
-def spread(block, axis, source):
-    block = jnp.where(lax.axis_index(axis) == source, block, jnp.zeros_like(block))
-    return lax.psum(block, axis)
 
 
 def rope_tables(length, head_dim):
@@ -54,9 +49,20 @@
     return (lax.dynamic_slice_in_dim(decoder, row_offset, BLOCK, 0), owner_dict)
 
 
-def fetch_slice(decoder, block_num):
-    dec_rows, owner_dict = owner_rows(decoder, block_num)
-    return spread(dec_rows, "dict", owner_dict)
+def fetch_blocks(decoder, block_ids):
+    dict_pos = lax.axis_index("dict")
+    dict_count = lax.axis_size("dict")
+    blocks = []
+    for number in range(ABLATION_STEPS):
+        dec_rows, owner_dict = owner_rows(decoder, block_ids[number])
+        blocks.append(jnp.where(dict_pos == owner_dict, dec_rows, jnp.zeros_like(dec_rows)))
+    held = jnp.stack(blocks)
+    step = 1
+    while step < dict_count:
+        pairs = [(i, i ^ step) for i in range(dict_count)]
+        held = held + lax.ppermute(held, "dict", pairs)
+        step *= 2
+    return held
 
 
 def body(
@@ -82,8 +88,9 @@
         for number in range(ABLATION_STEPS)
     ]
     col_list = []
+    dec_blocks = fetch_blocks(decoder, block_ids)
     for number in range(ABLATION_STEPS):
-        dec_slice = fetch_slice(decoder, block_ids[number])
+        dec_slice = dec_blocks[number]
         removed = jnp.dot(coef_list[number], dec_slice, preferred_element_type=jnp.float32)
         col_list.append((residual.astype(jnp.float32) - removed).astype(jnp.bfloat16))
     own_cols = jnp.stack(col_list)
@@ -98,14 +105,13 @@
     kv_index = tensor_pos * heads_dev // query_group_size
     key_cols = lax.dynamic_slice_in_dim(w_key, kv_index * HEAD_SIZE, HEAD_SIZE, 1)
     value_cols = lax.dynamic_slice_in_dim(value_weight, kv_index * HEAD_SIZE, HEAD_SIZE, 1)
-    pieces = (
-        lax.all_gather(w_query, "dict", axis=0, tiled=True),
-        lax.all_gather(key_cols, "dict", axis=0, tiled=True),
-        lax.all_gather(value_cols, "dict", axis=0, tiled=True),
-    )
-    query_vec, key_vector, value_vector = tuple(
-        (jnp.dot(normed, w_part, preferred_element_type=jnp.float32) for w_part in pieces)
-    )
+    packed = jnp.concatenate([w_query, key_cols, value_cols, w_out.T], axis=1)
+    gathered = lax.all_gather(packed, "dict", axis=0, tiled=True)
+    qkv_cols = head_cols + 2 * HEAD_SIZE
+    qkv = jnp.dot(normed, gathered[:, :qkv_cols], preferred_element_type=jnp.float32)
+    query_vec = qkv[:, :head_cols]
+    key_vector = qkv[:, head_cols : head_cols + HEAD_SIZE]
+    value_vector = qkv[:, head_cols + HEAD_SIZE : qkv_cols]
     prompt_count = row_count // PROMPT_ROWS
     cosine_table, sine_table = rope_tables(PROMPT_ROWS, HEAD_SIZE)
     query_vec = apply_rotary(
@@ -134,9 +140,10 @@
         "sphqk,spkd->spqhd", weights, value_vector, preferred_element_type=jnp.float32
     )
     context = context.astype(jnp.bfloat16).reshape(ABLATION_STEPS * row_count, head_cols)
-    partial_value = jnp.dot(
+    partial_value = lax.dot_general(
         context,
-        lax.all_gather(w_out, "dict", axis=1, tiled=True),
+        gathered[:, qkv_cols:],
+        (((1,), (1,)), ((), ())),
         preferred_element_type=jnp.float32,
     ).astype(jnp.bfloat16)
     summed = lax.psum_scatter(

time: 761 us -> 516 us (0.68)
  waiting for transfers between devices: 671 us -> 426 us
  matrix products: 36.2 us -> 25.8 us
  starting transfers between devices: 0.24 us -> 9.86 us
    psum x1 -> x0, waiting for transfers between devices: 162 us -> none  [spread(): return lax.psum(block, axis)]
    all_gather x4 -> x1, waiting for transfers between devices: 297 us -> 204 us  [body(): gathered = lax.all_gather(packed, 'dict', axis=0, tiled=True)]
    ppermute x0 -> x4, waiting for transfers between devices: none -> 14.1 us  [fetch_blocks(): held = held + lax.ppermute(held, 'dict', pairs)]
    ppermute x0 -> x4, starting transfers between devices: none -> 9.78 us  [fetch_blocks(): held = held + lax.ppermute(held, 'dict', pairs)]
    dot_general x3 -> x2, matrix products: 26 us -> 22 us  [the longest x1 11.9 us: body(): jnp.dot(normed, gathered[:, :qkv_cols], preferred_element_type=jnp.float32)]
  transfers between devices with their start and end apart: 7 -> 7, of which waited for: 7 -> 6; matrix products, arithmetic and copies ran while one was open for 7% -> 5% of each run, Pallas kernels for 0% -> 0%
where the time goes in v1:
time: 516 us
  waiting for transfers between devices  426 us (83%)
  other arithmetic  30.3 us (6%)
  matrix products  25.8 us (5%)
  between operations  15.4 us (3%)
  starting transfers between devices  9.86 us (2%)
  local copies, waits for them, and re-layouts  8.89 us (2%)
    all_gather x1, waiting for transfers between devices, body(): gathered = lax.all_gather(packed, 'dict', axis=0, tiled=True)  204 us
    all_gather x1, waiting for transfers between devices, body(): ablated = lax.all_gather(own_cols, 'tensor', axis=2, tiled=True)  104 us
    reduce_scatter x1, waiting for transfers between devices, body(): lax.psum_scatter(partial_value.astype(jnp.float32).astype(jnp.bfloat16),...  104 us
    ppermute x4, waiting for transfers between devices, fetch_blocks(): held = held + lax.ppermute(held, 'dict', pairs)  14.1 us
    dot_general x1, matrix products, body(): jnp.dot(normed, gathered[:, :qkv_cols], preferred_element_type=jnp.float32)  11.9 us
  transfers between devices with their start and end apart: 7, of which 6 were waited for; matrix products, arithmetic and copies ran while one was open for 5% of the time, Pallas kernels for 0%

profile of v1, /device:TPU:6, one launch (start us, length us, event | category | flops | bytes accessed | tf_op | source)
XLA Modules:
  0.0 515.8 jit_solution(17349654488387138816)
XLA Ops:
  6.5 1.4 fusion.37
  9.3 1.0 select_bitcast_fusion.1
  10.4 1.5 collective-permute-done
  12.0 7.3 %collective-permute-start.1 = (bf16[2,128,512]{2,1,0:T(8,128)(2,1)S(1)}, bf16[2,128,512]{2,1,0:T(8,128)(2,1)S(1)}, u32[]{:S(2)}, u32[]{:S(2)}) collective-permute-start(bf16[2,128,512]{2,1,0:T(8,128)(2,1)S(1)} %fusion.35), channel_id=1, source_target_pairs={{0,32},{16,48},{32,0},{48,16},{64,96},{80,112},{96,64},{112,80},{1... | collective-permute-start | bytes 786440 | tf_op jit(solution)/shard_map/ppermute | solution.py:63
  19.3 7.7 %collective-permute-done.1 = bf16[2,128,512]{2,1,0:T(8,128)(2,1)S(1)} collective-permute-done((bf16[2,128,512]{2,1,0:T(8,128)(2,1)S(1)}, bf16[2,128,512]{2,1,0:T(8,128)(2,1)S(1)}, u32[]{:S(2)}, u32[]{:S(2)}) %collective-permute-start.1) | collective-permute-done | bytes 262176 | tf_op jit(solution)/shard_map/ppermute | solution.py:63
  27.1 0.9 collective-permute-start.2
  28.0 0.8 broadcast_subtract_fusion
  29.0 0.9 copy.36
  30.0 4.8 collective-permute-done.2
  34.8 1.5 collective-permute-start.3
  36.3 7.8 %select_reduce_fusion.1 = (bf16[256,128]{1,0:T(8,128)(2,1)S(1)}, bf16[256,128]{1,0:T(8,128)(2,1)S(1)}) fusion(f32[256,64]{1,0:T(8,128)S(1)} %copy.36, s32[256,64]{1,0:T(8,128)S(1)} %copy.35, s32[256,64]{1,0:T(8,128)S(1)} %copy.37), kind=kLoop, calls=%fused_computation.11 | loop fusion | flops 12517376 | bytes 327680 | tf_op jit(solution)/shard_map/reduce_sum | solution.py:41
  44.3 1.2 fusion.11
  45.4 1.2 fusion.10
  46.6 0.8 pad_maximum_fusion.1
  47.5 1.0 constant_dynamic-slice_fusion
  49.0 1.2 pad_maximum_fusion
  51.0 0.5 fusion.31
  51.6 104.0 %all-gather.3.cloned.1.call-done = bf16[2,256,8192]{2,1,0:T(8,128)(2,1)} async-done(((bf16[2,256,512]{2,1,0:T(8,128)(2,1)}), bf16[2,256,8192]{2,1,0:T(8,128)(2,1)}) %all-gather.3.cloned.1.call-update) | async-done | bytes 8388624 | tf_op jit(solution)/shard_map/all_gather | solution.py:97
  155.6 5.1 fusion
  160.7 10.1 %fusion.2 = bf16[2,256,8192]{2,1,0:T(8,128)(2,1)} fusion(bf16[2,256,8192]{2,1,0:T(8,128)(2,1)} %all-gather.3.cloned.1.call-done, f32[8192]{0:T(1024)S(1)} %copy-done.4, f32[2,256]{1,0:T(2,128)S(1)} %add_rsqrt_fusion), kind=kLoop, calls=%fused_computation.4 | loop fusion | flops 16777216 | bytes 16812032 | tf_op jit(solution)/shard_map/convert_element_type | solution.py:100
  170.8 203.8 %all-gather.5.cloned.1.call-done = bf16[8192,1280]{0,1:T(8,128)(2,1)} async-done(((bf16[512,1280]{0,1:T(8,128)(2,1)}), bf16[8192,1280]{0,1:T(8,128)(2,1)}) %all-gather.5.cloned.1.call-update) | async-done | bytes 20971536 | tf_op jit(solution)/shard_map/all_gather | solution.py:109
  374.7 11.9 %fusion.3 = f32[512,768]{1,0:T(8,128)S(1)} fusion(bf16[512,8192]{1,0:T(8,128)(2,1)} %bitcast.68, bf16[8192,1280]{0,1:T(8,128)(2,1)} %all-gather.5.cloned.1.call-done), kind=kOutput, calls=%fused_computation.5 | convolution fusion | flops 6442450944 | bytes 22544384 | tf_op jit(solution)/shard_map/dot_general | solution.py:111
  386.6 1.2 copy-done.1
  387.9 0.4 reshape.250
  388.7 1.0 slice.59
  389.6 1.0 slice.79
  390.6 0.6 fusion.36
  391.5 0.9 fusion.38
  392.8 0.5 fusion.7
  393.6 10.1 %convolution_convert_fusion = bf16[512,8192]{1,0:T(8,128)(2,1)} fusion(bf16[8192,1280]{0,1:T(8,128)(2,1)} %all-gather.5.cloned.1.call-done, bf16[64,8,4,128]{3,2,1,0:T(4,128)(2,1)S(1)} %bitcast.73), kind=kOutput, calls=%fused_computation.7 | convolution fusion | flops 4299161600 | bytes 17301504 | tf_op jit(solution)/shard_map/dot_general | solution.py:143
  403.7 103.6 %reduce-scatter.2.cloned.1.call-done = bf16[512,512]{1,0:T(8,128)(2,1)} async-done(((bf16[512,8192]{1,0:T(8,128)(2,1)}), bf16[512,512]{1,0:T(8,128)(2,1)}) %reduce-scatter.2.cloned.1.call-update) | async-done | bytes 524304 | tf_op jit(solution)/shard_map/reduce_scatter | solution.py:149
  507.3 2.0 fusion.15
  (39 shorter events, 2.7 us)
Async XLA Ops:
  6.5 42.3 %copy-start.3 = (bf16[512,512]{1,0:T(8,128)(2,1)S(1)}, bf16[512,512]{1,0:T(8,128)(2,1)}, u32[]{:S(2)}) copy-start(bf16[512,512]{1,0:T(8,128)(2,1)} %param.13) | copy-start | bytes 1572868
  6.5 42.5 %copy-start.2 = (bf16[512,512]{1,0:T(8,128)(2,1)S(1)}, bf16[512,512]{1,0:T(8,128)(2,1)}, u32[]{:S(2)}) copy-start(bf16[512,512]{1,0:T(8,128)(2,1)} %param.16) | copy-start | bytes 1572868
  6.5 149.1 %all-gather.3.cloned.1.call-start = ((), (), s32[]{:S(2)}) async-start(), calls=%async_computation.1 | async-start | bytes 8912896 | tf_op jit(solution)/shard_map/all_gather | solution.py:97
  10.3 1.6 collective-permute-start
  12.0 15.0 %collective-permute-start.1 = (bf16[2,128,512]{2,1,0:T(8,128)(2,1)S(1)}, bf16[2,128,512]{2,1,0:T(8,128)(2,1)S(1)}, u32[]{:S(2)}, u32[]{:S(2)}) collective-permute-start(bf16[2,128,512]{2,1,0:T(8,128)(2,1)S(1)} %fusion.35), channel_id=1, source_target_pairs={{0,32},{16,48},{32,0},{48,16},{64,96},{80,112},{96,64},{112,80},{1... | collective-permute-start | bytes 786440 | tf_op jit(solution)/shard_map/ppermute | solution.py:63
  27.1 7.7 %collective-permute-start.2 = (bf16[2,128,512]{2,1,0:T(8,128)(2,1)S(1)}, bf16[2,128,512]{2,1,0:T(8,128)(2,1)S(1)}, u32[]{:S(2)}, u32[]{:S(2)}) collective-permute-start(bf16[2,128,512]{2,1,0:T(8,128)(2,1)S(1)} %fusion.43), channel_id=1, source_target_pairs={{0,64},{16,80},{32,96},{48,112},{64,0},{80,16},{96,32},{112,48},{1... | collective-permute-start | bytes 786440 | tf_op jit(solution)/shard_map/ppermute | solution.py:63
  34.8 9.3 %collective-permute-start.3 = (bf16[2,128,512]{2,1,0:T(8,128)(2,1)S(1)}, bf16[2,128,512]{2,1,0:T(8,128)(2,1)S(1)}, u32[]{:S(2)}, u32[]{:S(2)}) collective-permute-start(bf16[2,128,512]{2,1,0:T(8,128)(2,1)S(1)} %add.57), channel_id=1, source_target_pairs={{0,128},{16,144},{32,160},{48,176},{64,192},{80,208},{96,224},{112... | collective-permute-start | bytes 786440 | tf_op jit(solution)/shard_map/ppermute | solution.py:63
  46.6 114.1 %copy-start.4 = (f32[8192]{0:T(1024)S(1)}, f32[8192]{0:T(1024)}, u32[]{:S(2)}) copy-start(f32[8192]{0:T(1024)} %param.12) | copy-start | bytes 98308
  47.5 327.2 %all-gather.5.cloned.1.call-start = ((), (), s32[]{:S(2)}) async-start(), calls=%async_computation.2 | async-start | bytes 22282240 | tf_op jit(solution)/shard_map/all_gather | solution.py:109
  50.2 457.1 %reduce-scatter.2.cloned.1.call-start = ((), (), s32[]{:S(2)}) async-start(), calls=%async_computation.3 | async-start | bytes 8912896 | tf_op jit(solution)/shard_map/reduce_scatter | solution.py:149
  386.6 1.2 copy-start.1
  403.7 103.6 %copy-start = (bf16[2,256,512]{2,1,0:T(8,128)(2,1)S(1)}, bf16[2,256,512]{2,1,0:T(8,128)(2,1)}, u32[]{:S(2)}) copy-start(bf16[2,256,512]{2,1,0:T(8,128)(2,1)} %pad_maximum_fusion.1) | copy-start | bytes 1572868
Sparse Core Ops, SparseCore 0:
  47.6 107.9 all-gather.2
  158.2 216.4 all-gather.4
  403.9 103.4 reduce-scatter.1

commit v2 on v1

--- a/solution.py
+++ b/solution.py
@@ -63,6 +63,34 @@
         held = held + lax.ppermute(held, "dict", pairs)
         step *= 2
     return held
+
+
+def gather_tensor(own, axis):
+    count = lax.axis_size("tensor")
+    inner = 4 if count % 4 == 0 else 1
+    outer = count // inner
+    pos = lax.axis_index("tensor")
+    hi = pos // inner
+    lo = pos % inner
+    grid = []
+    for d_hi in range(outer):
+        row = []
+        for d_lo in range(inner):
+            if d_hi == 0 and d_lo == 0:
+                row.append(own)
+                continue
+            pairs = []
+            for src_pos in range(count):
+                dst_hi = (src_pos // inner - d_hi) % outer
+                dst_lo = (src_pos % inner - d_lo) % inner
+                pairs.append((src_pos, dst_hi * inner + dst_lo))
+            row.append(lax.ppermute(own, "tensor", pairs))
+        grid.append(jnp.stack(row))
+    grid = jnp.stack(grid)
+    grid = jnp.roll(grid, hi, axis=0)
+    grid = jnp.roll(grid, lo, axis=1)
+    grid = grid.reshape((count,) + own.shape)
+    return jnp.concatenate([grid[j] for j in range(count)], axis=axis)
 
 
 def body(
@@ -94,7 +122,7 @@
         removed = jnp.dot(coef_list[number], dec_slice, preferred_element_type=jnp.float32)
         col_list.append((residual.astype(jnp.float32) - removed).astype(jnp.bfloat16))
     own_cols = jnp.stack(col_list)
-    ablated = lax.all_gather(own_cols, "tensor", axis=2, tiled=True)
+    ablated = gather_tensor(own_cols, 2)
     widened = ablated.astype(jnp.float32)
     mean_sq = jnp.mean(widened * widened, axis=-1, keepdims=True)
     normed = (widened * lax.rsqrt(mean_sq + EPSILON) * norm_gain).astype(jnp.bfloat16)

time: 516 us -> 564 us (1.093)
  starting transfers between devices: 9.86 us -> 163 us
  waiting for transfers between devices: 426 us -> 289 us
  local copies, waits for them, and re-layouts: 8.89 us -> 32.6 us
  other arithmetic: 30.3 us -> 36.7 us
    all_gather x1, waiting for transfers between devices: 204 us -> 0.01 us  [body(): gathered = lax.all_gather(packed, 'dict', axis=0, tiled=True)]
    ppermute x0 -> x15, starting transfers between devices: none -> 153 us  [gather_tensor(): row.append(lax.ppermute(own, 'tensor', pairs))]
    ppermute x0 -> x15, waiting for transfers between devices: none -> 141 us  [gather_tensor(): row.append(lax.ppermute(own, 'tensor', pairs))]
    all_gather x1 -> x0, waiting for transfers between devices: 104 us -> none  [body(): ablated = lax.all_gather(own_cols, 'tensor', axis=2, tiled=True)]
    reduce_scatter x1, waiting for transfers between devices: 104 us -> 120 us  [body(): lax.psum_scatter(partial_value.astype(jnp.float32).astype(jnp.bfloat16),...]
    unnamed x15 -> x50, local copies, waits for them, and re-layouts: 2.64 us -> 16.9 us
    ppermute x4, waiting for transfers between devices: 14.1 us -> 28.2 us  [fetch_blocks(): held = held + lax.ppermute(held, 'dict', pairs)]
    unnamed x0 -> x8, other arithmetic: none -> 13.1 us
  transfers between devices with their start and end apart: 7 -> 21, of which waited for: 6 -> 12; matrix products, arithmetic and copies ran while one was open for 5% -> 10% of each run, Pallas kernels for 0% -> 0%
where the time goes in v2:
time: 564 us; the launch traced here: 563 us
  waiting for transfers between devices  289 us (51%)
  starting transfers between devices  163 us (29%)
  other arithmetic  36.7 us (7%)
  local copies, waits for them, and re-layouts  32.6 us (6%)
  matrix products  25.7 us (5%)
  between operations  15.8 us (3%)
    ppermute x15, starting transfers between devices, gather_tensor(): row.append(lax.ppermute(own, 'tensor', pairs))  153 us
    ppermute x15, waiting for transfers between devices, gather_tensor(): row.append(lax.ppermute(own, 'tensor', pairs))  141 us
    reduce_scatter x1, waiting for transfers between devices, body(): lax.psum_scatter(partial_value.astype(jnp.float32).astype(jnp.bfloat16),...  120 us
    ppermute x4, waiting for transfers between devices, fetch_blocks(): held = held + lax.ppermute(held, 'dict', pairs)  28.2 us
    unnamed x50, local copies, waits for them, and re-layouts  16.9 us
    dot_general x1, matrix products, body(): jnp.dot(normed, gathered[:, :qkv_cols], preferred_element_type=jnp.float32)  13.7 us
    unnamed x8, other arithmetic  13.1 us
  transfers between devices with their start and end apart: 21, of which 12 were waited for; matrix products, arithmetic and copies ran while one was open for 10% of the time, Pallas kernels for 0%

profile of v2, /device:TPU:6, one launch (start us, length us, event | category | flops | bytes accessed | tf_op | source)
XLA Modules:
  0.0 562.5 jit_solution(7581483109195606571)
XLA Ops:
  9.1 2.2 pad_maximum_fusion
  16.8 7.3 %collective-permute-start.1 = (bf16[2,128,512]{2,1,0:T(8,128)(2,1)S(1)}, bf16[2,128,512]{2,1,0:T(8,128)(2,1)S(1)}, u32[]{:S(2)}, u32[]{:S(2)}) collective-permute-start(bf16[2,128,512]{2,1,0:T(8,128)(2,1)S(1)} %fusion.43), channel_id=1, source_target_pairs={{0,32},{16,48},{32,0},{48,16},{64,96},{80,112},{96,64},{112,80},{1... | collective-permute-start | bytes 786440 | tf_op jit(solution)/shard_map/ppermute | solution.py:63
  24.1 16.4 %collective-permute-done.1 = bf16[2,128,512]{2,1,0:T(8,128)(2,1)S(1)} collective-permute-done((bf16[2,128,512]{2,1,0:T(8,128)(2,1)S(1)}, bf16[2,128,512]{2,1,0:T(8,128)(2,1)S(1)}, u32[]{:S(2)}, u32[]{:S(2)}) %collective-permute-start.1) | collective-permute-done | bytes 262176 | tf_op jit(solution)/shard_map/ppermute | solution.py:63
  41.8 10.3 %collective-permute-done.2 = bf16[2,128,512]{2,1,0:T(8,128)(2,1)S(1)} collective-permute-done((bf16[2,128,512]{2,1,0:T(8,128)(2,1)S(1)}, bf16[2,128,512]{2,1,0:T(8,128)(2,1)S(1)}, u32[]{:S(2)}, u32[]{:S(2)}) %collective-permute-start.2) | collective-permute-done | bytes 262176 | tf_op jit(solution)/shard_map/ppermute | solution.py:63
  52.1 1.9 collective-permute-start.3
  54.0 7.8 %select_reduce_fusion.1 = (bf16[256,128]{1,0:T(8,128)(2,1)S(1)}, bf16[256,128]{1,0:T(8,128)(2,1)S(1)}) fusion(f32[256,64]{1,0:T(8,128)S(1)} %copy.36, s32[256,64]{1,0:T(8,128)S(1)} %copy.35, s32[256,64]{1,0:T(8,128)S(1)} %copy.37), kind=kLoop, calls=%fused_computation.13 | loop fusion | flops 12517376 | bytes 327680 | tf_op jit(solution)/shard_map/reduce_sum | solution.py:41
  62.5 2.9 collective-permute-start.4
  68.0 5.0 collective-permute-start.8
  73.6 17.0 %collective-permute-done.4 = bf16[2,256,512]{2,1,0:T(8,128)(2,1)S(1)} collective-permute-done((bf16[2,256,512]{2,1,0:T(8,128)(2,1)S(1)}, bf16[2,256,512]{2,1,0:T(8,128)(2,1)S(1)}, u32[]{:S(2)}, u32[]{:S(2)}) %collective-permute-start.4) | collective-permute-done | bytes 524320 | tf_op jit(solution)/shard_map/ppermute | solution.py:87
  90.7 16.5 %collective-permute-start.10 = (bf16[2,256,512]{2,1,0:T(8,128)(2,1)S(1)}, bf16[2,256,512]{2,1,0:T(8,128)(2,1)S(1)}, u32[]{:S(2)}, u32[]{:S(2)}) collective-permute-start(bf16[2,256,512]{2,1,0:T(8,128)(2,1)S(1)} %get-tuple-element.28), channel_id=1, source_target_pairs={{0,13},{1,14},{2,15},{3,12},{4,1},{5,2},{6,3},{7,0},{8,5},{9,6},{1... | collective-permute-start | bytes 1572872 | tf_op jit(solution)/shard_map/ppermute | solution.py:87
  107.3 3.5 collective-permute-start.13
  110.9 27.9 %collective-permute-done.9 = bf16[2,256,512]{2,1,0:T(8,128)(2,1)S(1)} collective-permute-done((bf16[2,256,512]{2,1,0:T(8,128)(2,1)S(1)}, bf16[2,256,512]{2,1,0:T(8,128)(2,1)S(1)}, u32[]{:S(2)}, u32[]{:S(2)}) %collective-permute-start.9) | collective-permute-done | bytes 524320 | tf_op jit(solution)/shard_map/ppermute | solution.py:87
  138.8 2.3 collective-permute-start.14
  141.6 27.3 %collective-permute-done.10 = bf16[2,256,512]{2,1,0:T(8,128)(2,1)S(1)} collective-permute-done((bf16[2,256,512]{2,1,0:T(8,128)(2,1)S(1)}, bf16[2,256,512]{2,1,0:T(8,128)(2,1)S(1)}, u32[]{:S(2)}, u32[]{:S(2)}) %collective-permute-start.10) | collective-permute-done | bytes 524320 | tf_op jit(solution)/shard_map/ppermute | solution.py:87
  168.8 120.1 %collective-permute-start.15 = (bf16[2,256,512]{2,1,0:T(8,128)(2,1)S(1)}, bf16[2,256,512]{2,1,0:T(8,128)(2,1)S(1)}, u32[]{:S(2)}, u32[]{:S(2)}) collective-permute-start(bf16[2,256,512]{2,1,0:T(8,128)(2,1)S(1)} %get-tuple-element.28), channel_id=1, source_target_pairs={{0,4},{1,5},{2,6},{3,7},{4,8},{5,9},{6,10},{7,11},{8,12},{9,13},{1... | collective-permute-start | bytes 1572872 | tf_op jit(solution)/shard_map/ppermute | solution.py:87
  289.0 14.1 %collective-permute-done.11 = bf16[2,256,512]{2,1,0:T(8,128)(2,1)S(1)} collective-permute-done((bf16[2,256,512]{2,1,0:T(8,128)(2,1)S(1)}, bf16[2,256,512]{2,1,0:T(8,128)(2,1)S(1)}, u32[]{:S(2)}, u32[]{:S(2)}) %collective-permute-start.11) | collective-permute-done | bytes 524320 | tf_op jit(solution)/shard_map/ppermute | solution.py:87
  303.1 24.8 %collective-permute-done.12 = bf16[2,256,512]{2,1,0:T(8,128)(2,1)S(1)} collective-permute-done((bf16[2,256,512]{2,1,0:T(8,128)(2,1)S(1)}, bf16[2,256,512]{2,1,0:T(8,128)(2,1)S(1)}, u32[]{:S(2)}, u32[]{:S(2)}) %collective-permute-start.12) | collective-permute-done | bytes 524320 | tf_op jit(solution)/shard_map/ppermute | solution.py:87
  327.9 22.4 %collective-permute-done.13 = bf16[2,256,512]{2,1,0:T(8,128)(2,1)S(1)} collective-permute-done((bf16[2,256,512]{2,1,0:T(8,128)(2,1)S(1)}, bf16[2,256,512]{2,1,0:T(8,128)(2,1)S(1)}, u32[]{:S(2)}, u32[]{:S(2)}) %collective-permute-start.13) | collective-permute-done | bytes 524320 | tf_op jit(solution)/shard_map/ppermute | solution.py:87
  350.3 1.6 fusion.23
  351.9 2.6 fusion.21
  354.5 1.7 collective-permute-done.14
  356.2 1.6 fusion.19
  357.8 5.6 collective-permute-done.18
  366.5 2.6 fusion.22
  370.6 1.6 fusion.18
  372.2 7.4 %constant_dynamic-slice_fusion.2 = bf16[4,4,2,256,512]{4,3,2,1,0:T(8,128)(2,1)} fusion(bf16[8,4,2,256,512]{4,3,2,1,0:T(8,128)(2,1)} %fusion.18, s32[]{:T(128)S(6)} %select_n.89), kind=kLoop, calls=%fused_computation.115 | loop fusion | bytes 16777220 | tf_op jit(solution)/shard_map/jit(_roll_dynamic)/dynamic_slice | solution.py:90
  379.7 5.6 %fusion.2 = bf16[4,4,2,256,512]{4,3,2,1,0:T(8,128)(2,1)S(1)} fusion(s32[]{:T(128)S(6)} %select_n.92, bf16[4,4,2,256,512]{4,3,2,1,0:T(8,128)(2,1)} %constant_dynamic-slice_fusion.2), kind=kLoop, calls=%fused_computation.7 | loop fusion | flops 4194304 | bytes 16777220 | tf_op jit(solution)/shard_map/jit(_roll_dynamic)/concatenate | solution.py:91
  386.6 1.7 multiply_reduce_fusion
  403.3 13.7 %fusion = f32[512,768]{1,0:T(8,128)S(1)} fusion(bf16[8192,1280]{0,1:T(8,128)(2,1)} %all-gather.2.cloned.1.call-done, bf16[512,8192]{1,0:T(8,128)(2,1)} %constant_dynamic-update-slice_fusion, f32[8192]{0:T(1024)S(1)} %copy-done.6, f32[512]{0:T(512)S(1)} %bitcast.226), kind=kOutput, calls=%fused_computation.4 | convolution fusion | flops 6459228160 | bytes 22579200 | tf_op jit(solution)/shard_map/dot_general | solution.py:139
  423.9 10.1 %convolution_convert_fusion = bf16[512,8192]{1,0:T(8,128)(2,1)} fusion(bf16[8192,1280]{0,1:T(8,128)(2,1)} %all-gather.2.cloned.1.call-done, bf16[64,8,4,128]{3,2,1,0:T(4,128)(2,1)S(1)} %bitcast.224), kind=kOutput, calls=%fused_computation.6 | convolution fusion | flops 4299161600 | bytes 17301504 | tf_op jit(solution)/shard_map/dot_general | solution.py:171
  434.1 119.6 %reduce-scatter.2.cloned.1.call-done = bf16[512,512]{1,0:T(8,128)(2,1)} async-done(((bf16[512,8192]{1,0:T(8,128)(2,1)}), bf16[512,512]{1,0:T(8,128)(2,1)}) %reduce-scatter.2.cloned.1.call-update) | async-done | bytes 524304 | tf_op jit(solution)/shard_map/reduce_scatter | solution.py:177
  553.7 2.0 fusion.15
  (113 shorter events, 39.6 us)
Async XLA Ops:
  6.5 34.9 %copy-start.4 = (s32[256,64]{0,1:T(8,128)S(1)}, s32[256,64]{0,1:T(8,128)}, u32[]{:S(2)}) copy-start(s32[256,64]{0,1:T(8,128)} %param.19) | copy-start | bytes 196612
  6.5 35.1 %copy-start.5 = (f32[256,64]{0,1:T(8,128)S(1)}, f32[256,64]{0,1:T(8,128)}, u32[]{:S(2)}) copy-start(f32[256,64]{0,1:T(8,128)} %param.20) | copy-start | bytes 196612
  6.5 55.4 %copy-start.3 = (bf16[256,512]{1,0:T(8,128)(2,1)S(1)}, bf16[256,512]{1,0:T(8,128)(2,1)}, u32[]{:S(2)}) copy-start(bf16[256,512]{1,0:T(8,128)(2,1)} %param.11) | copy-start | bytes 786436
  6.5 396.7 %all-gather.2.cloned.1.call-start = ((), (), s32[]{:S(2)}) async-start(), calls=%async_computation.1 | async-start | bytes 22282240 | tf_op jit(solution)/shard_map/all_gather | solution.py:137
  11.3 542.4 %reduce-scatter.2.cloned.1.call-start = ((), (), s32[]{:S(2)}) async-start(), calls=%async_computation.2 | async-start | bytes 8912896 | tf_op jit(solution)/shard_map/reduce_scatter | solution.py:177
  15.1 1.6 collective-permute-start
  16.8 23.7 %collective-permute-start.1 = (bf16[2,128,512]{2,1,0:T(8,128)(2,1)S(1)}, bf16[2,128,512]{2,1,0:T(8,128)(2,1)S(1)}, u32[]{:S(2)}, u32[]{:S(2)}) collective-permute-start(bf16[2,128,512]{2,1,0:T(8,128)(2,1)S(1)} %fusion.43), channel_id=1, source_target_pairs={{0,32},{16,48},{32,0},{48,16},{64,96},{80,112},{96,64},{112,80},{1... | collective-permute-start | bytes 786440 | tf_op jit(solution)/shard_map/ppermute | solution.py:63
  40.5 11.5 %collective-permute-start.2 = (bf16[2,128,512]{2,1,0:T(8,128)(2,1)S(1)}, bf16[2,128,512]{2,1,0:T(8,128)(2,1)S(1)}, u32[]{:S(2)}, u32[]{:S(2)}) collective-permute-start(bf16[2,128,512]{2,1,0:T(8,128)(2,1)S(1)} %fusion.52), channel_id=1, source_target_pairs={{0,64},{16,80},{32,96},{48,112},{64,0},{80,16},{96,32},{112,48},{1... | collective-permute-start | bytes 786440 | tf_op jit(solution)/shard_map/ppermute | solution.py:63
  52.1 9.7 %collective-permute-start.3 = (bf16[2,128,512]{2,1,0:T(8,128)(2,1)S(1)}, bf16[2,128,512]{2,1,0:T(8,128)(2,1)S(1)}, u32[]{:S(2)}, u32[]{:S(2)}) collective-permute-start(bf16[2,128,512]{2,1,0:T(8,128)(2,1)S(1)} %add.82), channel_id=1, source_target_pairs={{0,128},{16,144},{32,160},{48,176},{64,192},{80,208},{96,224},{112... | collective-permute-start | bytes 786440 | tf_op jit(solution)/shard_map/ppermute | solution.py:63
  62.5 302.5 %copy-start = (bf16[2,256,512]{2,1,0:T(8,128)(2,1)}, bf16[2,256,512]{2,1,0:T(8,128)(2,1)S(1)}, u32[]{:S(2)}) copy-start(bf16[2,256,512]{2,1,0:T(8,128)(2,1)S(1)} %get-tuple-element.28) | copy-start | bytes 1572868
  62.5 28.2 %collective-permute-start.4 = (bf16[2,256,512]{2,1,0:T(8,128)(2,1)S(1)}, bf16[2,256,512]{2,1,0:T(8,128)(2,1)S(1)}, u32[]{:S(2)}, u32[]{:S(2)}) collective-permute-start(bf16[2,256,512]{2,1,0:T(8,128)(2,1)S(1)} %get-tuple-element.28), channel_id=1, source_target_pairs={{0,3},{1,0},{2,1},{3,2},{4,7},{5,4},{6,5},{7,6},{8,11},{9,8},{10,9... | collective-permute-start | bytes 1572872 | tf_op jit(solution)/shard_map/ppermute | solution.py:87
  65.4 25.3 %collective-permute-start.5 = (bf16[2,256,512]{2,1,0:T(8,128)(2,1)S(1)}, bf16[2,256,512]{2,1,0:T(8,128)(2,1)S(1)}, u32[]{:S(2)}, u32[]{:S(2)}) collective-permute-start(bf16[2,256,512]{2,1,0:T(8,128)(2,1)S(1)} %get-tuple-element.28), channel_id=1, source_target_pairs={{0,2},{1,3},{2,0},{3,1},{4,6},{5,7},{6,4},{7,5},{8,10},{9,11},{10,... | collective-permute-start | bytes 1572872 | tf_op jit(solution)/shard_map/ppermute | solution.py:87
  66.1 41.0 %collective-permute-start.6 = (bf16[2,256,512]{2,1,0:T(8,128)(2,1)S(1)}, bf16[2,256,512]{2,1,0:T(8,128)(2,1)S(1)}, u32[]{:S(2)}, u32[]{:S(2)}) collective-permute-start(bf16[2,256,512]{2,1,0:T(8,128)(2,1)S(1)} %get-tuple-element.28), channel_id=1, source_target_pairs={{0,1},{1,2},{2,3},{3,0},{4,5},{5,6},{6,7},{7,4},{8,9},{9,10},{10,1... | collective-permute-start | bytes 1572872 | tf_op jit(solution)/shard_map/ppermute | solution.py:87
  67.1 40.1 %collective-permute-start.7 = (bf16[2,256,512]{2,1,0:T(8,128)(2,1)S(1)}, bf16[2,256,512]{2,1,0:T(8,128)(2,1)S(1)}, u32[]{:S(2)}, u32[]{:S(2)}) collective-permute-start(bf16[2,256,512]{2,1,0:T(8,128)(2,1)S(1)} %get-tuple-element.28), channel_id=1, source_target_pairs={{0,12},{1,13},{2,14},{3,15},{4,0},{5,1},{6,2},{7,3},{8,4},{9,5},{1... | collective-permute-start | bytes 1572872 | tf_op jit(solution)/shard_map/ppermute | solution.py:87
  68.0 39.3 %collective-permute-start.8 = (bf16[2,256,512]{2,1,0:T(8,128)(2,1)S(1)}, bf16[2,256,512]{2,1,0:T(8,128)(2,1)}, u32[]{:S(2)}, u32[]{:S(2)}) collective-permute-start(bf16[2,256,512]{2,1,0:T(8,128)(2,1)S(1)} %get-tuple-element.28), channel_id=1, source_target_pairs={{0,15},{1,12},{2,13},{3,14},{4,3},{5,0},{6,1},{7,2},{8,7},{9,4},{1... | collective-permute-start | bytes 1572872 | tf_op jit(solution)/shard_map/ppermute | solution.py:87
  90.6 48.1 %collective-permute-start.9 = (bf16[2,256,512]{2,1,0:T(8,128)(2,1)S(1)}, bf16[2,256,512]{2,1,0:T(8,128)(2,1)S(1)}, u32[]{:S(2)}, u32[]{:S(2)}) collective-permute-start(bf16[2,256,512]{2,1,0:T(8,128)(2,1)S(1)} %get-tuple-element.28), channel_id=1, source_target_pairs={{0,14},{1,15},{2,12},{3,13},{4,2},{5,3},{6,0},{7,1},{8,6},{9,7},{1... | collective-permute-start | bytes 1572872 | tf_op jit(solution)/shard_map/ppermute | solution.py:87
  90.7 78.2 %collective-permute-start.10 = (bf16[2,256,512]{2,1,0:T(8,128)(2,1)S(1)}, bf16[2,256,512]{2,1,0:T(8,128)(2,1)S(1)}, u32[]{:S(2)}, u32[]{:S(2)}) collective-permute-start(bf16[2,256,512]{2,1,0:T(8,128)(2,1)S(1)} %get-tuple-element.28), channel_id=1, source_target_pairs={{0,13},{1,14},{2,15},{3,12},{4,1},{5,2},{6,3},{7,0},{8,5},{9,6},{1... | collective-permute-start | bytes 1572872 | tf_op jit(solution)/shard_map/ppermute | solution.py:87
  107.1 195.9 %collective-permute-start.11 = (bf16[2,256,512]{2,1,0:T(8,128)(2,1)S(1)}, bf16[2,256,512]{2,1,0:T(8,128)(2,1)S(1)}, u32[]{:S(2)}, u32[]{:S(2)}) collective-permute-start(bf16[2,256,512]{2,1,0:T(8,128)(2,1)S(1)} %get-tuple-element.28), channel_id=1, source_target_pairs={{0,8},{1,9},{2,10},{3,11},{4,12},{5,13},{6,14},{7,15},{8,0},{9,1},... | collective-permute-start | bytes 1572872 | tf_op jit(solution)/shard_map/ppermute | solution.py:87
  107.2 220.7 %collective-permute-start.12 = (bf16[2,256,512]{2,1,0:T(8,128)(2,1)S(1)}, bf16[2,256,512]{2,1,0:T(8,128)(2,1)S(1)}, u32[]{:S(2)}, u32[]{:S(2)}) collective-permute-start(bf16[2,256,512]{2,1,0:T(8,128)(2,1)S(1)} %get-tuple-element.28), channel_id=1, source_target_pairs={{0,11},{1,8},{2,9},{3,10},{4,15},{5,12},{6,13},{7,14},{8,3},{9,0},... | collective-permute-start | bytes 1572872 | tf_op jit(solution)/shard_map/ppermute | solution.py:87
  107.3 243.0 %collective-permute-start.13 = (bf16[2,256,512]{2,1,0:T(8,128)(2,1)S(1)}, bf16[2,256,512]{2,1,0:T(8,128)(2,1)S(1)}, u32[]{:S(2)}, u32[]{:S(2)}) collective-permute-start(bf16[2,256,512]{2,1,0:T(8,128)(2,1)S(1)} %get-tuple-element.28), channel_id=1, source_target_pairs={{0,10},{1,11},{2,8},{3,9},{4,14},{5,15},{6,12},{7,13},{8,2},{9,3},... | collective-permute-start | bytes 1572872 | tf_op jit(solution)/shard_map/ppermute | solution.py:87
  138.8 217.4 %collective-permute-start.14 = (bf16[2,256,512]{2,1,0:T(8,128)(2,1)S(1)}, bf16[2,256,512]{2,1,0:T(8,128)(2,1)S(1)}, u32[]{:S(2)}, u32[]{:S(2)}) collective-permute-start(bf16[2,256,512]{2,1,0:T(8,128)(2,1)S(1)} %get-tuple-element.28), channel_id=1, source_target_pairs={{0,9},{1,10},{2,11},{3,8},{4,13},{5,14},{6,15},{7,12},{8,1},{9,2},... | collective-permute-start | bytes 1572872 | tf_op jit(solution)/shard_map/ppermute | solution.py:87
  168.8 189.0 %collective-permute-start.15 = (bf16[2,256,512]{2,1,0:T(8,128)(2,1)S(1)}, bf16[2,256,512]{2,1,0:T(8,128)(2,1)S(1)}, u32[]{:S(2)}, u32[]{:S(2)}) collective-permute-start(bf16[2,256,512]{2,1,0:T(8,128)(2,1)S(1)} %get-tuple-element.28), channel_id=1, source_target_pairs={{0,4},{1,5},{2,6},{3,7},{4,8},{5,9},{6,10},{7,11},{8,12},{9,13},{1... | collective-permute-start | bytes 1572872 | tf_op jit(solution)/shard_map/ppermute | solution.py:87
  303.1 54.8 %collective-permute-start.16 = (bf16[2,256,512]{2,1,0:T(8,128)(2,1)S(1)}, bf16[2,256,512]{2,1,0:T(8,128)(2,1)S(1)}, u32[]{:S(2)}, u32[]{:S(2)}) collective-permute-start(bf16[2,256,512]{2,1,0:T(8,128)(2,1)S(1)} %get-tuple-element.28), channel_id=1, source_target_pairs={{0,7},{1,4},{2,5},{3,6},{4,11},{5,8},{6,9},{7,10},{8,15},{9,12},{1... | collective-permute-start | bytes 1572872 | tf_op jit(solution)/shard_map/ppermute | solution.py:87
  327.9 29.9 %collective-permute-start.17 = (bf16[2,256,512]{2,1,0:T(8,128)(2,1)S(1)}, bf16[2,256,512]{2,1,0:T(8,128)(2,1)S(1)}, u32[]{:S(2)}, u32[]{:S(2)}) collective-permute-start(bf16[2,256,512]{2,1,0:T(8,128)(2,1)S(1)} %get-tuple-element.28), channel_id=1, source_target_pairs={{0,6},{1,7},{2,4},{3,5},{4,10},{5,11},{6,8},{7,9},{8,14},{9,15},{1... | collective-permute-start | bytes 1572872 | tf_op jit(solution)/shard_map/ppermute | solution.py:87
  350.3 13.1 %collective-permute-start.18 = (bf16[2,256,512]{2,1,0:T(8,128)(2,1)S(1)}, bf16[2,256,512]{2,1,0:T(8,128)(2,1)S(1)}, u32[]{:S(2)}, u32[]{:S(2)}) collective-permute-start(bf16[2,256,512]{2,1,0:T(8,128)(2,1)S(1)} %get-tuple-element.28), channel_id=1, source_target_pairs={{0,5},{1,6},{2,7},{3,4},{4,9},{5,10},{6,11},{7,8},{8,13},{9,14},{1... | collective-permute-start | bytes 1572872 | tf_op jit(solution)/shard_map/ppermute | solution.py:87
  389.3 13.9 %copy-start.6 = (f32[8192]{0:T(1024)S(1)}, f32[8192]{0:T(1024)}, u32[]{:S(2)}) copy-start(f32[8192]{0:T(1024)} %param.12) | copy-start | bytes 98308
  416.9 1.2 copy-start.2
  434.1 119.7 %copy-start.1 = (bf16[2,256,512]{2,1,0:T(8,128)(2,1)S(1)}, bf16[2,256,512]{2,1,0:T(8,128)(2,1)}, u32[]{:S(2)}) copy-start(bf16[2,256,512]{2,1,0:T(8,128)(2,1)} %copy-done) | copy-start | bytes 1572868
Sparse Core Ops, SparseCore 0:
  11.5 284.5 all-gather.1
  434.2 119.4 reduce-scatter.1

commit v3 on v1

--- a/solution.py
+++ b/solution.py
@@ -83,6 +83,17 @@
     tensor_pos = lax.axis_index("tensor")
     tensor_count = lax.axis_size("tensor")
     full_width = col_count * tensor_count
+    head_cols = w_query.shape[1]
+    heads_dev = head_cols // HEAD_SIZE
+    query_group_size = QUERY_HEADS // KEY_VALUE_HEADS
+    kv_index = tensor_pos * heads_dev // query_group_size
+    assert 2 * heads_dev <= query_group_size
+    is_key_side = tensor_pos % 2 == 0
+    key_cols = lax.dynamic_slice_in_dim(w_key, kv_index * HEAD_SIZE, HEAD_SIZE, 1)
+    value_cols = lax.dynamic_slice_in_dim(value_weight, kv_index * HEAD_SIZE, HEAD_SIZE, 1)
+    kv_cols = jnp.where(is_key_side, key_cols, value_cols)
+    packed = jnp.concatenate([w_query, kv_cols, w_out.T], axis=1)
+    gathered = lax.all_gather(packed, "dict", axis=0, tiled=True)
     coef_list = [
         dense_codes(latent_ids, latent_vals, block_ids[number] * BLOCK)
         for number in range(ABLATION_STEPS)
@@ -94,24 +105,16 @@
         removed = jnp.dot(coef_list[number], dec_slice, preferred_element_type=jnp.float32)
         col_list.append((residual.astype(jnp.float32) - removed).astype(jnp.bfloat16))
     own_cols = jnp.stack(col_list)
+    own_cols, gathered = lax.optimization_barrier((own_cols, gathered))
     ablated = lax.all_gather(own_cols, "tensor", axis=2, tiled=True)
     widened = ablated.astype(jnp.float32)
     mean_sq = jnp.mean(widened * widened, axis=-1, keepdims=True)
     normed = (widened * lax.rsqrt(mean_sq + EPSILON) * norm_gain).astype(jnp.bfloat16)
     normed = normed.reshape(ABLATION_STEPS * row_count, full_width)
-    head_cols = w_query.shape[1]
-    heads_dev = head_cols // HEAD_SIZE
-    query_group_size = QUERY_HEADS // KEY_VALUE_HEADS
-    kv_index = tensor_pos * heads_dev // query_group_size
-    key_cols = lax.dynamic_slice_in_dim(w_key, kv_index * HEAD_SIZE, HEAD_SIZE, 1)
-    value_cols = lax.dynamic_slice_in_dim(value_weight, kv_index * HEAD_SIZE, HEAD_SIZE, 1)
-    packed = jnp.concatenate([w_query, key_cols, value_cols, w_out.T], axis=1)
-    gathered = lax.all_gather(packed, "dict", axis=0, tiled=True)
-    qkv_cols = head_cols + 2 * HEAD_SIZE
+    qkv_cols = head_cols + HEAD_SIZE
     qkv = jnp.dot(normed, gathered[:, :qkv_cols], preferred_element_type=jnp.float32)
     query_vec = qkv[:, :head_cols]
-    key_vector = qkv[:, head_cols : head_cols + HEAD_SIZE]
-    value_vector = qkv[:, head_cols + HEAD_SIZE : qkv_cols]
+    kv_vector = qkv[:, head_cols:qkv_cols]
     prompt_count = row_count // PROMPT_ROWS
     cosine_table, sine_table = rope_tables(PROMPT_ROWS, HEAD_SIZE)
     query_vec = apply_rotary(
@@ -119,14 +122,13 @@
         cosine_table[:, None, :],
         sine_table[:, None, :],
     ).astype(jnp.bfloat16)
-    key_vector = apply_rotary(
-        key_vector.reshape(ABLATION_STEPS, prompt_count, PROMPT_ROWS, HEAD_SIZE),
-        cosine_table,
-        sine_table,
-    ).astype(jnp.bfloat16)
-    value_vector = value_vector.reshape(
-        ABLATION_STEPS, prompt_count, PROMPT_ROWS, HEAD_SIZE
-    ).astype(jnp.bfloat16)
+    kv_vector = kv_vector.reshape(ABLATION_STEPS, prompt_count, PROMPT_ROWS, HEAD_SIZE)
+    kv_rotated = apply_rotary(kv_vector, cosine_table, sine_table)
+    own_kv = jnp.where(is_key_side, kv_rotated, kv_vector).astype(jnp.bfloat16)
+    tensor_pairs = [(i, i ^ 1) for i in range(tensor_count)]
+    other_kv = lax.ppermute(own_kv, "tensor", tensor_pairs)
+    key_vector = jnp.where(is_key_side, own_kv, other_kv)
+    value_vector = jnp.where(is_key_side, other_kv, own_kv)
     positions = jnp.arange(PROMPT_ROWS, dtype=jnp.int32)
     scores = jnp.einsum(
         "spqhd,spkd->sphqk", query_vec, key_vector, preferred_element_type=jnp.float32

time: 516 us -> 490 us (0.950)
  waiting for transfers between devices: 426 us -> 392 us
    all_gather x1, waiting for transfers between devices: 204 us -> 162 us  [body(): gathered = lax.all_gather(packed, 'dict', axis=0, tiled=True)]
    ppermute x4, waiting for transfers between devices: 14.1 us -> 26.6 us  [fetch_blocks(): held = held + lax.ppermute(held, 'dict', pairs)]
    all_gather x1, waiting for transfers between devices: 104 us -> 96.4 us  [body(): ablated = lax.all_gather(own_cols, 'tensor', axis=2, tiled=True)]
  transfers between devices with their start and end apart: 7 -> 8, of which waited for: 6 -> 7; matrix products, arithmetic and copies ran while one was open for 5% -> 4% of each run, Pallas kernels for 0% -> 0%
where the time goes in v3:
time: 490 us
  waiting for transfers between devices  392 us (80%)
  other arithmetic  32 us (7%)
  matrix products  28.3 us (6%)
  between operations  15.4 us (3%)
  local copies, waits for them, and re-layouts  11.3 us (2%)
  starting transfers between devices  10.9 us (2%)
    all_gather x1, waiting for transfers between devices, body(): gathered = lax.all_gather(packed, 'dict', axis=0, tiled=True)  162 us
    reduce_scatter x1, waiting for transfers between devices, body(): lax.psum_scatter(partial_value.astype(jnp.float32).astype(jnp.bfloat16),...  105 us
    all_gather x1, waiting for transfers between devices, body(): ablated = lax.all_gather(own_cols, 'tensor', axis=2, tiled=True)  96.4 us
    ppermute x4, waiting for transfers between devices, fetch_blocks(): held = held + lax.ppermute(held, 'dict', pairs)  26.6 us
    dot_general x1, matrix products, body(): jnp.dot(normed, gathered[:, :qkv_cols], preferred_element_type=jnp.float32)  14.9 us
    ppermute x4, starting transfers between devices, fetch_blocks(): held = held + lax.ppermute(held, 'dict', pairs)  10.3 us
    dot_general x1, matrix products, body(): lax.dot_general(context, gathered[:, qkv_cols:], (((1,), (1,)), ((), ()))...  10.1 us
    convert_element_type x1, other arithmetic, body(): (widened * lax.rsqrt(mean_sq + EPSILON) * norm_gain).astype(jnp.bfloat16)  9.89 us
  transfers between devices with their start and end apart: 8, of which 7 were waited for; matrix products, arithmetic and copies ran while one was open for 4% of the time, Pallas kernels for 0%

profile of v3, /device:TPU:6, one launch (start us, length us, event | category | flops | bytes accessed | tf_op | source)
XLA Modules:
  0.0 489.8 jit_solution(650572145126132683)
XLA Ops:
  6.5 1.0 constant_dynamic-slice_fusion
  7.8 1.3 copy.52
  9.1 2.1 pad_maximum_fusion
  11.3 1.4 fusion.39
  14.1 1.0 select_bitcast_fusion.1
  15.3 1.5 collective-permute-done
  16.9 7.3 %collective-permute-start.1 = (bf16[2,128,512]{2,1,0:T(8,128)(2,1)S(1)}, bf16[2,128,512]{2,1,0:T(8,128)(2,1)S(1)}, u32[]{:S(2)}, u32[]{:S(2)}) collective-permute-start(bf16[2,128,512]{2,1,0:T(8,128)(2,1)S(1)} %fusion.37), channel_id=1, source_target_pairs={{0,32},{16,48},{32,0},{48,16},{64,96},{80,112},{96,64},{112,80},{1... | collective-permute-start | bytes 786440 | tf_op jit(solution)/shard_map/ppermute | solution.py:63
  24.1 16.4 %collective-permute-done.1 = bf16[2,128,512]{2,1,0:T(8,128)(2,1)S(1)} collective-permute-done((bf16[2,128,512]{2,1,0:T(8,128)(2,1)S(1)}, bf16[2,128,512]{2,1,0:T(8,128)(2,1)S(1)}, u32[]{:S(2)}, u32[]{:S(2)}) %collective-permute-start.1) | collective-permute-done | bytes 262176 | tf_op jit(solution)/shard_map/ppermute | solution.py:63
  40.6 0.9 collective-permute-start.2
  41.8 8.6 %collective-permute-done.2 = bf16[2,128,512]{2,1,0:T(8,128)(2,1)S(1)} collective-permute-done((bf16[2,128,512]{2,1,0:T(8,128)(2,1)S(1)}, bf16[2,128,512]{2,1,0:T(8,128)(2,1)S(1)}, u32[]{:S(2)}, u32[]{:S(2)}) %collective-permute-start.2) | collective-permute-done | bytes 262176 | tf_op jit(solution)/shard_map/ppermute | solution.py:63
  50.5 2.0 collective-permute-start.3
  52.5 7.8 %select_reduce_fusion.1 = (bf16[256,128]{1,0:T(8,128)(2,1)S(1)}, bf16[256,128]{1,0:T(8,128)(2,1)S(1)}) fusion(f32[256,64]{1,0:T(8,128)S(1)} %copy.48, s32[256,64]{1,0:T(8,128)S(1)} %copy.47, s32[256,64]{1,0:T(8,128)S(1)} %copy.49), kind=kLoop, calls=%fused_computation.11 | loop fusion | flops 12517376 | bytes 327680 | tf_op jit(solution)/shard_map/reduce_sum | solution.py:41
  60.9 0.8 pad_maximum_fusion.1
  61.8 161.9 %all-gather.3.cloned.1.call-done = bf16[8192,1152]{0,1:T(8,128)(2,1)} async-done(((bf16[512,1152]{0,1:T(8,128)(2,1)}), bf16[8192,1152]{0,1:T(8,128)(2,1)}) %all-gather.3.cloned.1.call-update) | async-done | bytes 18874384 | tf_op jit(solution)/shard_map/all_gather | solution.py:96
  224.5 0.8 copy.61
  225.2 0.8 copy.57
  226.6 0.7 fusion.25
  227.4 96.4 %all-gather.5.cloned.1.call-done = bf16[2,256,8192]{2,1,0:T(8,128)(2,1)} async-done(((bf16[2,256,512]{2,1,0:T(8,128)(2,1)}), bf16[2,256,8192]{2,1,0:T(8,128)(2,1)}) %all-gather.5.cloned.1.call-update) | async-done | bytes 8388624 | tf_op jit(solution)/shard_map/all_gather | solution.py:109
  323.7 5.1 %fusion = f32[2,256]{1,0:T(2,128)S(1)} fusion(bf16[2,256,8192]{2,1,0:T(8,128)(2,1)} %all-gather.5.cloned.1.call-done), kind=kLoop, calls=%fused_computation.2 | loop fusion | flops 12582400 | bytes 8390656 | tf_op jit(solution)/shard_map/reduce_sum | solution.py:111
  328.8 9.9 %fusion.2 = bf16[2,256,8192]{2,1,0:T(8,128)(2,1)} fusion(bf16[2,256,8192]{2,1,0:T(8,128)(2,1)} %all-gather.5.cloned.1.call-done, f32[8192]{0:T(1024)S(1)} %copy-done.4, f32[2,256]{1,0:T(2,128)S(1)} %add_rsqrt_fusion), kind=kLoop, calls=%fused_computation.4 | loop fusion | flops 16777216 | bytes 16812032 | tf_op jit(solution)/shard_map/convert_element_type | solution.py:112
  338.7 14.9 %fusion.3 = f32[512,640]{1,0:T(8,128)S(1)} fusion(bf16[512,8192]{1,0:T(8,128)(2,1)} %bitcast.65, bf16[8192,1152]{0,1:T(8,128)(2,1)} %all-gather.3.cloned.1.call-done), kind=kOutput, calls=%fused_computation.6 | convolution fusion | flops 5368709120 | bytes 20185088 | tf_op jit(solution)/shard_map/dot_general | solution.py:115
  353.8 0.7 slice.52
  354.9 1.6 fusion.38
  356.5 1.1 copy.53
  358.0 1.3 fusion.14
  359.3 1.3 reshape.289
  360.7 2.3 collective-permute-done.4
  363.1 2.2 fusion.40
  365.6 0.6 fusion.7
  366.5 10.1 %convolution_convert_fusion = bf16[512,8192]{1,0:T(8,128)(2,1)} fusion(bf16[8192,1152]{0,1:T(8,128)(2,1)} %all-gather.3.cloned.1.call-done, bf16[64,8,4,128]{3,2,1,0:T(4,128)(2,1)S(1)} %bitcast.68), kind=kOutput, calls=%fused_computation.5 | convolution fusion | flops 4299161600 | bytes 17301504 | tf_op jit(solution)/shard_map/dot_general | solution.py:145
  376.6 104.7 %reduce-scatter.2.cloned.1.call-done = bf16[512,512]{1,0:T(8,128)(2,1)} async-done(((bf16[512,8192]{1,0:T(8,128)(2,1)}), bf16[512,512]{1,0:T(8,128)(2,1)}) %reduce-scatter.2.cloned.1.call-update) | async-done | bytes 524304 | tf_op jit(solution)/shard_map/reduce_scatter | solution.py:151
  481.3 2.0 fusion.15
  (45 shorter events, 3.7 us)
Async XLA Ops:
  6.5 35.0 %copy-start.2 = (f32[256,64]{0,1:T(8,128)S(1)}, f32[256,64]{0,1:T(8,128)}, u32[]{:S(2)}) copy-start(f32[256,64]{0,1:T(8,128)} %param.20) | copy-start | bytes 196612
  6.5 35.1 %copy-start.3 = (s32[256,64]{0,1:T(8,128)S(1)}, s32[256,64]{0,1:T(8,128)}, u32[]{:S(2)}) copy-start(s32[256,64]{0,1:T(8,128)} %param.19) | copy-start | bytes 196612
  6.5 53.9 %copy-start.1 = (bf16[256,512]{1,0:T(8,128)(2,1)S(1)}, bf16[256,512]{1,0:T(8,128)(2,1)}, u32[]{:S(2)}) copy-start(bf16[256,512]{1,0:T(8,128)(2,1)} %param.11) | copy-start | bytes 786436
  6.5 217.1 %all-gather.3.cloned.1.call-start = ((), (), s32[]{:S(2)}) async-start(), calls=%async_computation.1 | async-start | bytes 20054016 | tf_op jit(solution)/shard_map/all_gather | solution.py:96
  11.3 312.4 %all-gather.5.cloned.1.call-start = ((), (), s32[]{:S(2)}) async-start(), calls=%async_computation.2 | async-start | bytes 8912896 | tf_op jit(solution)/shard_map/all_gather | solution.py:109
  15.2 313.6 %copy-start.4 = (f32[8192]{0:T(1024)S(1)}, f32[8192]{0:T(1024)}, u32[]{:S(2)}) copy-start(f32[8192]{0:T(1024)} %param.12) | copy-start | bytes 98308
  15.2 1.6 collective-permute-start
  16.9 23.7 %collective-permute-start.1 = (bf16[2,128,512]{2,1,0:T(8,128)(2,1)S(1)}, bf16[2,128,512]{2,1,0:T(8,128)(2,1)S(1)}, u32[]{:S(2)}, u32[]{:S(2)}) collective-permute-start(bf16[2,128,512]{2,1,0:T(8,128)(2,1)S(1)} %fusion.37), channel_id=1, source_target_pairs={{0,32},{16,48},{32,0},{48,16},{64,96},{80,112},{96,64},{112,80},{1... | collective-permute-start | bytes 786440 | tf_op jit(solution)/shard_map/ppermute | solution.py:63
  40.6 9.9 %collective-permute-start.2 = (bf16[2,128,512]{2,1,0:T(8,128)(2,1)S(1)}, bf16[2,128,512]{2,1,0:T(8,128)(2,1)S(1)}, u32[]{:S(2)}, u32[]{:S(2)}) collective-permute-start(bf16[2,128,512]{2,1,0:T(8,128)(2,1)S(1)} %fusion.44), channel_id=1, source_target_pairs={{0,64},{16,80},{32,96},{48,112},{64,0},{80,16},{96,32},{112,48},{1... | collective-permute-start | bytes 786440 | tf_op jit(solution)/shard_map/ppermute | solution.py:63
  50.5 9.9 %collective-permute-start.3 = (bf16[2,128,512]{2,1,0:T(8,128)(2,1)S(1)}, bf16[2,128,512]{2,1,0:T(8,128)(2,1)S(1)}, u32[]{:S(2)}, u32[]{:S(2)}) collective-permute-start(bf16[2,128,512]{2,1,0:T(8,128)(2,1)S(1)} %add.66), channel_id=1, source_target_pairs={{0,128},{16,144},{32,160},{48,176},{64,192},{80,208},{96,224},{112... | collective-permute-start | bytes 786440 | tf_op jit(solution)/shard_map/ppermute | solution.py:63
  223.7 257.7 %reduce-scatter.2.cloned.1.call-start = ((), (), s32[]{:S(2)}) async-start(), calls=%async_computation.3 | async-start | bytes 8912896 | tf_op jit(solution)/shard_map/reduce_scatter | solution.py:151
  357.7 5.4 %collective-permute-start.4 = (bf16[2,1,256,128]{2,3,0,1:T(8,128)(2,1)S(1)}, bf16[2,1,256,128]{2,3,0,1:T(8,128)(2,1)S(1)}, u32[]{:S(2)}, u32[]{:S(2)}) collective-permute-start(bf16[2,1,256,128]{2,3,0,1:T(8,128)(2,1)S(1)} %fusion.24), channel_id=1, source_target_pairs={{0,1},{1,0},{2,3},{3,2},{4,5},{5,4},{6,7},{7,6},{8,9},{9,8},{10,11... | collective-permute-start | bytes 393224 | tf_op jit(solution)/shard_map/ppermute | solution.py:129
  376.6 104.7 %copy-start = (bf16[2,256,512]{2,1,0:T(8,128)(2,1)S(1)}, bf16[2,256,512]{2,1,0:T(8,128)(2,1)}, u32[]{:S(2)}) copy-start(bf16[2,256,512]{2,1,0:T(8,128)(2,1)} %pad_maximum_fusion.1) | copy-start | bytes 1572868
Sparse Core Ops, SparseCore 0:
  11.4 212.1 all-gather.2
  225.4 98.2 all-gather.4
  376.8 104.5 reduce-scatter.1

commit v4 on v3

--- a/solution.py
+++ b/solution.py
@@ -49,9 +49,29 @@
     return (lax.dynamic_slice_in_dim(decoder, row_offset, BLOCK, 0), owner_dict)
 
 
+DICT = ("dict_hi", "core")
+
+
+def dict_index():
+    return lax.axis_index("dict_hi") * lax.axis_size("core") + lax.axis_index("core")
+
+
+def dict_size():
+    return lax.axis_size("dict_hi") * lax.axis_size("core")
+
+
+def butterfly_sum(value, axis, count):
+    step = 1
+    while step < count:
+        pairs = [(i, i ^ step) for i in range(count)]
+        value = value + lax.ppermute(value, axis, pairs)
+        step *= 2
+    return value
+
+
 def fetch_blocks(decoder, block_ids):
-    dict_pos = lax.axis_index("dict")
-    dict_count = lax.axis_size("dict")
+    dict_pos = dict_index()
+    dict_count = dict_size()
     blocks = []
     for number in range(ABLATION_STEPS):
         dec_rows, owner_dict = owner_rows(decoder, block_ids[number])
@@ -60,7 +80,7 @@
     step = 1
     while step < dict_count:
         pairs = [(i, i ^ step) for i in range(dict_count)]
-        held = held + lax.ppermute(held, "dict", pairs)
+        held = held + lax.ppermute(held, DICT, pairs)
         step *= 2
     return held
 
@@ -93,7 +113,7 @@
     value_cols = lax.dynamic_slice_in_dim(value_weight, kv_index * HEAD_SIZE, HEAD_SIZE, 1)
     kv_cols = jnp.where(is_key_side, key_cols, value_cols)
     packed = jnp.concatenate([w_query, kv_cols, w_out.T], axis=1)
-    gathered = lax.all_gather(packed, "dict", axis=0, tiled=True)
+    own_half = lax.all_gather(packed, "dict_hi", axis=0, tiled=False)
     coef_list = [
         dense_codes(latent_ids, latent_vals, block_ids[number] * BLOCK)
         for number in range(ABLATION_STEPS)
@@ -105,11 +125,26 @@
         removed = jnp.dot(coef_list[number], dec_slice, preferred_element_type=jnp.float32)
         col_list.append((residual.astype(jnp.float32) - removed).astype(jnp.bfloat16))
     own_cols = jnp.stack(col_list)
-    own_cols, gathered = lax.optimization_barrier((own_cols, gathered))
-    ablated = lax.all_gather(own_cols, "tensor", axis=2, tiled=True)
-    widened = ablated.astype(jnp.float32)
-    mean_sq = jnp.mean(widened * widened, axis=-1, keepdims=True)
-    normed = (widened * lax.rsqrt(mean_sq + EPSILON) * norm_gain).astype(jnp.bfloat16)
+    widened = own_cols.astype(jnp.float32)
+    sum_sq = butterfly_sum(jnp.sum(widened * widened, axis=-1, keepdims=True), "tensor", tensor_count)
+    mean_sq = sum_sq / full_width
+    gain_cols = lax.dynamic_slice_in_dim(norm_gain, tensor_pos * col_count, col_count)
+    normed_cols = (widened * lax.rsqrt(mean_sq + EPSILON) * gain_cols).astype(jnp.bfloat16)
+    normed_cols, own_half = lax.optimization_barrier((normed_cols, own_half))
+    core_count = lax.axis_size("core")
+    core_pos = lax.axis_index("core")
+    halves = [own_half]
+    for shift in range(1, core_count):
+        core_pairs = [(i, (i + shift) % core_count) for i in range(core_count)]
+        halves.append(lax.ppermute(own_half, "core", core_pairs))
+    ordered = []
+    for core_id in range(core_count):
+        pick = halves[0]
+        for k in range(1, core_count):
+            pick = jnp.where((core_pos - k) % core_count == core_id, halves[k], pick)
+        ordered.append(pick)
+    gathered = jnp.stack(ordered, axis=1).reshape(-1, packed.shape[1])
+    normed = lax.all_gather(normed_cols, "tensor", axis=2, tiled=True)
     normed = normed.reshape(ABLATION_STEPS * row_count, full_width)
     qkv_cols = head_cols + HEAD_SIZE
     qkv = jnp.dot(normed, gathered[:, :qkv_cols], preferred_element_type=jnp.float32)
@@ -159,18 +194,22 @@
 
 
 def solution(mesh):
+    dict_count = mesh.shape["dict"]
+    core_count = 2 if dict_count % 2 == 0 else 1
+    devices = mesh.devices.reshape(dict_count // core_count, core_count, mesh.shape["tensor"])
+    fine = jax.sharding.Mesh(devices, ("dict_hi", "core", "tensor"))
     in_specs = (
-        P("dict", "tensor"),
+        P(DICT, "tensor"),
         P(),
-        P("dict", "tensor"),
-        P("dict", None),
-        P("dict", None),
-        P("tensor", "dict"),
-        P("dict", "tensor"),
+        P(DICT, "tensor"),
+        P(DICT, None),
+        P(DICT, None),
+        P("tensor", DICT),
+        P(DICT, "tensor"),
         P(),
-        P("dict", None),
-        P("dict", None),
-        P("dict"),
+        P(DICT, None),
+        P(DICT, None),
+        P(DICT),
     )
-    out_specs = P(None, "dict", "tensor")
-    return jax.shard_map(body, mesh=mesh, in_specs=in_specs, out_specs=out_specs, check_vma=False)
+    out_specs = P(None, DICT, "tensor")
+    return jax.shard_map(body, mesh=fine, in_specs=in_specs, out_specs=out_specs, check_vma=False)

time: 490 us -> 481 us (0.982)
  waiting for transfers between devices: 392 us -> 358 us
  local copies, waits for them, and re-layouts: 11.3 us -> 24.2 us
  starting transfers between devices: 10.9 us -> 21.5 us
    all_gather x2, waiting for transfers between devices: 258 us -> 207 us  [the longest x1 140 us: body(): own_half = lax.all_gather(packed, 'dict_hi', axis=0, tiled=False)]
    ppermute x4 -> x9, waiting for transfers between devices: 26.6 us -> 46.1 us  [the longest x4 26.6 us: fetch_blocks(): held = held + lax.ppermute(held, DICT, pairs)]
    another operation x1 -> x2, other arithmetic: 0.84 us -> 16.2 us  [body(): gathered = jnp.stack(ordered, axis=1).reshape(-1, packed.shape[1])]
    all_gather x0 -> x1, local copies, waits for them, and re-layouts: none -> 12.7 us  [body(): own_half = lax.all_gather(packed, 'dict_hi', axis=0, tiled=False)]
    ppermute x4 -> x9, starting transfers between devices: 10.3 us -> 21.3 us  [the longest x4 10.7 us: butterfly_sum(): value = value + lax.ppermute(value, axis, pairs)]
    convert_element_type x1 -> x2, other arithmetic: 9.89 us -> 1.06 us  [the longest x1 0.99 us: body(): (widened * lax.rsqrt(mean_sq + EPSILON) * gain_cols).astype(jnp.bfloat16)]
    reduce_sum x1, other arithmetic: 5.1 us -> 0.18 us  [body(): jnp.sum(widened * widened, axis=-1, keepdims=True)]
  transfers between devices with their start and end apart: 8 -> 13, of which waited for: 7 -> 12; matrix products, arithmetic and copies ran while one was open for 4% -> 7% of each run, Pallas kernels for 0% -> 0%
where the time goes in v4:
time: 481 us; the launch traced here: 480 us
  waiting for transfers between devices  358 us (74%)
  other arithmetic  32.5 us (7%)
  matrix products  28.5 us (6%)
  local copies, waits for them, and re-layouts  24.2 us (5%)
  starting transfers between devices  21.5 us (4%)
  between operations  15.4 us (3%)
    all_gather x1, waiting for transfers between devices, body(): own_half = lax.all_gather(packed, 'dict_hi', axis=0, tiled=False)  140 us
    reduce_scatter x1, waiting for transfers between devices, body(): lax.psum_scatter(partial_value.astype(jnp.float32).astype(jnp.bfloat16),...  104 us
    all_gather x1, waiting for transfers between devices, body(): normed = lax.all_gather(normed_cols, 'tensor', axis=2, tiled=True)  66.9 us
    ppermute x4, waiting for transfers between devices, fetch_blocks(): held = held + lax.ppermute(held, DICT, pairs)  26.6 us
    another operation x2, other arithmetic, body(): gathered = jnp.stack(ordered, axis=1).reshape(-1, packed.shape[1])  16.2 us
    dot_general x1, matrix products, body(): jnp.dot(normed, gathered[:, :qkv_cols], preferred_element_type=jnp.float32)  14.5 us
    all_gather x1, local copies, waits for them, and re-layouts, body(): own_half = lax.all_gather(packed, 'dict_hi', axis=0, tiled=False)  12.7 us
    ppermute x1, waiting for transfers between devices, body(): halves.append(lax.ppermute(own_half, 'core', core_pairs))  11.5 us
  transfers between devices with their start and end apart: 13, of which 12 were waited for; matrix products, arithmetic and copies ran while one was open for 7% of the time, Pallas kernels for 0%

profile of v4, /device:TPU:6, one launch (start us, length us, event | category | flops | bytes accessed | tf_op | source)
XLA Modules:
  0.0 480.2 jit_solution(7442471102292123059)
XLA Ops:
  7.8 1.3 copy.54
  9.1 2.1 pad_maximum_fusion.1
  11.3 1.4 fusion.36
  15.2 1.5 collective-permute-done
  16.8 7.3 %collective-permute-start.1 = (bf16[2,128,512]{2,1,0:T(8,128)(2,1)S(1)}, bf16[2,128,512]{2,1,0:T(8,128)(2,1)S(1)}, u32[]{:S(2)}, u32[]{:S(2)}) collective-permute-start(bf16[2,128,512]{2,1,0:T(8,128)(2,1)S(1)} %fusion.34), channel_id=1, source_target_pairs={{0,32},{16,48},{32,0},{48,16},{64,96},{80,112},{96,64},{112,80},{1... | collective-permute-start | bytes 786440 | tf_op jit(solution)/shard_map/ppermute | solution.py:83
  24.1 16.4 %collective-permute-done.1 = bf16[2,128,512]{2,1,0:T(8,128)(2,1)S(1)} collective-permute-done((bf16[2,128,512]{2,1,0:T(8,128)(2,1)S(1)}, bf16[2,128,512]{2,1,0:T(8,128)(2,1)S(1)}, u32[]{:S(2)}, u32[]{:S(2)}) %collective-permute-start.1) | collective-permute-done | bytes 262176 | tf_op jit(solution)/shard_map/ppermute | solution.py:83
  41.8 8.7 %collective-permute-done.2 = bf16[2,128,512]{2,1,0:T(8,128)(2,1)S(1)} collective-permute-done((bf16[2,128,512]{2,1,0:T(8,128)(2,1)S(1)}, bf16[2,128,512]{2,1,0:T(8,128)(2,1)S(1)}, u32[]{:S(2)}, u32[]{:S(2)}) %collective-permute-start.2) | collective-permute-done | bytes 262176 | tf_op jit(solution)/shard_map/ppermute | solution.py:83
  50.5 2.0 collective-permute-start.3
  52.6 7.8 %select_reduce_fusion.1 = (bf16[256,128]{1,0:T(8,128)(2,1)S(1)}, bf16[256,128]{1,0:T(8,128)(2,1)S(1)}) fusion(f32[256,64]{1,0:T(8,128)S(1)} %copy.50, s32[256,64]{1,0:T(8,128)S(1)} %copy.49, s32[256,64]{1,0:T(8,128)S(1)} %copy.51), kind=kLoop, calls=%fused_computation.9 | loop fusion | flops 12517376 | bytes 327680 | tf_op jit(solution)/shard_map/reduce_sum | solution.py:41
  61.1 1.6 collective-permute-start.4
  62.7 2.1 collective-permute-done.4
  64.8 3.0 collective-permute-start.5
  67.8 2.1 collective-permute-done.5
  69.9 4.6 collective-permute-start.6
  74.5 1.6 collective-permute-done.6
  76.1 1.5 collective-permute-start.7
  78.3 2.2 collective-permute-done.7
  81.6 139.9 %all-gather.6.cloned.1.call-done = bf16[4096,1152]{0,1:T(8,128)(2,1)} async-done(((bf16[512,1152]{0,1:T(8,128)(2,1)}), bf16[4096,1152]{0,1:T(8,128)(2,1)}) %all-gather.6.cloned.1.call-update) | async-done | bytes 9437200 | tf_op jit(solution)/shard_map/all_gather | solution.py:116
  221.5 12.7 %copy.55 = bf16[4096,1152]{1,0:T(8,128)(2,1)} copy(bf16[4096,1152]{0,1:T(8,128)(2,1)} %all-gather.6.cloned.1.call-done) | data formatting | bytes 18874368 | tf_op jit(solution)/shard_map/all_gather | solution.py:116
  238.1 11.5 %collective-permute-done.8 = bf16[8,512,1152]{2,1,0:T(8,128)(2,1)} collective-permute-done((bf16[8,512,1152]{2,1,0:T(8,128)(2,1)}, bf16[8,512,1152]{2,1,0:T(8,128)(2,1)}, u32[]{:S(2)}, u32[]{:S(2)}) %collective-permute-start.8) | collective-permute-done | bytes 9437216 | tf_op jit(solution)/shard_map/ppermute | solution.py:139
  249.6 7.8 %select_bitcast_fusion.1 = (bf16[8,1,512,1152]{3,2,1,0:T(8,128)(2,1)S(1)}, bf16[8,1,512,1152]{3,2,1,0:T(8,128)(2,1)S(1)}) fusion(bf16[8,512,1152]{2,1,0:T(8,128)(2,1)} %collective-permute-done.8, bf16[8,512,1152]{2,1,0:T(8,128)(2,1)} %bitcast.79, pred[]{:T(512)S(6)} %eq.54, pred[]{:T(512)S(6)} %eq.55), kind=kLoop, calls=%fused_computation.5 | loop fusion | flops 9437184 | bytes 37748736 | tf_op jit(solution)/shard_map/stack | solution.py:146
  257.4 8.4 %pad_maximum_fusion = bf16[8,2,512,1152]{3,2,1,0:T(8,128)(2,1)} fusion(bf16[8,1,512,1152]{3,2,1,0:T(8,128)(2,1)S(1)} %get-tuple-element.12, bf16[8,1,512,1152]{3,2,1,0:T(8,128)(2,1)S(1)} %get-tuple-element.11), kind=kLoop, calls=%fused_computation | loop fusion | flops 9437184 | bytes 37748736 | tf_op jit(solution)/shard_map/stack | solution.py:146
  265.8 66.9 %all-gather.4.cloned.1.call-done = bf16[2,256,8192]{2,1,0:T(8,128)(2,1)} async-done(((bf16[2,256,512]{2,1,0:T(8,128)(2,1)}), bf16[2,256,8192]{2,1,0:T(8,128)(2,1)}) %all-gather.4.cloned.1.call-update) | async-done | bytes 8388624 | tf_op jit(solution)/shard_map/all_gather | solution.py:147
  332.6 14.5 %fusion = f32[512,640]{1,0:T(8,128)S(1)} fusion(bf16[512,8192]{1,0:T(8,128)(2,1)} %bitcast.87, bf16[8192,1152]{1,0:T(8,128)(2,1)} %bitcast.80), kind=kOutput, calls=%fused_computation.2 | convolution fusion | flops 5368709120 | bytes 20185088 | tf_op jit(solution)/shard_map/dot_general | solution.py:150
  348.1 1.6 fusion.35
  350.1 1.3 copy.93
  351.4 1.5 collective-permute-done.9
  352.9 1.9 fusion.37
  355.1 1.5 fusion.4
  356.8 10.2 %convolution_convert_fusion = bf16[512,8192]{1,0:T(8,128)(2,1)} fusion(bf16[8192,1152]{1,0:T(8,128)(2,1)} %bitcast.81, bf16[64,8,4,128]{3,2,1,0:T(4,128)(2,1)S(1)} %bitcast.84), kind=kOutput, calls=%fused_computation.1 | convolution fusion | flops 4299161600 | bytes 17301504 | tf_op jit(solution)/shard_map/dot_general | solution.py:180
  368.1 103.5 %reduce-scatter.2.cloned.1.call-done = bf16[512,512]{1,0:T(8,128)(2,1)} async-done(((bf16[512,8192]{1,0:T(8,128)(2,1)}), bf16[512,512]{1,0:T(8,128)(2,1)}) %reduce-scatter.2.cloned.1.call-update) | async-done | bytes 524304 | tf_op jit(solution)/shard_map/reduce_scatter | solution.py:186
  471.6 2.0 fusion.13
  (62 shorter events, 12.3 us)
Async XLA Ops:
  6.5 34.9 %copy-start.3 = (s32[256,64]{0,1:T(8,128)S(1)}, s32[256,64]{0,1:T(8,128)}, u32[]{:S(2)}) copy-start(s32[256,64]{0,1:T(8,128)} %param.19) | copy-start | bytes 196612
  6.5 35.1 %copy-start.4 = (f32[256,64]{0,1:T(8,128)S(1)}, f32[256,64]{0,1:T(8,128)}, u32[]{:S(2)}) copy-start(f32[256,64]{0,1:T(8,128)} %param.20) | copy-start | bytes 196612
  6.5 54.0 %copy-start.2 = (bf16[256,512]{1,0:T(8,128)(2,1)S(1)}, bf16[256,512]{1,0:T(8,128)(2,1)}, u32[]{:S(2)}) copy-start(bf16[256,512]{1,0:T(8,128)(2,1)} %param.11) | copy-start | bytes 786436
  6.5 215.0 %all-gather.6.cloned.1.call-start = ((), (), s32[]{:S(2)}) async-start(), calls=%async_computation.3 | async-start | bytes 10616832 | tf_op jit(solution)/shard_map/all_gather | solution.py:116
  11.3 321.3 %all-gather.4.cloned.1.call-start = ((), (), s32[]{:S(2)}) async-start(), calls=%async_computation.1 | async-start | bytes 8912896 | tf_op jit(solution)/shard_map/all_gather | solution.py:147
  15.1 1.6 collective-permute-start
  16.8 23.7 %collective-permute-start.1 = (bf16[2,128,512]{2,1,0:T(8,128)(2,1)S(1)}, bf16[2,128,512]{2,1,0:T(8,128)(2,1)S(1)}, u32[]{:S(2)}, u32[]{:S(2)}) collective-permute-start(bf16[2,128,512]{2,1,0:T(8,128)(2,1)S(1)} %fusion.34), channel_id=1, source_target_pairs={{0,32},{16,48},{32,0},{48,16},{64,96},{80,112},{96,64},{112,80},{1... | collective-permute-start | bytes 786440 | tf_op jit(solution)/shard_map/ppermute | solution.py:83
  40.5 10.0 %collective-permute-start.2 = (bf16[2,128,512]{2,1,0:T(8,128)(2,1)S(1)}, bf16[2,128,512]{2,1,0:T(8,128)(2,1)S(1)}, u32[]{:S(2)}, u32[]{:S(2)}) collective-permute-start(bf16[2,128,512]{2,1,0:T(8,128)(2,1)S(1)} %fusion.41), channel_id=1, source_target_pairs={{0,64},{16,80},{32,96},{48,112},{64,0},{80,16},{96,32},{112,48},{1... | collective-permute-start | bytes 786440 | tf_op jit(solution)/shard_map/ppermute | solution.py:83
  50.5 9.9 %collective-permute-start.3 = (bf16[2,128,512]{2,1,0:T(8,128)(2,1)S(1)}, bf16[2,128,512]{2,1,0:T(8,128)(2,1)S(1)}, u32[]{:S(2)}, u32[]{:S(2)}) collective-permute-start(bf16[2,128,512]{2,1,0:T(8,128)(2,1)S(1)} %add.85), channel_id=1, source_target_pairs={{0,128},{16,144},{32,160},{48,176},{64,192},{80,208},{96,224},{112... | collective-permute-start | bytes 786440 | tf_op jit(solution)/shard_map/ppermute | solution.py:83
  60.9 173.3 %copy-start = (bf16[1,256,512]{2,1,0:T(8,128)(2,1)}, bf16[1,256,512]{2,1,0:T(8,128)(2,1)S(1)}, u32[]{:S(2)}) copy-start(bf16[1,256,512]{2,1,0:T(8,128)(2,1)S(1)} %fusion.7) | copy-start | bytes 786436
  61.1 3.7 collective-permute-start.4
  64.8 5.1 %collective-permute-start.5 = (f32[2,256,1]{1,0,2:T(2,128)S(1)}, f32[2,256,1]{1,0,2:T(2,128)S(1)}, u32[]{:S(2)}, u32[]{:S(2)}) collective-permute-start(f32[2,256,1]{1,0,2:T(2,128)S(1)} %bitcast_add_fusion.1), channel_id=1, source_target_pairs={{0,2},{1,3},{2,0},{3,1},{4,6},{5,7},{6,4},{7,5},{8,10},{9,11},{10,... | collective-permute-start | bytes 6152 | tf_op jit(solution)/shard_map/ppermute | solution.py:67
  69.9 6.2 %collective-permute-start.6 = (f32[2,256,1]{1,0,2:T(2,128)S(1)}, f32[2,256,1]{1,0,2:T(2,128)S(1)}, u32[]{:S(2)}, u32[]{:S(2)}) collective-permute-start(f32[2,256,1]{1,0,2:T(2,128)S(1)} %add.89), channel_id=1, source_target_pairs={{0,4},{1,5},{2,6},{3,7},{4,0},{5,1},{6,2},{7,3},{8,12},{9,13},{10,... | collective-permute-start | bytes 6152 | tf_op jit(solution)/shard_map/ppermute | solution.py:67
  76.1 4.5 collective-permute-start.7
  234.2 237.4 %reduce-scatter.2.cloned.1.call-start = ((), (), s32[]{:S(2)}) async-start(), calls=%async_computation.2 | async-start | bytes 8912896 | tf_op jit(solution)/shard_map/reduce_scatter | solution.py:186
  234.3 15.3 %collective-permute-start.8 = (bf16[8,512,1152]{2,1,0:T(8,128)(2,1)}, bf16[8,512,1152]{2,1,0:T(8,128)(2,1)}, u32[]{:S(2)}, u32[]{:S(2)}) collective-permute-start(bf16[8,512,1152]{2,1,0:T(8,128)(2,1)} %bitcast.78), channel_id=1, source_target_pairs={{0,16},{16,0},{1,17},{17,1},{2,18},{18,2},{3,19},{19,3},{4,20},{20... | collective-permute-start | bytes 28311560 | tf_op jit(solution)/shard_map/ppermute | solution.py:139
  347.6 5.3 %collective-permute-start.9 = (bf16[2,1,256,128]{2,3,0,1:T(8,128)(2,1)S(1)}, bf16[2,1,256,128]{2,3,0,1:T(8,128)(2,1)}, u32[]{:S(2)}, u32[]{:S(2)}) collective-permute-start(bf16[2,1,256,128]{2,3,0,1:T(8,128)(2,1)S(1)} %fusion.21), channel_id=1, source_target_pairs={{0,1},{1,0},{2,3},{3,2},{4,5},{5,4},{6,7},{7,6},{8,9},{9,8},{10,11... | collective-permute-start | bytes 393224 | tf_op jit(solution)/shard_map/ppermute | solution.py:164
  367.0 0.9 copy-start.1
Sparse Core Ops, SparseCore 0:
  11.4 210.0 all-gather.5
  234.4 98.2 all-gather.3
  367.2 104.3 reduce-scatter.1

commit v5 on v4

--- a/solution.py
+++ b/solution.py
@@ -113,7 +113,7 @@
     value_cols = lax.dynamic_slice_in_dim(value_weight, kv_index * HEAD_SIZE, HEAD_SIZE, 1)
     kv_cols = jnp.where(is_key_side, key_cols, value_cols)
     packed = jnp.concatenate([w_query, kv_cols, w_out.T], axis=1)
-    own_half = lax.all_gather(packed, "dict_hi", axis=0, tiled=False)
+    gathered = lax.all_gather(packed, DICT, axis=0, tiled=True)
     coef_list = [
         dense_codes(latent_ids, latent_vals, block_ids[number] * BLOCK)
         for number in range(ABLATION_STEPS)
@@ -130,20 +130,7 @@
     mean_sq = sum_sq / full_width
     gain_cols = lax.dynamic_slice_in_dim(norm_gain, tensor_pos * col_count, col_count)
     normed_cols = (widened * lax.rsqrt(mean_sq + EPSILON) * gain_cols).astype(jnp.bfloat16)
-    normed_cols, own_half = lax.optimization_barrier((normed_cols, own_half))
-    core_count = lax.axis_size("core")
-    core_pos = lax.axis_index("core")
-    halves = [own_half]
-    for shift in range(1, core_count):
-        core_pairs = [(i, (i + shift) % core_count) for i in range(core_count)]
-        halves.append(lax.ppermute(own_half, "core", core_pairs))
-    ordered = []
-    for core_id in range(core_count):
-        pick = halves[0]
-        for k in range(1, core_count):
-            pick = jnp.where((core_pos - k) % core_count == core_id, halves[k], pick)
-        ordered.append(pick)
-    gathered = jnp.stack(ordered, axis=1).reshape(-1, packed.shape[1])
+    normed_cols, gathered = lax.optimization_barrier((normed_cols, gathered))
     normed = lax.all_gather(normed_cols, "tensor", axis=2, tiled=True)
     normed = normed.reshape(ABLATION_STEPS * row_count, full_width)
     qkv_cols = head_cols + HEAD_SIZE

time: 481 us -> 469 us (0.975)
  waiting for transfers between devices: 358 us -> 378 us
  other arithmetic: 32.5 us -> 15.3 us
  local copies, waits for them, and re-layouts: 24.2 us -> 10.8 us
    all_gather x1, waiting for transfers between devices: 66.9 us -> 96.5 us  [body(): normed = lax.all_gather(normed_cols, 'tensor', axis=2, tiled=True)]
    another operation x2 -> x0, other arithmetic: 16.2 us -> none  [body(): gathered = jnp.stack(ordered, axis=1).reshape(-1, packed.shape[1])]
    all_gather x1 -> x0, local copies, waits for them, and re-layouts: 12.7 us -> none  [body(): own_half = lax.all_gather(packed, 'dict_hi', axis=0, tiled=False)]
    ppermute x1 -> x0, waiting for transfers between devices: 11.5 us -> none  [body(): halves.append(lax.ppermute(own_half, 'core', core_pairs))]
  transfers between devices with their start and end apart: 13 -> 12, of which waited for: 12 -> 11; matrix products, arithmetic and copies ran while one was open for 7% -> 4% of each run, Pallas kernels for 0% -> 0%
where the time goes in v5:
time: 469 us
  waiting for transfers between devices  378 us (81%)
  matrix products  28.9 us (6%)
  starting transfers between devices  20.2 us (4%)
  between operations  15.4 us (3%)
  other arithmetic  15.3 us (3%)
  local copies, waits for them, and re-layouts  10.8 us (2%)
    all_gather x1, waiting for transfers between devices, body(): gathered = lax.all_gather(packed, DICT, axis=0, tiled=True)  141 us
    reduce_scatter x1, waiting for transfers between devices, body(): lax.psum_scatter(partial_value.astype(jnp.float32).astype(jnp.bfloat16),...  104 us
    all_gather x1, waiting for transfers between devices, body(): normed = lax.all_gather(normed_cols, 'tensor', axis=2, tiled=True)  96.5 us
    ppermute x4, waiting for transfers between devices, fetch_blocks(): held = held + lax.ppermute(held, DICT, pairs)  27.5 us
    dot_general x1, matrix products, body(): jnp.dot(normed, gathered[:, :qkv_cols], preferred_element_type=jnp.float32)  14.9 us
    ppermute x4, starting transfers between devices, fetch_blocks(): held = held + lax.ppermute(held, DICT, pairs)  10.4 us
    dot_general x1, matrix products, body(): lax.dot_general(context, gathered[:, qkv_cols:], (((1,), (1,)), ((), ()))...  10.2 us
    ppermute x4, starting transfers between devices, butterfly_sum(): value = value + lax.ppermute(value, axis, pairs)  9.49 us
  transfers between devices with their start and end apart: 12, of which 11 were waited for; matrix products, arithmetic and copies ran while one was open for 4% of the time, Pallas kernels for 0%

profile of v5, /device:TPU:6, one launch (start us, length us, event | category | flops | bytes accessed | tf_op | source)
XLA Modules:
  0.0 468.8 jit_solution(4086987414414530162)
XLA Ops:
  6.5 1.0 constant_dynamic-slice_fusion
  7.9 1.3 copy.52
  9.2 1.1 pad_maximum_fusion
  12.2 1.0 select_bitcast_fusion.1
  13.4 1.5 collective-permute-done
  14.9 7.3 %collective-permute-start.1 = (bf16[2,128,512]{2,1,0:T(8,128)(2,1)S(1)}, bf16[2,128,512]{2,1,0:T(8,128)(2,1)S(1)}, u32[]{:S(2)}, u32[]{:S(2)}) collective-permute-start(bf16[2,128,512]{2,1,0:T(8,128)(2,1)S(1)} %fusion.34), channel_id=1, source_target_pairs={{0,32},{16,48},{32,0},{48,16},{64,96},{80,112},{96,64},{112,80},{1... | collective-permute-start | bytes 786440 | tf_op jit(solution)/shard_map/ppermute | solution.py:83
  22.2 16.7 %collective-permute-done.1 = bf16[2,128,512]{2,1,0:T(8,128)(2,1)S(1)} collective-permute-done((bf16[2,128,512]{2,1,0:T(8,128)(2,1)S(1)}, bf16[2,128,512]{2,1,0:T(8,128)(2,1)S(1)}, u32[]{:S(2)}, u32[]{:S(2)}) %collective-permute-start.1) | collective-permute-done | bytes 262176 | tf_op jit(solution)/shard_map/ppermute | solution.py:83
  39.0 1.0 collective-permute-start.2
  40.3 9.2 %collective-permute-done.2 = bf16[2,128,512]{2,1,0:T(8,128)(2,1)S(1)} collective-permute-done((bf16[2,128,512]{2,1,0:T(8,128)(2,1)S(1)}, bf16[2,128,512]{2,1,0:T(8,128)(2,1)S(1)}, u32[]{:S(2)}, u32[]{:S(2)}) %collective-permute-start.2) | collective-permute-done | bytes 262176 | tf_op jit(solution)/shard_map/ppermute | solution.py:83
  49.5 2.0 collective-permute-start.3
  51.6 7.8 %select_reduce_fusion.1 = (bf16[256,128]{1,0:T(8,128)(2,1)S(1)}, bf16[256,128]{1,0:T(8,128)(2,1)S(1)}) fusion(f32[256,64]{1,0:T(8,128)S(1)} %copy.48, s32[256,64]{1,0:T(8,128)S(1)} %copy.47, s32[256,64]{1,0:T(8,128)S(1)} %copy.49), kind=kLoop, calls=%fused_computation.6 | loop fusion | flops 12517376 | bytes 327680 | tf_op jit(solution)/shard_map/reduce_sum | solution.py:41
  60.1 1.6 collective-permute-start.4
  61.7 2.1 collective-permute-done.4
  63.8 3.0 collective-permute-start.5
  66.8 2.1 collective-permute-done.5
  69.5 3.0 collective-permute-done.6
  72.5 4.3 collective-permute-start.7
  76.8 0.8 dynamic_slice.17
  77.6 0.8 collective-permute-done.7
  78.4 1.0 multiply_convert_fusion
  79.4 141.3 %all-gather.3.cloned.1.call-done = bf16[8192,1152]{0,1:T(8,128)(2,1)} async-done(((bf16[512,1152]{0,1:T(8,128)(2,1)}), bf16[8192,1152]{0,1:T(8,128)(2,1)}) %all-gather.3.cloned.1.call-update) | async-done | bytes 18874384 | tf_op jit(solution)/shard_map/all_gather | solution.py:116
  224.2 96.5 %all-gather.5.cloned.1.call-done = bf16[2,256,8192]{2,1,0:T(8,128)(2,1)} async-done(((bf16[2,256,512]{2,1,0:T(8,128)(2,1)}), bf16[2,256,8192]{2,1,0:T(8,128)(2,1)}) %all-gather.5.cloned.1.call-update) | async-done | bytes 8388624 | tf_op jit(solution)/shard_map/all_gather | solution.py:134
  320.8 14.9 %fusion = f32[512,640]{1,0:T(8,128)S(1)} fusion(bf16[512,8192]{1,0:T(8,128)(2,1)} %bitcast.75, bf16[8192,1152]{0,1:T(8,128)(2,1)} %all-gather.3.cloned.1.call-done), kind=kOutput, calls=%fused_computation.1 | convolution fusion | flops 5368709120 | bytes 20185088 | tf_op jit(solution)/shard_map/dot_general | solution.py:137
  336.8 1.6 fusion.35
  338.8 1.3 copy.89
  340.1 1.5 collective-permute-done.8
  341.6 1.9 fusion.37
  343.8 1.5 fusion.4
  345.5 10.2 %convolution_convert_fusion = bf16[512,8192]{1,0:T(8,128)(2,1)} fusion(bf16[8192,1152]{0,1:T(8,128)(2,1)} %all-gather.3.cloned.1.call-done, bf16[64,8,4,128]{3,2,1,0:T(4,128)(2,1)S(1)} %bitcast.72), kind=kOutput, calls=%fused_computation | convolution fusion | flops 4299161600 | bytes 17301504 | tf_op jit(solution)/shard_map/dot_general | solution.py:167
  355.7 0.9 copy-done.1
  356.7 103.5 %reduce-scatter.2.cloned.1.call-done = bf16[512,512]{1,0:T(8,128)(2,1)} async-done(((bf16[512,8192]{1,0:T(8,128)(2,1)}), bf16[512,512]{1,0:T(8,128)(2,1)}) %reduce-scatter.2.cloned.1.call-update) | async-done | bytes 524304 | tf_op jit(solution)/shard_map/reduce_scatter | solution.py:173
  460.3 2.0 fusion.13
  (61 shorter events, 7.7 us)
Async XLA Ops:
  6.5 2.6 copy-start.3
  6.5 214.1 %all-gather.3.cloned.1.call-start = ((), (), s32[]{:S(2)}) async-start(), calls=%async_computation.1 | async-start | bytes 20054016 | tf_op jit(solution)/shard_map/all_gather | solution.py:116
  7.8 2.5 copy-start.6
  10.3 29.7 %copy-start.4 = (s32[256,64]{0,1:T(8,128)S(1)}, s32[256,64]{0,1:T(8,128)}, u32[]{:S(2)}) copy-start(s32[256,64]{0,1:T(8,128)} %param.19) | copy-start | bytes 196612
  10.3 29.9 %copy-start.5 = (f32[256,64]{0,1:T(8,128)S(1)}, f32[256,64]{0,1:T(8,128)}, u32[]{:S(2)}) copy-start(f32[256,64]{0,1:T(8,128)} %param.20) | copy-start | bytes 196612
  10.3 310.5 %all-gather.5.cloned.1.call-start = ((), (), s32[]{:S(2)}) async-start(), calls=%async_computation.2 | async-start | bytes 8912896 | tf_op jit(solution)/shard_map/all_gather | solution.py:134
  13.3 46.2 %copy-start.2 = (bf16[256,512]{1,0:T(8,128)(2,1)S(1)}, bf16[256,512]{1,0:T(8,128)(2,1)}, u32[]{:S(2)}) copy-start(bf16[256,512]{1,0:T(8,128)(2,1)} %param.11) | copy-start | bytes 786436
  13.3 1.6 collective-permute-start
  14.9 24.0 %collective-permute-start.1 = (bf16[2,128,512]{2,1,0:T(8,128)(2,1)S(1)}, bf16[2,128,512]{2,1,0:T(8,128)(2,1)S(1)}, u32[]{:S(2)}, u32[]{:S(2)}) collective-permute-start(bf16[2,128,512]{2,1,0:T(8,128)(2,1)S(1)} %fusion.34), channel_id=1, source_target_pairs={{0,32},{16,48},{32,0},{48,16},{64,96},{80,112},{96,64},{112,80},{1... | collective-permute-start | bytes 786440 | tf_op jit(solution)/shard_map/ppermute | solution.py:83
  39.0 10.5 %collective-permute-start.2 = (bf16[2,128,512]{2,1,0:T(8,128)(2,1)S(1)}, bf16[2,128,512]{2,1,0:T(8,128)(2,1)S(1)}, u32[]{:S(2)}, u32[]{:S(2)}) collective-permute-start(bf16[2,128,512]{2,1,0:T(8,128)(2,1)S(1)} %fusion.41), channel_id=1, source_target_pairs={{0,64},{16,80},{32,96},{48,112},{64,0},{80,16},{96,32},{112,48},{1... | collective-permute-start | bytes 786440 | tf_op jit(solution)/shard_map/ppermute | solution.py:83
  49.5 9.9 %collective-permute-start.3 = (bf16[2,128,512]{2,1,0:T(8,128)(2,1)S(1)}, bf16[2,128,512]{2,1,0:T(8,128)(2,1)S(1)}, u32[]{:S(2)}, u32[]{:S(2)}) collective-permute-start(bf16[2,128,512]{2,1,0:T(8,128)(2,1)S(1)} %add.80), channel_id=1, source_target_pairs={{0,128},{16,144},{32,160},{48,176},{64,192},{80,208},{96,224},{112... | collective-permute-start | bytes 786440 | tf_op jit(solution)/shard_map/ppermute | solution.py:83
  59.9 275.8 %copy-start = (bf16[1,256,512]{2,1,0:T(8,128)(2,1)}, bf16[1,256,512]{2,1,0:T(8,128)(2,1)S(1)}, u32[]{:S(2)}) copy-start(bf16[1,256,512]{2,1,0:T(8,128)(2,1)S(1)} %fusion.7) | copy-start | bytes 786436
  60.1 3.7 collective-permute-start.4
  63.8 5.1 %collective-permute-start.5 = (f32[2,256,1]{1,0,2:T(2,128)S(1)}, f32[2,256,1]{1,0,2:T(2,128)S(1)}, u32[]{:S(2)}, u32[]{:S(2)}) collective-permute-start(f32[2,256,1]{1,0,2:T(2,128)S(1)} %bitcast_add_fusion.1), channel_id=1, source_target_pairs={{0,2},{1,3},{2,0},{3,1},{4,6},{5,7},{6,4},{7,5},{8,10},{9,11},{10,... | collective-permute-start | bytes 6152 | tf_op jit(solution)/shard_map/ppermute | solution.py:67
  68.9 3.6 collective-permute-start.6
  72.5 5.9 %collective-permute-start.7 = (f32[2,256,1]{1,0,2:T(2,128)S(1)}, f32[2,256,1]{1,0,2:T(2,128)S(1)}, u32[]{:S(2)}, u32[]{:S(2)}) collective-permute-start(f32[2,256,1]{1,0,2:T(2,128)S(1)} %add.85), channel_id=1, source_target_pairs={{0,8},{1,9},{2,10},{3,11},{4,12},{5,13},{6,14},{7,15},{8,0},{9,1},... | collective-permute-start | bytes 6152 | tf_op jit(solution)/shard_map/ppermute | solution.py:67
  220.7 239.6 %reduce-scatter.2.cloned.1.call-start = ((), (), s32[]{:S(2)}) async-start(), calls=%async_computation.3 | async-start | bytes 8912896 | tf_op jit(solution)/shard_map/reduce_scatter | solution.py:173
  336.1 5.5 %collective-permute-start.8 = (bf16[2,1,256,128]{2,3,0,1:T(8,128)(2,1)S(1)}, bf16[2,1,256,128]{2,3,0,1:T(8,128)(2,1)}, u32[]{:S(2)}, u32[]{:S(2)}) collective-permute-start(bf16[2,1,256,128]{2,3,0,1:T(8,128)(2,1)S(1)} %fusion.21), channel_id=1, source_target_pairs={{0,1},{1,0},{2,3},{3,2},{4,5},{5,4},{6,7},{7,6},{8,9},{9,8},{10,11... | collective-permute-start | bytes 393224 | tf_op jit(solution)/shard_map/ppermute | solution.py:151
  355.7 0.9 copy-start.1
Sparse Core Ops, SparseCore 0:
  10.4 210.2 all-gather.2
  222.5 98.2 all-gather.4
  355.8 104.3 reduce-scatter.1

commit v6 on v5

--- a/solution.py
+++ b/solution.py
@@ -67,6 +67,32 @@
         value = value + lax.ppermute(value, axis, pairs)
         step *= 2
     return value
+
+
+def ring_gather_dict(block):
+    count = dict_size()
+    cores = lax.axis_size("core")
+    hi = lax.axis_size("dict_hi")
+    lanes = 2 if hi % 2 == 0 else 1
+    along = hi // lanes
+    chips = [(x, 0) for x in range(along)]
+    if lanes == 2:
+        chips += [(x, 1) for x in reversed(range(along))]
+    ring = [(x * lanes + z) * cores + c for (x, z) in chips for c in range(cores)]
+    pairs = [(ring[i], ring[(i + 1) % count]) for i in range(count)]
+    place = [0] * count
+    for i, d in enumerate(ring):
+        place[d] = i
+    place = jnp.array(place, jnp.int32)
+    my_place = place[dict_index()]
+    pieces = [block]
+    moving = block
+    for _ in range(count - 1):
+        moving = lax.ppermute(moving, DICT, pairs)
+        pieces.append(moving)
+    order = (my_place - place) % count
+    ordered = jnp.take(jnp.stack(pieces), order, axis=0)
+    return ordered.reshape(count * block.shape[0], block.shape[1])
 
 
 def fetch_blocks(decoder, block_ids):
@@ -112,8 +138,9 @@
     key_cols = lax.dynamic_slice_in_dim(w_key, kv_index * HEAD_SIZE, HEAD_SIZE, 1)
     value_cols = lax.dynamic_slice_in_dim(value_weight, kv_index * HEAD_SIZE, HEAD_SIZE, 1)
     kv_cols = jnp.where(is_key_side, key_cols, value_cols)
-    packed = jnp.concatenate([w_query, kv_cols, w_out.T], axis=1)
+    packed = jnp.concatenate([w_query, kv_cols], axis=1)
     gathered = lax.all_gather(packed, DICT, axis=0, tiled=True)
+    out_rows = ring_gather_dict(w_out.T)
     coef_list = [
         dense_codes(latent_ids, latent_vals, block_ids[number] * BLOCK)
         for number in range(ABLATION_STEPS)
@@ -134,7 +161,7 @@
     normed = lax.all_gather(normed_cols, "tensor", axis=2, tiled=True)
     normed = normed.reshape(ABLATION_STEPS * row_count, full_width)
     qkv_cols = head_cols + HEAD_SIZE
-    qkv = jnp.dot(normed, gathered[:, :qkv_cols], preferred_element_type=jnp.float32)
+    qkv = jnp.dot(normed, gathered, preferred_element_type=jnp.float32)
     query_vec = qkv[:, :head_cols]
     kv_vector = qkv[:, head_cols:qkv_cols]
     prompt_count = row_count // PROMPT_ROWS
@@ -166,7 +193,7 @@
     context = context.astype(jnp.bfloat16).reshape(ABLATION_STEPS * row_count, head_cols)
     partial_value = lax.dot_general(
         context,
-        gathered[:, qkv_cols:],
+        out_rows,
         (((1,), (1,)), ((), ())),
         preferred_element_type=jnp.float32,
     ).astype(jnp.bfloat16)

time: 469 us -> 620 us (1.32)
  starting transfers between devices: 20.2 us -> 206 us
  waiting for transfers between devices: 378 us -> 306 us
  local copies, waits for them, and re-layouts: 10.8 us -> 35.9 us
  other arithmetic: 15.3 us -> 27.6 us
    ppermute x0 -> x15, starting transfers between devices: none -> 178 us  [ring_gather_dict(): moving = lax.ppermute(moving, DICT, pairs)]
    all_gather x1, waiting for transfers between devices: 96.5 us -> 0.01 us  [body(): normed = lax.all_gather(normed_cols, 'tensor', axis=2, tiled=True)]
    reduce_scatter x1, waiting for transfers between devices: 104 us -> 189 us  [body(): lax.psum_scatter(partial_value.astype(jnp.float32).astype(jnp.bfloat16),...]
    all_gather x1, waiting for transfers between devices: 141 us -> 57 us  [body(): gathered = lax.all_gather(packed, DICT, axis=0, tiled=True)]
    ppermute x0 -> x15, waiting for transfers between devices: none -> 26.1 us  [ring_gather_dict(): moving = lax.ppermute(moving, DICT, pairs)]
    unnamed x19 -> x37, local copies, waits for them, and re-layouts: 3.83 us -> 21.8 us
    gather x0 -> x1, local copies, waits for them, and re-layouts: none -> 8.19 us  [ring_gather_dict(): ordered = jnp.take(jnp.stack(pieces), order, axis=0)]
    ppermute x4, starting transfers between devices: 9.49 us -> 17.2 us  [butterfly_sum(): value = value + lax.ppermute(value, axis, pairs)]
  transfers between devices with their start and end apart: 12 -> 27, of which waited for: 11 -> 21; matrix products, arithmetic and copies ran while one was open for 4% -> 9% of each run, Pallas kernels for 0% -> 0%
where the time goes in v6:
time: 620 us; the launch traced here: 619 us
  waiting for transfers between devices  306 us (49%)
  starting transfers between devices  206 us (33%)
  local copies, waits for them, and re-layouts  35.9 us (6%)
  matrix products  28.5 us (5%)
  other arithmetic  27.6 us (4%)
  between operations  15.5 us (2%)
    reduce_scatter x1, waiting for transfers between devices, body(): lax.psum_scatter(partial_value.astype(jnp.float32).astype(jnp.bfloat16),...  189 us
    ppermute x15, starting transfers between devices, ring_gather_dict(): moving = lax.ppermute(moving, DICT, pairs)  178 us
    all_gather x1, waiting for transfers between devices, body(): gathered = lax.all_gather(packed, DICT, axis=0, tiled=True)  57 us
    ppermute x15, waiting for transfers between devices, ring_gather_dict(): moving = lax.ppermute(moving, DICT, pairs)  26.1 us
    ppermute x4, waiting for transfers between devices, fetch_blocks(): held = held + lax.ppermute(held, DICT, pairs)  22.5 us
    unnamed x37, local copies, waits for them, and re-layouts  21.8 us
    ppermute x4, starting transfers between devices, butterfly_sum(): value = value + lax.ppermute(value, axis, pairs)  17.2 us
    dot_general x1, matrix products, body(): qkv = jnp.dot(normed, gathered, preferred_element_type=jnp.float32)  14.9 us
  transfers between devices with their start and end apart: 27, of which 21 were waited for; matrix products, arithmetic and copies ran while one was open for 9% of the time, Pallas kernels for 0%

profile of v6, /device:TPU:6, one launch (start us, length us, event | category | flops | bytes accessed | tf_op | source)
XLA Modules:
  0.0 618.9 jit_solution(14350327700180239963)
XLA Ops:
  15.2 7.3 %collective-permute-start.1 = (bf16[2,128,512]{2,1,0:T(8,128)(2,1)S(1)}, bf16[2,128,512]{2,1,0:T(8,128)(2,1)S(1)}, u32[]{:S(2)}, u32[]{:S(2)}) collective-permute-start(bf16[2,128,512]{2,1,0:T(8,128)(2,1)S(1)} %fusion.32), channel_id=1, source_target_pairs={{0,32},{16,48},{32,0},{48,16},{64,96},{80,112},{96,64},{112,80},{1... | collective-permute-start | bytes 786440 | tf_op jit(solution)/shard_map/ppermute | solution.py:109
  22.5 17.0 %collective-permute-done.1 = bf16[2,128,512]{2,1,0:T(8,128)(2,1)S(1)} collective-permute-done((bf16[2,128,512]{2,1,0:T(8,128)(2,1)S(1)}, bf16[2,128,512]{2,1,0:T(8,128)(2,1)S(1)}, u32[]{:S(2)}, u32[]{:S(2)}) %collective-permute-start.1) | collective-permute-done | bytes 262176 | tf_op jit(solution)/shard_map/ppermute | solution.py:109
  42.4 3.6 collective-permute-done.2
  47.9 7.8 %select_reduce_fusion.1 = (bf16[256,128]{1,0:T(8,128)(2,1)S(1)}, bf16[256,128]{1,0:T(8,128)(2,1)S(1)}) fusion(f32[256,64]{1,0:T(8,128)S(1)} %copy.59, s32[256,64]{1,0:T(8,128)S(1)} %copy.58, s32[256,64]{1,0:T(8,128)S(1)} %copy.60), kind=kLoop, calls=%fused_computation.4 | loop fusion | flops 12517376 | bytes 327680 | tf_op jit(solution)/shard_map/reduce_sum | solution.py:41
  58.2 2.2 collective-permute-done.4
  60.4 2.8 collective-permute-start.5
  63.2 2.3 collective-permute-done.5
  65.5 12.3 %collective-permute-start.6 = (f32[2,256,1]{1,0,2:T(2,128)S(1)}, f32[2,256,1]{1,0,2:T(2,128)S(1)}, u32[]{:S(2)}, u32[]{:S(2)}) collective-permute-start(f32[2,256,1]{1,0,2:T(2,128)S(1)} %add.98), channel_id=1, source_target_pairs={{0,4},{1,5},{2,6},{3,7},{4,0},{5,1},{6,2},{7,3},{8,12},{9,13},{10,... | collective-permute-start | bytes 6152 | tf_op jit(solution)/shard_map/ppermute | solution.py:67
  81.1 3.2 collective-permute-done.7
  85.3 57.0 %all-gather.3.cloned.1.call-done = bf16[8192,640]{1,0:T(8,128)(2,1)} async-done(((bf16[512,640]{1,0:T(8,128)(2,1)}), bf16[8192,640]{1,0:T(8,128)(2,1)}) %all-gather.3.cloned.1.call-update) | async-done | bytes 10485776 | tf_op jit(solution)/shard_map/all_gather | solution.py:142
  142.9 8.4 %collective-permute-done.9 = bf16[512,512]{1,0:T(8,128)(2,1)S(1)} collective-permute-done((bf16[512,512]{1,0:T(8,128)(2,1)S(1)}, bf16[512,512]{1,0:T(8,128)(2,1)S(1)}, u32[]{:S(2)}, u32[]{:S(2)}) %collective-permute-start.9) | collective-permute-done | bytes 524320 | tf_op jit(solution)/shard_map/ppermute | solution.py:91
  151.3 8.6 %collective-permute-done.10 = bf16[512,512]{1,0:T(8,128)(2,1)S(1)} collective-permute-done((bf16[512,512]{1,0:T(8,128)(2,1)S(1)}, bf16[512,512]{1,0:T(8,128)(2,1)S(1)}, u32[]{:S(2)}, u32[]{:S(2)}) %collective-permute-start.10) | collective-permute-done | bytes 524320 | tf_op jit(solution)/shard_map/ppermute | solution.py:91
  159.9 9.7 %collective-permute-start.11 = (bf16[512,512]{1,0:T(8,128)(2,1)S(1)}, bf16[512,512]{1,0:T(8,128)(2,1)S(1)}, u32[]{:S(2)}, u32[]{:S(2)}) collective-permute-start(bf16[512,512]{1,0:T(8,128)(2,1)S(1)} %collective-permute-done.10), channel_id=1, source_target_pairs={{0,16},{16,64},{64,80},{80,128},{128,144},{144,192},{192,208},{208... | collective-permute-start | bytes 1572872 | tf_op jit(solution)/shard_map/ppermute | solution.py:91
  171.1 22.2 %collective-permute-start.12 = (bf16[512,512]{1,0:T(8,128)(2,1)S(1)}, bf16[512,512]{1,0:T(8,128)(2,1)S(1)}, u32[]{:S(2)}, u32[]{:S(2)}) collective-permute-start(bf16[512,512]{1,0:T(8,128)(2,1)S(1)} %collective-permute-done.11), channel_id=1, source_target_pairs={{0,16},{16,64},{64,80},{80,128},{128,144},{144,192},{192,208},{208... | collective-permute-start | bytes 1572872 | tf_op jit(solution)/shard_map/ppermute | solution.py:91
  194.9 21.9 %collective-permute-start.13 = (bf16[512,512]{1,0:T(8,128)(2,1)S(1)}, bf16[512,512]{1,0:T(8,128)(2,1)S(1)}, u32[]{:S(2)}, u32[]{:S(2)}) collective-permute-start(bf16[512,512]{1,0:T(8,128)(2,1)S(1)} %collective-permute-done.12), channel_id=1, source_target_pairs={{0,16},{16,64},{64,80},{80,128},{128,144},{144,192},{192,208},{208... | collective-permute-start | bytes 1572872 | tf_op jit(solution)/shard_map/ppermute | solution.py:91
  218.3 19.9 %collective-permute-start.14 = (bf16[512,512]{1,0:T(8,128)(2,1)S(1)}, bf16[512,512]{1,0:T(8,128)(2,1)S(1)}, u32[]{:S(2)}, u32[]{:S(2)}) collective-permute-start(bf16[512,512]{1,0:T(8,128)(2,1)S(1)} %collective-permute-done.13), channel_id=1, source_target_pairs={{0,16},{16,64},{64,80},{80,128},{128,144},{144,192},{192,208},{208... | collective-permute-start | bytes 1572872 | tf_op jit(solution)/shard_map/ppermute | solution.py:91
  240.5 17.7 %collective-permute-start.15 = (bf16[512,512]{1,0:T(8,128)(2,1)S(1)}, bf16[512,512]{1,0:T(8,128)(2,1)}, u32[]{:S(2)}, u32[]{:S(2)}) collective-permute-start(bf16[512,512]{1,0:T(8,128)(2,1)S(1)} %collective-permute-done.14), channel_id=1, source_target_pairs={{0,16},{16,64},{64,80},{80,128},{128,144},{144,192},{192,208},{208... | collective-permute-start | bytes 1572872 | tf_op jit(solution)/shard_map/ppermute | solution.py:91
  259.9 18.2 %collective-permute-start.16 = (bf16[512,512]{1,0:T(8,128)(2,1)}, bf16[512,512]{1,0:T(8,128)(2,1)}, u32[]{:S(2)}, u32[]{:S(2)}) collective-permute-start(bf16[512,512]{1,0:T(8,128)(2,1)} %collective-permute-done.15), channel_id=1, source_target_pairs={{0,16},{16,64},{64,80},{80,128},{128,144},{144,192},{192,208},{208... | collective-permute-start | bytes 1572872 | tf_op jit(solution)/shard_map/ppermute | solution.py:91
  280.0 12.0 %collective-permute-start.17 = (bf16[512,512]{1,0:T(8,128)(2,1)}, bf16[512,512]{1,0:T(8,128)(2,1)S(1)}, u32[]{:S(2)}, u32[]{:S(2)}) collective-permute-start(bf16[512,512]{1,0:T(8,128)(2,1)} %collective-permute-done.16), channel_id=1, source_target_pairs={{0,16},{16,64},{64,80},{80,128},{128,144},{144,192},{192,208},{208... | collective-permute-start | bytes 1572872 | tf_op jit(solution)/shard_map/ppermute | solution.py:91
  293.8 11.2 %collective-permute-start.18 = (bf16[512,512]{1,0:T(8,128)(2,1)S(1)}, bf16[512,512]{1,0:T(8,128)(2,1)}, u32[]{:S(2)}, u32[]{:S(2)}) collective-permute-start(bf16[512,512]{1,0:T(8,128)(2,1)S(1)} %collective-permute-done.17), channel_id=1, source_target_pairs={{0,16},{16,64},{64,80},{80,128},{128,144},{144,192},{192,208},{208... | collective-permute-start | bytes 1572872 | tf_op jit(solution)/shard_map/ppermute | solution.py:91
  306.6 10.8 %collective-permute-start.19 = (bf16[512,512]{1,0:T(8,128)(2,1)}, bf16[512,512]{1,0:T(8,128)(2,1)}, u32[]{:S(2)}, u32[]{:S(2)}) collective-permute-start(bf16[512,512]{1,0:T(8,128)(2,1)} %collective-permute-done.18), channel_id=1, source_target_pairs={{0,16},{16,64},{64,80},{80,128},{128,144},{144,192},{192,208},{208... | collective-permute-start | bytes 1572872 | tf_op jit(solution)/shard_map/ppermute | solution.py:91
  319.3 11.1 %collective-permute-start.20 = (bf16[512,512]{1,0:T(8,128)(2,1)}, bf16[512,512]{1,0:T(8,128)(2,1)S(1)}, u32[]{:S(2)}, u32[]{:S(2)}) collective-permute-start(bf16[512,512]{1,0:T(8,128)(2,1)} %collective-permute-done.19), channel_id=1, source_target_pairs={{0,16},{16,64},{64,80},{80,128},{128,144},{144,192},{192,208},{208... | collective-permute-start | bytes 1572872 | tf_op jit(solution)/shard_map/ppermute | solution.py:91
  334.9 8.2 %collective-permute-start.21 = (bf16[512,512]{1,0:T(8,128)(2,1)S(1)}, bf16[512,512]{1,0:T(8,128)(2,1)S(1)}, u32[]{:S(2)}, u32[]{:S(2)}) collective-permute-start(bf16[512,512]{1,0:T(8,128)(2,1)S(1)} %collective-permute-done.20), channel_id=1, source_target_pairs={{0,16},{16,64},{64,80},{80,128},{128,144},{144,192},{192,208},{208... | collective-permute-start | bytes 1572872 | tf_op jit(solution)/shard_map/ppermute | solution.py:91
  348.8 6.8 %collective-permute-start.22 = (bf16[512,512]{1,0:T(8,128)(2,1)S(1)}, bf16[512,512]{1,0:T(8,128)(2,1)S(1)}, u32[]{:S(2)}, u32[]{:S(2)}) collective-permute-start(bf16[512,512]{1,0:T(8,128)(2,1)S(1)} %collective-permute-done.21), channel_id=1, source_target_pairs={{0,16},{16,64},{64,80},{80,128},{128,144},{144,192},{192,208},{208... | collective-permute-start | bytes 1572872 | tf_op jit(solution)/shard_map/ppermute | solution.py:91
  360.2 7.9 %collective-permute-start.23 = (bf16[512,512]{1,0:T(8,128)(2,1)S(1)}, bf16[512,512]{1,0:T(8,128)(2,1)S(1)}, u32[]{:S(2)}, u32[]{:S(2)}) collective-permute-start(bf16[512,512]{1,0:T(8,128)(2,1)S(1)} %collective-permute-done.22), channel_id=1, source_target_pairs={{0,16},{16,64},{64,80},{80,128},{128,144},{144,192},{192,208},{208... | collective-permute-start | bytes 1572872 | tf_op jit(solution)/shard_map/ppermute | solution.py:91
  371.4 8.2 %gather_fusion = bf16[16,512,512]{2,1,0:T(8,128)(2,1)} fusion(bf16[16,512,512]{2,1,0:T(8,128)(2,1)} %bitcast_dynamic-update-slice_fusion.1, s32[1024]{0:T(1024)S(1)} %pad_clamp_fusion), kind=kCustom, calls=%fused_computation | custom fusion | bytes 16777280 | tf_op jit(solution)/shard_map/jit(_take)/gather | solution.py:94
  379.6 7.5 %broadcast_select_fusion = bf16[16,512,512]{2,1,0:T(8,128)(2,1)} fusion(bf16[16,512,512]{2,1,0:T(8,128)(2,1)} %gather_fusion, pred[16]{0:T(512)(128)(4,1)S(1)} %get-tuple-element.11), kind=kLoop, calls=%fused_computation.6 | loop fusion | flops 4194304 | bytes 16777232 | tf_op jit(solution)/shard_map/jit(_take)/select_n | solution.py:94
  387.2 14.9 %fusion.36 = f32[512,640]{1,0:T(8,128)S(1)} fusion(bf16[512,8192]{1,0:T(8,128)(2,1)} %bitcast.111, bf16[8192,640]{1,0:T(8,128)(2,1)} %all-gather.3.cloned.1.call-done), kind=kOutput, calls=%fused_computation.96 | convolution fusion | flops 5368709120 | bytes 20185088 | tf_op jit(solution)/shard_map/dot_general | solution.py:164
  407.7 2.4 fusion.35
  411.3 10.2 %convolution_convert_fusion = bf16[512,8192]{1,0:T(8,128)(2,1)} fusion(bf16[8192,512]{1,0:T(8,128)(2,1)} %bitcast.106, bf16[64,8,4,128]{3,2,1,0:T(4,128)(2,1)S(1)} %bitcast.109), kind=kOutput, calls=%fused_computation.1 | convolution fusion | flops 4299161600 | bytes 17301504 | tf_op jit(solution)/shard_map/dot_general | solution.py:194
  421.7 188.7 %reduce-scatter.2.cloned.1.call-done = bf16[512,512]{1,0:T(8,128)(2,1)} async-done(((bf16[512,8192]{1,0:T(8,128)(2,1)}), bf16[512,512]{1,0:T(8,128)(2,1)}) %reduce-scatter.2.cloned.1.call-update) | async-done | bytes 524304 | tf_op jit(solution)/shard_map/reduce_scatter | solution.py:200
  610.3 2.0 fusion.10
  (114 shorter events, 59.3 us)
Async XLA Ops:
  6.5 272.2 %copy-start.9 = (s32[16]{0:T(128)S(1)}, s32[16]{0:T(128)}, u32[]{:S(2)}) copy-start(s32[16]{0:T(128)} %constant.126.clone) | copy-start | bytes 196
  6.5 286.0 %copy-start.8 = (s32[16]{0:T(128)S(1)}, s32[16]{0:T(128)}, u32[]{:S(2)}) copy-start(s32[16]{0:T(128)} %constant.128) | copy-start | bytes 196
  6.5 49.6 %copy-start = (bf16[256,512]{1,0:T(8,128)(2,1)S(1)}, bf16[256,512]{1,0:T(8,128)(2,1)}, u32[]{:S(2)}) copy-start(bf16[256,512]{1,0:T(8,128)(2,1)} %param.12) | copy-start | bytes 786436
  6.5 135.8 %copy-start.1 = (bf16[512,512]{1,0:T(8,128)(2,1)S(1)}, bf16[512,512]{1,0:T(8,128)(2,1)}, u32[]{:S(2)}) copy-start(bf16[512,512]{1,0:T(8,128)(2,1)} %param.17) | copy-start | bytes 1572868
  6.5 135.8 %all-gather.3.cloned.1.call-start = ((), (), s32[]{:S(2)}) async-start(), calls=%async_computation.1 | async-start | bytes 11141120 | tf_op jit(solution)/shard_map/all_gather | solution.py:142
  9.7 377.5 %all-gather.5.cloned.1.call-start = ((), (), s32[]{:S(2)}) async-start(), calls=%async_computation.2 | async-start | bytes 8912896 | tf_op jit(solution)/shard_map/all_gather | solution.py:161
  13.6 1.6 collective-permute-start
  15.2 24.3 %collective-permute-start.1 = (bf16[2,128,512]{2,1,0:T(8,128)(2,1)S(1)}, bf16[2,128,512]{2,1,0:T(8,128)(2,1)S(1)}, u32[]{:S(2)}, u32[]{:S(2)}) collective-permute-start(bf16[2,128,512]{2,1,0:T(8,128)(2,1)S(1)} %fusion.32), channel_id=1, source_target_pairs={{0,32},{16,48},{32,0},{48,16},{64,96},{80,112},{96,64},{112,80},{1... | collective-permute-start | bytes 786440 | tf_op jit(solution)/shard_map/ppermute | solution.py:109
  39.6 6.5 %collective-permute-start.2 = (bf16[2,128,512]{2,1,0:T(8,128)(2,1)S(1)}, bf16[2,128,512]{2,1,0:T(8,128)(2,1)S(1)}, u32[]{:S(2)}, u32[]{:S(2)}) collective-permute-start(bf16[2,128,512]{2,1,0:T(8,128)(2,1)S(1)} %fusion.42), channel_id=1, source_target_pairs={{0,64},{16,80},{32,96},{48,112},{64,0},{80,16},{96,32},{112,48},{1... | collective-permute-start | bytes 786440 | tf_op jit(solution)/shard_map/ppermute | solution.py:109
  46.1 9.9 %collective-permute-start.3 = (bf16[2,128,512]{2,1,0:T(8,128)(2,1)S(1)}, bf16[2,128,512]{2,1,0:T(8,128)(2,1)S(1)}, u32[]{:S(2)}, u32[]{:S(2)}) collective-permute-start(bf16[2,128,512]{2,1,0:T(8,128)(2,1)S(1)} %add.94), channel_id=1, source_target_pairs={{0,128},{16,144},{32,160},{48,176},{64,192},{80,208},{96,224},{112... | collective-permute-start | bytes 786440 | tf_op jit(solution)/shard_map/ppermute | solution.py:109
  56.7 3.7 collective-permute-start.4
  60.4 5.1 collective-permute-start.5
  65.5 14.1 %collective-permute-start.6 = (f32[2,256,1]{1,0,2:T(2,128)S(1)}, f32[2,256,1]{1,0,2:T(2,128)S(1)}, u32[]{:S(2)}, u32[]{:S(2)}) collective-permute-start(f32[2,256,1]{1,0,2:T(2,128)S(1)} %add.98), channel_id=1, source_target_pairs={{0,4},{1,5},{2,6},{3,7},{4,0},{5,1},{6,2},{7,3},{8,12},{9,13},{10,... | collective-permute-start | bytes 6152 | tf_op jit(solution)/shard_map/ppermute | solution.py:67
  79.6 4.7 collective-permute-start.7
  142.3 468.0 %reduce-scatter.2.cloned.1.call-start = ((), (), s32[]{:S(2)}) async-start(), calls=%async_computation.3 | async-start | bytes 8912896 | tf_op jit(solution)/shard_map/reduce_scatter | solution.py:200
  142.6 8.7 %collective-permute-start.9 = (bf16[512,512]{1,0:T(8,128)(2,1)S(1)}, bf16[512,512]{1,0:T(8,128)(2,1)S(1)}, u32[]{:S(2)}, u32[]{:S(2)}) collective-permute-start(bf16[512,512]{1,0:T(8,128)(2,1)S(1)} %bitcast.107), channel_id=1, source_target_pairs={{0,16},{16,64},{64,80},{80,128},{128,144},{144,192},{192,208},{208... | collective-permute-start | bytes 1572872 | tf_op jit(solution)/shard_map/ppermute | solution.py:91
  151.3 8.6 %collective-permute-start.10 = (bf16[512,512]{1,0:T(8,128)(2,1)S(1)}, bf16[512,512]{1,0:T(8,128)(2,1)S(1)}, u32[]{:S(2)}, u32[]{:S(2)}) collective-permute-start(bf16[512,512]{1,0:T(8,128)(2,1)S(1)} %collective-permute-done.9), channel_id=1, source_target_pairs={{0,16},{16,64},{64,80},{80,128},{128,144},{144,192},{192,208},{208... | collective-permute-start | bytes 1572872 | tf_op jit(solution)/shard_map/ppermute | solution.py:91
  159.9 11.3 %collective-permute-start.11 = (bf16[512,512]{1,0:T(8,128)(2,1)S(1)}, bf16[512,512]{1,0:T(8,128)(2,1)S(1)}, u32[]{:S(2)}, u32[]{:S(2)}) collective-permute-start(bf16[512,512]{1,0:T(8,128)(2,1)S(1)} %collective-permute-done.10), channel_id=1, source_target_pairs={{0,16},{16,64},{64,80},{80,128},{128,144},{144,192},{192,208},{208... | collective-permute-start | bytes 1572872 | tf_op jit(solution)/shard_map/ppermute | solution.py:91
  171.1 23.7 %collective-permute-start.12 = (bf16[512,512]{1,0:T(8,128)(2,1)S(1)}, bf16[512,512]{1,0:T(8,128)(2,1)S(1)}, u32[]{:S(2)}, u32[]{:S(2)}) collective-permute-start(bf16[512,512]{1,0:T(8,128)(2,1)S(1)} %collective-permute-done.11), channel_id=1, source_target_pairs={{0,16},{16,64},{64,80},{80,128},{128,144},{144,192},{192,208},{208... | collective-permute-start | bytes 1572872 | tf_op jit(solution)/shard_map/ppermute | solution.py:91
  194.9 97.1 %copy-start.2 = (bf16[512,512]{1,0:T(8,128)(2,1)}, bf16[512,512]{1,0:T(8,128)(2,1)S(1)}, u32[]{:S(2)}) copy-start(bf16[512,512]{1,0:T(8,128)(2,1)S(1)} %collective-permute-done.12) | copy-start | bytes 1572868
  194.9 23.5 %collective-permute-start.13 = (bf16[512,512]{1,0:T(8,128)(2,1)S(1)}, bf16[512,512]{1,0:T(8,128)(2,1)S(1)}, u32[]{:S(2)}, u32[]{:S(2)}) collective-permute-start(bf16[512,512]{1,0:T(8,128)(2,1)S(1)} %collective-permute-done.12), channel_id=1, source_target_pairs={{0,16},{16,64},{64,80},{80,128},{128,144},{144,192},{192,208},{208... | collective-permute-start | bytes 1572872 | tf_op jit(solution)/shard_map/ppermute | solution.py:91
  218.3 21.4 %collective-permute-start.14 = (bf16[512,512]{1,0:T(8,128)(2,1)S(1)}, bf16[512,512]{1,0:T(8,128)(2,1)S(1)}, u32[]{:S(2)}, u32[]{:S(2)}) collective-permute-start(bf16[512,512]{1,0:T(8,128)(2,1)S(1)} %collective-permute-done.13), channel_id=1, source_target_pairs={{0,16},{16,64},{64,80},{80,128},{128,144},{144,192},{192,208},{208... | collective-permute-start | bytes 1572872 | tf_op jit(solution)/shard_map/ppermute | solution.py:91
  240.5 19.3 %collective-permute-start.15 = (bf16[512,512]{1,0:T(8,128)(2,1)S(1)}, bf16[512,512]{1,0:T(8,128)(2,1)}, u32[]{:S(2)}, u32[]{:S(2)}) collective-permute-start(bf16[512,512]{1,0:T(8,128)(2,1)S(1)} %collective-permute-done.14), channel_id=1, source_target_pairs={{0,16},{16,64},{64,80},{80,128},{128,144},{144,192},{192,208},{208... | collective-permute-start | bytes 1572872 | tf_op jit(solution)/shard_map/ppermute | solution.py:91
  259.9 20.1 %collective-permute-start.16 = (bf16[512,512]{1,0:T(8,128)(2,1)}, bf16[512,512]{1,0:T(8,128)(2,1)}, u32[]{:S(2)}, u32[]{:S(2)}) collective-permute-start(bf16[512,512]{1,0:T(8,128)(2,1)} %collective-permute-done.15), channel_id=1, source_target_pairs={{0,16},{16,64},{64,80},{80,128},{128,144},{144,192},{192,208},{208... | collective-permute-start | bytes 1572872 | tf_op jit(solution)/shard_map/ppermute | solution.py:91
  280.0 13.8 %collective-permute-start.17 = (bf16[512,512]{1,0:T(8,128)(2,1)}, bf16[512,512]{1,0:T(8,128)(2,1)S(1)}, u32[]{:S(2)}, u32[]{:S(2)}) collective-permute-start(bf16[512,512]{1,0:T(8,128)(2,1)} %collective-permute-done.16), channel_id=1, source_target_pairs={{0,16},{16,64},{64,80},{80,128},{128,144},{144,192},{192,208},{208... | collective-permute-start | bytes 1572872 | tf_op jit(solution)/shard_map/ppermute | solution.py:91
  293.8 12.8 %collective-permute-start.18 = (bf16[512,512]{1,0:T(8,128)(2,1)S(1)}, bf16[512,512]{1,0:T(8,128)(2,1)}, u32[]{:S(2)}, u32[]{:S(2)}) collective-permute-start(bf16[512,512]{1,0:T(8,128)(2,1)S(1)} %collective-permute-done.17), channel_id=1, source_target_pairs={{0,16},{16,64},{64,80},{80,128},{128,144},{144,192},{192,208},{208... | collective-permute-start | bytes 1572872 | tf_op jit(solution)/shard_map/ppermute | solution.py:91
  306.6 12.7 %collective-permute-start.19 = (bf16[512,512]{1,0:T(8,128)(2,1)}, bf16[512,512]{1,0:T(8,128)(2,1)}, u32[]{:S(2)}, u32[]{:S(2)}) collective-permute-start(bf16[512,512]{1,0:T(8,128)(2,1)} %collective-permute-done.18), channel_id=1, source_target_pairs={{0,16},{16,64},{64,80},{80,128},{128,144},{144,192},{192,208},{208... | collective-permute-start | bytes 1572872 | tf_op jit(solution)/shard_map/ppermute | solution.py:91
  319.3 15.7 %collective-permute-start.20 = (bf16[512,512]{1,0:T(8,128)(2,1)}, bf16[512,512]{1,0:T(8,128)(2,1)S(1)}, u32[]{:S(2)}, u32[]{:S(2)}) collective-permute-start(bf16[512,512]{1,0:T(8,128)(2,1)} %collective-permute-done.19), channel_id=1, source_target_pairs={{0,16},{16,64},{64,80},{80,128},{128,144},{144,192},{192,208},{208... | collective-permute-start | bytes 1572872 | tf_op jit(solution)/shard_map/ppermute | solution.py:91
  334.9 13.8 %collective-permute-start.21 = (bf16[512,512]{1,0:T(8,128)(2,1)S(1)}, bf16[512,512]{1,0:T(8,128)(2,1)S(1)}, u32[]{:S(2)}, u32[]{:S(2)}) collective-permute-start(bf16[512,512]{1,0:T(8,128)(2,1)S(1)} %collective-permute-done.20), channel_id=1, source_target_pairs={{0,16},{16,64},{64,80},{80,128},{128,144},{144,192},{192,208},{208... | collective-permute-start | bytes 1572872 | tf_op jit(solution)/shard_map/ppermute | solution.py:91
  348.8 11.4 %collective-permute-start.22 = (bf16[512,512]{1,0:T(8,128)(2,1)S(1)}, bf16[512,512]{1,0:T(8,128)(2,1)S(1)}, u32[]{:S(2)}, u32[]{:S(2)}) collective-permute-start(bf16[512,512]{1,0:T(8,128)(2,1)S(1)} %collective-permute-done.21), channel_id=1, source_target_pairs={{0,16},{16,64},{64,80},{80,128},{128,144},{144,192},{192,208},{208... | collective-permute-start | bytes 1572872 | tf_op jit(solution)/shard_map/ppermute | solution.py:91
  360.2 10.4 %collective-permute-start.23 = (bf16[512,512]{1,0:T(8,128)(2,1)S(1)}, bf16[512,512]{1,0:T(8,128)(2,1)S(1)}, u32[]{:S(2)}, u32[]{:S(2)}) collective-permute-start(bf16[512,512]{1,0:T(8,128)(2,1)S(1)} %collective-permute-done.22), channel_id=1, source_target_pairs={{0,16},{16,64},{64,80},{80,128},{128,144},{144,192},{192,208},{208... | collective-permute-start | bytes 1572872 | tf_op jit(solution)/shard_map/ppermute | solution.py:91
  402.5 5.3 collective-permute-start.8
  (5 other events, 109.8 us)
Sparse Core Ops, SparseCore 0:
  10.0 132.2 all-gather.2
  144.1 150.5 all-gather.4
  421.7 188.5 reduce-scatter.1

commit v7 on v5

--- a/solution.py
+++ b/solution.py
@@ -112,7 +112,7 @@
     key_cols = lax.dynamic_slice_in_dim(w_key, kv_index * HEAD_SIZE, HEAD_SIZE, 1)
     value_cols = lax.dynamic_slice_in_dim(value_weight, kv_index * HEAD_SIZE, HEAD_SIZE, 1)
     kv_cols = jnp.where(is_key_side, key_cols, value_cols)
-    packed = jnp.concatenate([w_query, kv_cols, w_out.T], axis=1)
+    packed = jnp.concatenate([w_query, kv_cols], axis=1)
     gathered = lax.all_gather(packed, DICT, axis=0, tiled=True)
     coef_list = [
         dense_codes(latent_ids, latent_vals, block_ids[number] * BLOCK)
@@ -132,9 +132,11 @@
     normed_cols = (widened * lax.rsqrt(mean_sq + EPSILON) * gain_cols).astype(jnp.bfloat16)
     normed_cols, gathered = lax.optimization_barrier((normed_cols, gathered))
     normed = lax.all_gather(normed_cols, "tensor", axis=2, tiled=True)
+    normed, out_local = lax.optimization_barrier((normed, w_out.T))
+    out_rows = lax.all_gather(out_local, DICT, axis=0, tiled=True)
     normed = normed.reshape(ABLATION_STEPS * row_count, full_width)
     qkv_cols = head_cols + HEAD_SIZE
-    qkv = jnp.dot(normed, gathered[:, :qkv_cols], preferred_element_type=jnp.float32)
+    qkv = jnp.dot(normed, gathered, preferred_element_type=jnp.float32)
     query_vec = qkv[:, :head_cols]
     kv_vector = qkv[:, head_cols:qkv_cols]
     prompt_count = row_count // PROMPT_ROWS
@@ -166,7 +168,7 @@
     context = context.astype(jnp.bfloat16).reshape(ABLATION_STEPS * row_count, head_cols)
     partial_value = lax.dot_general(
         context,
-        gathered[:, qkv_cols:],
+        out_rows,
         (((1,), (1,)), ((), ())),
         preferred_element_type=jnp.float32,
     ).astype(jnp.bfloat16)

time: 469 us -> 480 us (1.023)
  starting transfers between devices: 20.2 us -> 28.1 us
  waiting for transfers between devices: 378 us -> 384 us
  local copies, waits for them, and re-layouts: 10.8 us -> 5.3 us
    all_gather x1, waiting for transfers between devices: 141 us -> 55.6 us  [body(): gathered = lax.all_gather(packed, DICT, axis=0, tiled=True)]
    all_gather x0 -> x1, waiting for transfers between devices: none -> 85.5 us  [body(): out_rows = lax.all_gather(out_local, DICT, axis=0, tiled=True)]
    ppermute x4, starting transfers between devices: 9.49 us -> 16.9 us  [butterfly_sum(): value = value + lax.ppermute(value, axis, pairs)]
    all_gather x1, waiting for transfers between devices: 96.5 us -> 103 us  [body(): normed = lax.all_gather(normed_cols, 'tensor', axis=2, tiled=True)]
    ppermute x4, waiting for transfers between devices: 27.5 us -> 21.7 us  [fetch_blocks(): held = held + lax.ppermute(held, DICT, pairs)]
  transfers between devices with their start and end apart: 12 -> 13, of which waited for: 11 -> 12; matrix products, arithmetic and copies ran while one was open for 4% -> 8% of each run, Pallas kernels for 0% -> 0%
where the time goes in v7:
time: 480 us
  waiting for transfers between devices  384 us (80%)
  matrix products  28.4 us (6%)
  starting transfers between devices  28.1 us (6%)
  other arithmetic  18.8 us (4%)
  between operations  15.4 us (3%)
  local copies, waits for them, and re-layouts  5.3 us (1%)
    reduce_scatter x1, waiting for transfers between devices, body(): lax.psum_scatter(partial_value.astype(jnp.float32).astype(jnp.bfloat16),...  104 us
    all_gather x1, waiting for transfers between devices, body(): normed = lax.all_gather(normed_cols, 'tensor', axis=2, tiled=True)  103 us
    all_gather x1, waiting for transfers between devices, body(): out_rows = lax.all_gather(out_local, DICT, axis=0, tiled=True)  85.5 us
    all_gather x1, waiting for transfers between devices, body(): gathered = lax.all_gather(packed, DICT, axis=0, tiled=True)  55.6 us
    ppermute x4, waiting for transfers between devices, fetch_blocks(): held = held + lax.ppermute(held, DICT, pairs)  21.7 us
    ppermute x4, starting transfers between devices, butterfly_sum(): value = value + lax.ppermute(value, axis, pairs)  16.9 us
    dot_general x1, matrix products, body(): qkv = jnp.dot(normed, gathered, preferred_element_type=jnp.float32)  14.9 us
    ppermute x4, waiting for transfers between devices, butterfly_sum(): value = value + lax.ppermute(value, axis, pairs)  12.2 us
  transfers between devices with their start and end apart: 13, of which 12 were waited for; matrix products, arithmetic and copies ran while one was open for 8% of the time, Pallas kernels for 0%

profile of v7, /device:TPU:6, one launch (start us, length us, event | category | flops | bytes accessed | tf_op | source)
XLA Modules:
  0.0 479.7 jit_solution(9809218023293915304)
XLA Ops:
  6.5 1.1 dynamic-slice_select_fusion
  7.6 1.9 pad_maximum_fusion
  9.6 1.3 fusion.33
  12.3 1.0 select_bitcast_fusion.1
  13.5 1.5 collective-permute-done
  15.0 7.3 %collective-permute-start.1 = (bf16[2,128,512]{2,1,0:T(8,128)(2,1)S(1)}, bf16[2,128,512]{2,1,0:T(8,128)(2,1)S(1)}, u32[]{:S(2)}, u32[]{:S(2)}) collective-permute-start(bf16[2,128,512]{2,1,0:T(8,128)(2,1)S(1)} %fusion.31), channel_id=1, source_target_pairs={{0,32},{16,48},{32,0},{48,16},{64,96},{80,112},{96,64},{112,80},{1... | collective-permute-start | bytes 786440 | tf_op jit(solution)/shard_map/ppermute | solution.py:83
  22.3 16.5 %collective-permute-done.1 = bf16[2,128,512]{2,1,0:T(8,128)(2,1)S(1)} collective-permute-done((bf16[2,128,512]{2,1,0:T(8,128)(2,1)S(1)}, bf16[2,128,512]{2,1,0:T(8,128)(2,1)S(1)}, u32[]{:S(2)}, u32[]{:S(2)}) %collective-permute-start.1) | collective-permute-done | bytes 262176 | tf_op jit(solution)/shard_map/ppermute | solution.py:83
  38.8 0.9 collective-permute-start.2
  39.7 0.8 broadcast_subtract_fusion
  40.8 0.9 copy.42
  41.7 3.7 collective-permute-done.2
  45.5 2.5 collective-permute-start.3
  48.0 7.8 %select_reduce_fusion.1 = (bf16[256,128]{1,0:T(8,128)(2,1)S(1)}, bf16[256,128]{1,0:T(8,128)(2,1)S(1)}) fusion(f32[256,64]{1,0:T(8,128)S(1)} %copy.42, s32[256,64]{1,0:T(8,128)S(1)} %copy.41, s32[256,64]{1,0:T(8,128)S(1)} %copy.43), kind=kLoop, calls=%fused_computation.3 | loop fusion | flops 12517376 | bytes 327680 | tf_op jit(solution)/shard_map/reduce_sum | solution.py:41
  56.5 1.5 collective-permute-start.4
  58.0 2.1 collective-permute-done.4
  60.2 3.0 collective-permute-start.5
  63.2 2.1 collective-permute-done.5
  65.3 12.4 %collective-permute-start.6 = (f32[2,256,1]{1,0,2:T(2,128)S(1)}, f32[2,256,1]{1,0,2:T(2,128)S(1)}, u32[]{:S(2)}, u32[]{:S(2)}) collective-permute-start(f32[2,256,1]{1,0,2:T(2,128)S(1)} %add.84), channel_id=1, source_target_pairs={{0,4},{1,5},{2,6},{3,7},{4,0},{5,1},{6,2},{7,3},{8,12},{9,13},{10,... | collective-permute-start | bytes 6152 | tf_op jit(solution)/shard_map/ppermute | solution.py:67
  77.6 4.1 collective-permute-done.6
  81.7 0.8 dynamic_slice.17
  82.5 3.9 collective-permute-done.7
  86.4 1.0 multiply_convert_fusion
  87.4 55.6 %all-gather.4.cloned.1.call-done = bf16[8192,640]{1,0:T(8,128)(2,1)} async-done(((bf16[512,640]{1,0:T(8,128)(2,1)}), bf16[8192,640]{1,0:T(8,128)(2,1)}) %all-gather.4.cloned.1.call-update) | async-done | bytes 10485776 | tf_op jit(solution)/shard_map/all_gather | solution.py:116
  143.1 102.8 %all-gather.6.cloned.1.call-done = bf16[2,256,8192]{2,1,0:T(8,128)(2,1)} async-done(((bf16[2,256,512]{2,1,0:T(8,128)(2,1)}), bf16[2,256,8192]{2,1,0:T(8,128)(2,1)}) %all-gather.6.cloned.1.call-update) | async-done | bytes 8388624 | tf_op jit(solution)/shard_map/all_gather | solution.py:134
  247.5 14.9 %fusion.35 = f32[512,640]{1,0:T(8,128)S(1)} fusion(bf16[512,8192]{1,0:T(8,128)(2,1)} %bitcast.75, bf16[8192,640]{1,0:T(8,128)(2,1)} %all-gather.4.cloned.1.call-done), kind=kOutput, calls=%fused_computation.71 | convolution fusion | flops 5368709120 | bytes 20185088 | tf_op jit(solution)/shard_map/dot_general | solution.py:139
  264.0 1.6 copy_bitcast_fusion
  266.0 2.1 collective-permute-done.8
  268.1 2.4 fusion.34
  271.7 85.5 %all-gather.8.cloned.1.call-done = bf16[8192,512]{0,1:T(8,128)(2,1)} async-done(((bf16[512,512]{0,1:T(8,128)(2,1)}), bf16[8192,512]{0,1:T(8,128)(2,1)}) %all-gather.8.cloned.1.call-update) | async-done | bytes 8388624 | tf_op jit(solution)/shard_map/all_gather | solution.py:136
  357.2 10.1 %convolution_convert_fusion = bf16[512,8192]{1,0:T(8,128)(2,1)} fusion(bf16[8192,512]{0,1:T(8,128)(2,1)} %all-gather.8.cloned.1.call-done, bf16[64,8,4,128]{3,2,1,0:T(4,128)(2,1)S(1)} %bitcast.73), kind=kOutput, calls=%fused_computation | convolution fusion | flops 4299161600 | bytes 17301504 | tf_op jit(solution)/shard_map/dot_general | solution.py:169
  367.4 103.8 %reduce-scatter.2.cloned.1.call-done = bf16[512,512]{1,0:T(8,128)(2,1)} async-done(((bf16[512,8192]{1,0:T(8,128)(2,1)}), bf16[512,512]{1,0:T(8,128)(2,1)}) %reduce-scatter.2.cloned.1.call-update) | async-done | bytes 524304 | tf_op jit(solution)/shard_map/reduce_scatter | solution.py:175
  471.1 2.0 fusion.10
  (47 shorter events, 5.3 us)
Async XLA Ops:
  6.5 49.4 %copy-start = (bf16[256,512]{1,0:T(8,128)(2,1)S(1)}, bf16[256,512]{1,0:T(8,128)(2,1)}, u32[]{:S(2)}) copy-start(bf16[256,512]{1,0:T(8,128)(2,1)} %param.11) | copy-start | bytes 786436
  6.5 136.5 %all-gather.4.cloned.1.call-start = ((), (), s32[]{:S(2)}) async-start(), calls=%async_computation.1 | async-start | bytes 11141120 | tf_op jit(solution)/shard_map/all_gather | solution.py:116
  9.6 236.3 %all-gather.6.cloned.1.call-start = ((), (), s32[]{:S(2)}) async-start(), calls=%async_computation.2 | async-start | bytes 8912896 | tf_op jit(solution)/shard_map/all_gather | solution.py:134
  13.4 1.6 collective-permute-start
  15.0 23.8 %collective-permute-start.1 = (bf16[2,128,512]{2,1,0:T(8,128)(2,1)S(1)}, bf16[2,128,512]{2,1,0:T(8,128)(2,1)S(1)}, u32[]{:S(2)}, u32[]{:S(2)}) collective-permute-start(bf16[2,128,512]{2,1,0:T(8,128)(2,1)S(1)} %fusion.31), channel_id=1, source_target_pairs={{0,32},{16,48},{32,0},{48,16},{64,96},{80,112},{96,64},{112,80},{1... | collective-permute-start | bytes 786440 | tf_op jit(solution)/shard_map/ppermute | solution.py:83
  38.8 6.6 %collective-permute-start.2 = (bf16[2,128,512]{2,1,0:T(8,128)(2,1)S(1)}, bf16[2,128,512]{2,1,0:T(8,128)(2,1)S(1)}, u32[]{:S(2)}, u32[]{:S(2)}) collective-permute-start(bf16[2,128,512]{2,1,0:T(8,128)(2,1)S(1)} %fusion.41), channel_id=1, source_target_pairs={{0,64},{16,80},{32,96},{48,112},{64,0},{80,16},{96,32},{112,48},{1... | collective-permute-start | bytes 786440 | tf_op jit(solution)/shard_map/ppermute | solution.py:83
  45.5 10.3 %collective-permute-start.3 = (bf16[2,128,512]{2,1,0:T(8,128)(2,1)S(1)}, bf16[2,128,512]{2,1,0:T(8,128)(2,1)S(1)}, u32[]{:S(2)}, u32[]{:S(2)}) collective-permute-start(bf16[2,128,512]{2,1,0:T(8,128)(2,1)S(1)} %add.80), channel_id=1, source_target_pairs={{0,128},{16,144},{32,160},{48,176},{64,192},{80,208},{96,224},{112... | collective-permute-start | bytes 786440 | tf_op jit(solution)/shard_map/ppermute | solution.py:83
  56.5 3.7 collective-permute-start.4
  60.2 5.1 %collective-permute-start.5 = (f32[2,256,1]{1,0,2:T(2,128)S(1)}, f32[2,256,1]{1,0,2:T(2,128)S(1)}, u32[]{:S(2)}, u32[]{:S(2)}) collective-permute-start(f32[2,256,1]{1,0,2:T(2,128)S(1)} %bitcast_add_fusion.1), channel_id=1, source_target_pairs={{0,2},{1,3},{2,0},{3,1},{4,6},{5,7},{6,4},{7,5},{8,10},{9,11},{10,... | collective-permute-start | bytes 6152 | tf_op jit(solution)/shard_map/ppermute | solution.py:67
  65.3 16.5 %collective-permute-start.6 = (f32[2,256,1]{1,0,2:T(2,128)S(1)}, f32[2,256,1]{1,0,2:T(2,128)S(1)}, u32[]{:S(2)}, u32[]{:S(2)}) collective-permute-start(f32[2,256,1]{1,0,2:T(2,128)S(1)} %add.84), channel_id=1, source_target_pairs={{0,4},{1,5},{2,6},{3,7},{4,0},{5,1},{6,2},{7,3},{8,12},{9,13},{10,... | collective-permute-start | bytes 6152 | tf_op jit(solution)/shard_map/ppermute | solution.py:67
  81.7 4.7 collective-permute-start.7
  143.1 214.1 %all-gather.8.cloned.1.call-start = ((), (), s32[]{:S(2)}) async-start(), calls=%async_computation.3 | async-start | bytes 8912896 | tf_op jit(solution)/shard_map/all_gather | solution.py:136
  245.9 225.3 %reduce-scatter.2.cloned.1.call-start = ((), (), s32[]{:S(2)}) async-start(), calls=%async_computation.4 | async-start | bytes 8912896 | tf_op jit(solution)/shard_map/reduce_scatter | solution.py:175
  262.8 5.3 %collective-permute-start.8 = (bf16[2,1,256,128]{2,3,0,1:T(8,128)(2,1)S(1)}, bf16[2,1,256,128]{2,3,0,1:T(8,128)(2,1)S(1)}, u32[]{:S(2)}, u32[]{:S(2)}) collective-permute-start(bf16[2,1,256,128]{2,3,0,1:T(8,128)(2,1)S(1)} %fusion.18), channel_id=1, source_target_pairs={{0,1},{1,0},{2,3},{3,2},{4,5},{5,4},{6,7},{7,6},{8,9},{9,8},{10,11... | collective-permute-start | bytes 393224 | tf_op jit(solution)/shard_map/ppermute | solution.py:153
Sparse Core Ops, SparseCore 0:
  10.0 132.9 all-gather.3
  144.8 100.9 all-gather.5
  248.4 108.7 all-gather.7
  367.4 103.6 reduce-scatter.1

commit v8 on v5

--- a/solution.py
+++ b/solution.py
@@ -49,15 +49,18 @@
     return (lax.dynamic_slice_in_dim(decoder, row_offset, BLOCK, 0), owner_dict)
 
 
-DICT = ("dict_hi", "core")
+DICT = ("dict_x", "dict_z", "core")
+DICT_RING = ("dict_z", "dict_x", "core")
 
 
 def dict_index():
-    return lax.axis_index("dict_hi") * lax.axis_size("core") + lax.axis_index("core")
+    return (lax.axis_index("dict_x") * lax.axis_size("dict_z") + lax.axis_index("dict_z")) * lax.axis_size(
+        "core"
+    ) + lax.axis_index("core")
 
 
 def dict_size():
-    return lax.axis_size("dict_hi") * lax.axis_size("core")
+    return lax.axis_size("dict_x") * lax.axis_size("dict_z") * lax.axis_size("core")
 
 
 def butterfly_sum(value, axis, count):
@@ -113,7 +116,7 @@
     value_cols = lax.dynamic_slice_in_dim(value_weight, kv_index * HEAD_SIZE, HEAD_SIZE, 1)
     kv_cols = jnp.where(is_key_side, key_cols, value_cols)
     packed = jnp.concatenate([w_query, kv_cols, w_out.T], axis=1)
-    gathered = lax.all_gather(packed, DICT, axis=0, tiled=True)
+    ring_gathered = lax.all_gather(packed, DICT_RING, axis=0, tiled=True)
     coef_list = [
         dense_codes(latent_ids, latent_vals, block_ids[number] * BLOCK)
         for number in range(ABLATION_STEPS)
@@ -130,7 +133,12 @@
     mean_sq = sum_sq / full_width
     gain_cols = lax.dynamic_slice_in_dim(norm_gain, tensor_pos * col_count, col_count)
     normed_cols = (widened * lax.rsqrt(mean_sq + EPSILON) * gain_cols).astype(jnp.bfloat16)
-    normed_cols, gathered = lax.optimization_barrier((normed_cols, gathered))
+    normed_cols, ring_gathered = lax.optimization_barrier((normed_cols, ring_gathered))
+    x_count = lax.axis_size("dict_x")
+    z_count = lax.axis_size("dict_z")
+    core_count = lax.axis_size("core")
+    gathered = ring_gathered.reshape((z_count, x_count, core_count) + packed.shape)
+    gathered = jnp.transpose(gathered, (1, 0, 2, 3, 4)).reshape(-1, packed.shape[1])
     normed = lax.all_gather(normed_cols, "tensor", axis=2, tiled=True)
     normed = normed.reshape(ABLATION_STEPS * row_count, full_width)
     qkv_cols = head_cols + HEAD_SIZE
@@ -183,8 +191,10 @@
 def solution(mesh):
     dict_count = mesh.shape["dict"]
     core_count = 2 if dict_count % 2 == 0 else 1
-    devices = mesh.devices.reshape(dict_count // core_count, core_count, mesh.shape["tensor"])
-    fine = jax.sharding.Mesh(devices, ("dict_hi", "core", "tensor"))
+    z_count = 2 if dict_count % (2 * core_count) == 0 else 1
+    x_count = dict_count // (core_count * z_count)
+    devices = mesh.devices.reshape(x_count, z_count, core_count, mesh.shape["tensor"])
+    fine = jax.sharding.Mesh(devices, ("dict_x", "dict_z", "core", "tensor"))
     in_specs = (
         P(DICT, "tensor"),
         P(),

time: 469 us -> 457 us (0.974)
  waiting for transfers between devices: 378 us -> 351 us
  local copies, waits for them, and re-layouts: 10.8 us -> 21.8 us
    transpose x0 -> x1, local copies, waits for them, and re-layouts: none -> 16.8 us  [body(): jnp.transpose(gathered, (1, 0, 2, 3, 4)).reshape(-1, packed.shape[1])]
    all_gather x1, waiting for transfers between devices: 96.5 us -> 81.7 us  [body(): normed = lax.all_gather(normed_cols, 'tensor', axis=2, tiled=True)]
    all_gather x1, waiting for transfers between devices: 141 us -> 130 us  [body(): ring_gathered = lax.all_gather(packed, DICT_RING, axis=0, tiled=True)]
  transfers between devices with their start and end apart: 12 -> 12, of which waited for: 11 -> 11; matrix products, arithmetic and copies ran while one was open for 4% -> 7% of each run, Pallas kernels for 0% -> 0%
where the time goes in v8:
time: 457 us
  waiting for transfers between devices  351 us (77%)
  matrix products  28.1 us (6%)
  starting transfers between devices  22.5 us (5%)
  local copies, waits for them, and re-layouts  21.8 us (5%)
  other arithmetic  18.2 us (4%)
  between operations  15.4 us (3%)
    all_gather x1, waiting for transfers between devices, body(): ring_gathered = lax.all_gather(packed, DICT_RING, axis=0, tiled=True)  130 us
    reduce_scatter x1, waiting for transfers between devices, body(): lax.psum_scatter(partial_value.astype(jnp.float32).astype(jnp.bfloat16),...  105 us
    all_gather x1, waiting for transfers between devices, body(): normed = lax.all_gather(normed_cols, 'tensor', axis=2, tiled=True)  81.7 us
    ppermute x4, waiting for transfers between devices, fetch_blocks(): held = held + lax.ppermute(held, DICT, pairs)  27 us
    transpose x1, local copies, waits for them, and re-layouts, body(): jnp.transpose(gathered, (1, 0, 2, 3, 4)).reshape(-1, packed.shape[1])  16.8 us
    dot_general x1, matrix products, body(): jnp.dot(normed, gathered[:, :qkv_cols], preferred_element_type=jnp.float32)  14.5 us
    ppermute x4, starting transfers between devices, butterfly_sum(): value = value + lax.ppermute(value, axis, pairs)  13.7 us
    dot_general x1, matrix products, body(): lax.dot_general(context, gathered[:, qkv_cols:], (((1,), (1,)), ((), ()))...  10.2 us
  transfers between devices with their start and end apart: 12, of which 11 were waited for; matrix products, arithmetic and copies ran while one was open for 7% of the time, Pallas kernels for 0%

profile of v8, /device:TPU:6, one launch (start us, length us, event | category | flops | bytes accessed | tf_op | source)
XLA Modules:
  0.0 456.7 jit_solution(10597871949625409028)
XLA Ops:
  6.5 1.3 copy.67
  7.8 1.0 dynamic-slice_select_fusion
  8.8 2.2 pad_maximum_fusion
  11.1 0.6 fusion.36
  13.0 1.0 select_bitcast_fusion.1
  14.2 1.5 collective-permute-done
  15.8 7.3 %collective-permute-start.1 = (bf16[2,128,512]{2,1,0:T(8,128)(2,1)S(1)}, bf16[2,128,512]{2,1,0:T(8,128)(2,1)S(1)}, u32[]{:S(2)}, u32[]{:S(2)}) collective-permute-start(bf16[2,128,512]{2,1,0:T(8,128)(2,1)S(1)} %fusion.34), channel_id=1, source_target_pairs={{0,32},{16,48},{32,0},{48,16},{64,96},{80,112},{96,64},{112,80},{1... | collective-permute-start | bytes 786440 | tf_op jit(solution)/shard_map/ppermute | solution.py:86
  23.1 16.6 %collective-permute-done.1 = bf16[2,128,512]{2,1,0:T(8,128)(2,1)S(1)} collective-permute-done((bf16[2,128,512]{2,1,0:T(8,128)(2,1)S(1)}, bf16[2,128,512]{2,1,0:T(8,128)(2,1)S(1)}, u32[]{:S(2)}, u32[]{:S(2)}) %collective-permute-start.1) | collective-permute-done | bytes 262176 | tf_op jit(solution)/shard_map/ppermute | solution.py:86
  39.7 1.0 collective-permute-start.2
  41.0 8.9 %collective-permute-done.2 = bf16[2,128,512]{2,1,0:T(8,128)(2,1)S(1)} collective-permute-done((bf16[2,128,512]{2,1,0:T(8,128)(2,1)S(1)}, bf16[2,128,512]{2,1,0:T(8,128)(2,1)S(1)}, u32[]{:S(2)}, u32[]{:S(2)}) %collective-permute-start.2) | collective-permute-done | bytes 262176 | tf_op jit(solution)/shard_map/ppermute | solution.py:86
  50.1 7.8 %select_reduce_fusion.1 = (bf16[256,128]{1,0:T(8,128)(2,1)S(1)}, bf16[256,128]{1,0:T(8,128)(2,1)S(1)}) fusion(f32[256,64]{1,0:T(8,128)S(1)} %copy.65, s32[256,64]{1,0:T(8,128)S(1)} %copy.64, s32[256,64]{1,0:T(8,128)S(1)} %copy.66), kind=kLoop, calls=%fused_computation.6 | loop fusion | flops 12517376 | bytes 327680 | tf_op jit(solution)/shard_map/reduce_sum | solution.py:41
  58.6 2.2 collective-permute-start.4
  60.9 1.6 collective-permute-done.4
  62.4 3.5 collective-permute-start.5
  65.9 1.6 collective-permute-done.5
  67.5 4.9 %collective-permute-start.6 = (f32[2,256,1]{1,0,2:T(2,128)S(1)}, f32[2,256,1]{1,0,2:T(2,128)S(1)}, u32[]{:S(2)}, u32[]{:S(2)}) collective-permute-start(f32[2,256,1]{1,0,2:T(2,128)S(1)} %add.88), channel_id=1, source_target_pairs={{0,4},{1,5},{2,6},{3,7},{4,0},{5,1},{6,2},{7,3},{8,12},{9,13},{10,... | collective-permute-start | bytes 6152 | tf_op jit(solution)/shard_map/ppermute | solution.py:70
  72.4 1.6 collective-permute-done.6
  74.0 3.1 collective-permute-start.7
  77.1 0.8 dynamic_slice.17
  77.8 0.8 collective-permute-done.7
  78.6 1.0 multiply_convert_fusion
  79.6 129.5 %all-gather.3.cloned.1.call-done = bf16[8192,1152]{1,0:T(8,128)(2,1)} async-done(((bf16[512,1152]{1,0:T(8,128)(2,1)}), bf16[8192,1152]{1,0:T(8,128)(2,1)}) %all-gather.3.cloned.1.call-update) | async-done | bytes 18874384 | tf_op jit(solution)/shard_map/all_gather | solution.py:119
  210.8 16.8 %copy.68 = bf16[4,2,2,512,1152]{4,3,2,1,0:T(8,128)(2,1)} copy(bf16[4,2,2,512,1152]{4,3,2,0,1:T(8,128)(2,1)} %bitcast.73) | data formatting | bytes 37748736 | tf_op jit(solution)/shard_map/transpose | solution.py:141
  227.6 81.7 %all-gather.5.cloned.1.call-done = bf16[2,256,8192]{2,1,0:T(8,128)(2,1)} async-done(((bf16[2,256,512]{2,1,0:T(8,128)(2,1)}), bf16[2,256,8192]{2,1,0:T(8,128)(2,1)}) %all-gather.5.cloned.1.call-update) | async-done | bytes 8388624 | tf_op jit(solution)/shard_map/all_gather | solution.py:142
  309.3 14.5 %fusion = f32[512,640]{1,0:T(8,128)S(1)} fusion(bf16[512,8192]{1,0:T(8,128)(2,1)} %bitcast.80, bf16[8192,1152]{1,0:T(8,128)(2,1)} %bitcast.74), kind=kOutput, calls=%fused_computation.1 | convolution fusion | flops 5368709120 | bytes 20185088 | tf_op jit(solution)/shard_map/dot_general | solution.py:145
  324.9 0.6 fusion.35
  325.5 1.6 copy_bitcast_fusion
  327.5 2.1 collective-permute-done.8
  329.6 2.4 fusion.37
  333.2 10.2 %convolution_convert_fusion = bf16[512,8192]{1,0:T(8,128)(2,1)} fusion(bf16[8192,1152]{1,0:T(8,128)(2,1)} %bitcast.75, bf16[64,8,4,128]{3,2,1,0:T(4,128)(2,1)S(1)} %bitcast.78), kind=kOutput, calls=%fused_computation | convolution fusion | flops 4299161600 | bytes 17301504 | tf_op jit(solution)/shard_map/dot_general | solution.py:175
  343.5 104.7 %reduce-scatter.2.cloned.1.call-done = bf16[512,512]{1,0:T(8,128)(2,1)} async-done(((bf16[512,8192]{1,0:T(8,128)(2,1)}), bf16[512,512]{1,0:T(8,128)(2,1)}) %reduce-scatter.2.cloned.1.call-update) | async-done | bytes 524304 | tf_op jit(solution)/shard_map/reduce_scatter | solution.py:181
  448.1 2.0 fusion.13
  (52 shorter events, 4.9 us)
Async XLA Ops:
  6.5 202.6 %all-gather.3.cloned.1.call-start = ((), (), s32[]{:S(2)}) async-start(), calls=%async_computation.1 | async-start | bytes 20054016 | tf_op jit(solution)/shard_map/all_gather | solution.py:119
  6.5 4.5 copy-start.3
  11.0 29.7 %copy-start.1 = (s32[256,64]{0,1:T(8,128)S(1)}, s32[256,64]{0,1:T(8,128)}, u32[]{:S(2)}) copy-start(s32[256,64]{0,1:T(8,128)} %param.19) | copy-start | bytes 196612
  11.0 29.9 %copy-start.2 = (f32[256,64]{0,1:T(8,128)S(1)}, f32[256,64]{0,1:T(8,128)}, u32[]{:S(2)}) copy-start(f32[256,64]{0,1:T(8,128)} %param.20) | copy-start | bytes 196612
  11.0 298.3 %all-gather.5.cloned.1.call-start = ((), (), s32[]{:S(2)}) async-start(), calls=%async_computation.2 | async-start | bytes 8912896 | tf_op jit(solution)/shard_map/all_gather | solution.py:142
  14.1 43.9 %copy-start = (bf16[256,512]{1,0:T(8,128)(2,1)S(1)}, bf16[256,512]{1,0:T(8,128)(2,1)}, u32[]{:S(2)}) copy-start(bf16[256,512]{1,0:T(8,128)(2,1)} %param.11) | copy-start | bytes 786436
  14.1 1.6 collective-permute-start
  15.8 23.9 %collective-permute-start.1 = (bf16[2,128,512]{2,1,0:T(8,128)(2,1)S(1)}, bf16[2,128,512]{2,1,0:T(8,128)(2,1)S(1)}, u32[]{:S(2)}, u32[]{:S(2)}) collective-permute-start(bf16[2,128,512]{2,1,0:T(8,128)(2,1)S(1)} %fusion.34), channel_id=1, source_target_pairs={{0,32},{16,48},{32,0},{48,16},{64,96},{80,112},{96,64},{112,80},{1... | collective-permute-start | bytes 786440 | tf_op jit(solution)/shard_map/ppermute | solution.py:86
  39.7 10.2 %collective-permute-start.2 = (bf16[2,128,512]{2,1,0:T(8,128)(2,1)S(1)}, bf16[2,128,512]{2,1,0:T(8,128)(2,1)S(1)}, u32[]{:S(2)}, u32[]{:S(2)}) collective-permute-start(bf16[2,128,512]{2,1,0:T(8,128)(2,1)S(1)} %fusion.41), channel_id=1, source_target_pairs={{0,64},{16,80},{32,96},{48,112},{64,0},{80,16},{96,32},{112,48},{1... | collective-permute-start | bytes 786440 | tf_op jit(solution)/shard_map/ppermute | solution.py:86
  50.0 8.0 %collective-permute-start.3 = (bf16[2,128,512]{2,1,0:T(8,128)(2,1)S(1)}, bf16[2,128,512]{2,1,0:T(8,128)(2,1)S(1)}, u32[]{:S(2)}, u32[]{:S(2)}) collective-permute-start(bf16[2,128,512]{2,1,0:T(8,128)(2,1)S(1)} %add.84), channel_id=1, source_target_pairs={{0,128},{16,144},{32,160},{48,176},{64,192},{80,208},{96,224},{112... | collective-permute-start | bytes 786440 | tf_op jit(solution)/shard_map/ppermute | solution.py:86
  58.6 3.8 collective-permute-start.4
  62.4 5.1 %collective-permute-start.5 = (f32[2,256,1]{1,0,2:T(2,128)S(1)}, f32[2,256,1]{1,0,2:T(2,128)S(1)}, u32[]{:S(2)}, u32[]{:S(2)}) collective-permute-start(f32[2,256,1]{1,0,2:T(2,128)S(1)} %bitcast_add_fusion.1), channel_id=1, source_target_pairs={{0,2},{1,3},{2,0},{3,1},{4,6},{5,7},{6,4},{7,5},{8,10},{9,11},{10,... | collective-permute-start | bytes 6152 | tf_op jit(solution)/shard_map/ppermute | solution.py:70
  67.5 6.5 %collective-permute-start.6 = (f32[2,256,1]{1,0,2:T(2,128)S(1)}, f32[2,256,1]{1,0,2:T(2,128)S(1)}, u32[]{:S(2)}, u32[]{:S(2)}) collective-permute-start(f32[2,256,1]{1,0,2:T(2,128)S(1)} %add.88), channel_id=1, source_target_pairs={{0,4},{1,5},{2,6},{3,7},{4,0},{5,1},{6,2},{7,3},{8,12},{9,13},{10,... | collective-permute-start | bytes 6152 | tf_op jit(solution)/shard_map/ppermute | solution.py:70
  74.0 4.6 %collective-permute-start.7 = (f32[2,256,1]{1,0,2:T(2,128)S(1)}, f32[2,256,1]{1,0,2:T(2,128)S(1)}, u32[]{:S(2)}, u32[]{:S(2)}) collective-permute-start(f32[2,256,1]{1,0,2:T(2,128)S(1)} %add.89), channel_id=1, source_target_pairs={{0,8},{1,9},{2,10},{3,11},{4,12},{5,13},{6,14},{7,15},{8,0},{9,1},... | collective-permute-start | bytes 6152 | tf_op jit(solution)/shard_map/ppermute | solution.py:70
  209.2 238.9 %reduce-scatter.2.cloned.1.call-start = ((), (), s32[]{:S(2)}) async-start(), calls=%async_computation.3 | async-start | bytes 8912896 | tf_op jit(solution)/shard_map/reduce_scatter | solution.py:181
  324.3 5.3 %collective-permute-start.8 = (bf16[2,1,256,128]{2,3,0,1:T(8,128)(2,1)S(1)}, bf16[2,1,256,128]{2,3,0,1:T(8,128)(2,1)S(1)}, u32[]{:S(2)}, u32[]{:S(2)}) collective-permute-start(bf16[2,1,256,128]{2,3,0,1:T(8,128)(2,1)S(1)} %fusion.21), channel_id=1, source_target_pairs={{0,1},{1,0},{2,3},{3,2},{4,5},{5,4},{6,7},{7,6},{8,9},{9,8},{10,11... | collective-permute-start | bytes 393224 | tf_op jit(solution)/shard_map/ppermute | solution.py:159
Sparse Core Ops, SparseCore 0:
  11.1 197.9 all-gather.2
  210.9 98.3 all-gather.4
  343.5 104.5 reduce-scatter.1

commit v9 on v8

--- a/solution.py
+++ b/solution.py
@@ -50,7 +50,7 @@
 
 
 DICT = ("dict_x", "dict_z", "core")
-DICT_RING = ("dict_z", "dict_x", "core")
+DICT_RING = ("dict_z", "core", "dict_x")
 
 
 def dict_index():
@@ -137,8 +137,8 @@
     x_count = lax.axis_size("dict_x")
     z_count = lax.axis_size("dict_z")
     core_count = lax.axis_size("core")
-    gathered = ring_gathered.reshape((z_count, x_count, core_count) + packed.shape)
-    gathered = jnp.transpose(gathered, (1, 0, 2, 3, 4)).reshape(-1, packed.shape[1])
+    gathered = ring_gathered.reshape((z_count, core_count, x_count) + packed.shape)
+    gathered = jnp.transpose(gathered, (2, 0, 1, 3, 4)).reshape(-1, packed.shape[1])
     normed = lax.all_gather(normed_cols, "tensor", axis=2, tiled=True)
     normed = normed.reshape(ABLATION_STEPS * row_count, full_width)
     qkv_cols = head_cols + HEAD_SIZE

time: 457 us -> 457 us (level)
  no operation moved by 1% of the time
where the time goes in v9:
time: 457 us
  waiting for transfers between devices  351 us (77%)
  matrix products  28.1 us (6%)
  starting transfers between devices  22.5 us (5%)
  local copies, waits for them, and re-layouts  21.8 us (5%)
  other arithmetic  18.2 us (4%)
  between operations  15.4 us (3%)
    all_gather x1, waiting for transfers between devices, body(): ring_gathered = lax.all_gather(packed, DICT_RING, axis=0, tiled=True)  130 us
    reduce_scatter x1, waiting for transfers between devices, body(): lax.psum_scatter(partial_value.astype(jnp.float32).astype(jnp.bfloat16),...  105 us
    all_gather x1, waiting for transfers between devices, body(): normed = lax.all_gather(normed_cols, 'tensor', axis=2, tiled=True)  81.7 us
    ppermute x4, waiting for transfers between devices, fetch_blocks(): held = held + lax.ppermute(held, DICT, pairs)  27 us
    transpose x1, local copies, waits for them, and re-layouts, body(): jnp.transpose(gathered, (2, 0, 1, 3, 4)).reshape(-1, packed.shape[1])  16.8 us
    dot_general x1, matrix products, body(): jnp.dot(normed, gathered[:, :qkv_cols], preferred_element_type=jnp.float32)  14.5 us
    ppermute x4, starting transfers between devices, butterfly_sum(): value = value + lax.ppermute(value, axis, pairs)  13.7 us
    dot_general x1, matrix products, body(): lax.dot_general(context, gathered[:, qkv_cols:], (((1,), (1,)), ((), ()))...  10.2 us
  transfers between devices with their start and end apart: 12, of which 11 were waited for; matrix products, arithmetic and copies ran while one was open for 7% of the time, Pallas kernels for 0%

profile of v9, /device:TPU:6, one launch (start us, length us, event | category | flops | bytes accessed | tf_op | source)
XLA Modules:
  0.0 456.7 jit_solution(7599784094827931474)
XLA Ops:
  6.5 1.3 copy.67
  7.8 1.0 dynamic-slice_select_fusion
  8.8 2.2 pad_maximum_fusion
  11.1 0.6 fusion.36
  13.0 1.0 select_bitcast_fusion.1
  14.2 1.5 collective-permute-done
  15.8 7.3 %collective-permute-start.1 = (bf16[2,128,512]{2,1,0:T(8,128)(2,1)S(1)}, bf16[2,128,512]{2,1,0:T(8,128)(2,1)S(1)}, u32[]{:S(2)}, u32[]{:S(2)}) collective-permute-start(bf16[2,128,512]{2,1,0:T(8,128)(2,1)S(1)} %fusion.34), channel_id=1, source_target_pairs={{0,32},{16,48},{32,0},{48,16},{64,96},{80,112},{96,64},{112,80},{1... | collective-permute-start | bytes 786440 | tf_op jit(solution)/shard_map/ppermute | solution.py:86
  23.1 16.6 %collective-permute-done.1 = bf16[2,128,512]{2,1,0:T(8,128)(2,1)S(1)} collective-permute-done((bf16[2,128,512]{2,1,0:T(8,128)(2,1)S(1)}, bf16[2,128,512]{2,1,0:T(8,128)(2,1)S(1)}, u32[]{:S(2)}, u32[]{:S(2)}) %collective-permute-start.1) | collective-permute-done | bytes 262176 | tf_op jit(solution)/shard_map/ppermute | solution.py:86
  39.7 1.0 collective-permute-start.2
  41.0 8.9 %collective-permute-done.2 = bf16[2,128,512]{2,1,0:T(8,128)(2,1)S(1)} collective-permute-done((bf16[2,128,512]{2,1,0:T(8,128)(2,1)S(1)}, bf16[2,128,512]{2,1,0:T(8,128)(2,1)S(1)}, u32[]{:S(2)}, u32[]{:S(2)}) %collective-permute-start.2) | collective-permute-done | bytes 262176 | tf_op jit(solution)/shard_map/ppermute | solution.py:86
  50.1 7.8 %select_reduce_fusion.1 = (bf16[256,128]{1,0:T(8,128)(2,1)S(1)}, bf16[256,128]{1,0:T(8,128)(2,1)S(1)}) fusion(f32[256,64]{1,0:T(8,128)S(1)} %copy.65, s32[256,64]{1,0:T(8,128)S(1)} %copy.64, s32[256,64]{1,0:T(8,128)S(1)} %copy.66), kind=kLoop, calls=%fused_computation.6 | loop fusion | flops 12517376 | bytes 327680 | tf_op jit(solution)/shard_map/reduce_sum | solution.py:41
  58.6 2.2 collective-permute-start.4
  60.9 1.6 collective-permute-done.4
  62.4 3.5 collective-permute-start.5
  66.0 1.6 collective-permute-done.5
  67.5 4.9 %collective-permute-start.6 = (f32[2,256,1]{1,0,2:T(2,128)S(1)}, f32[2,256,1]{1,0,2:T(2,128)S(1)}, u32[]{:S(2)}, u32[]{:S(2)}) collective-permute-start(f32[2,256,1]{1,0,2:T(2,128)S(1)} %add.88), channel_id=1, source_target_pairs={{0,4},{1,5},{2,6},{3,7},{4,0},{5,1},{6,2},{7,3},{8,12},{9,13},{10,... | collective-permute-start | bytes 6152 | tf_op jit(solution)/shard_map/ppermute | solution.py:70
  72.4 1.6 collective-permute-done.6
  74.0 3.1 collective-permute-start.7
  77.1 0.8 dynamic_slice.17
  77.8 0.8 collective-permute-done.7
  78.6 1.0 multiply_convert_fusion
  79.6 129.5 %all-gather.3.cloned.1.call-done = bf16[8192,1152]{1,0:T(8,128)(2,1)} async-done(((bf16[512,1152]{1,0:T(8,128)(2,1)}), bf16[8192,1152]{1,0:T(8,128)(2,1)}) %all-gather.3.cloned.1.call-update) | async-done | bytes 18874384 | tf_op jit(solution)/shard_map/all_gather | solution.py:119
  210.8 16.8 %copy.68 = bf16[4,2,2,512,1152]{4,3,2,1,0:T(8,128)(2,1)} copy(bf16[4,2,2,512,1152]{4,3,0,2,1:T(8,128)(2,1)} %bitcast.73) | data formatting | bytes 37748736 | tf_op jit(solution)/shard_map/transpose | solution.py:141
  227.6 81.7 %all-gather.5.cloned.1.call-done = bf16[2,256,8192]{2,1,0:T(8,128)(2,1)} async-done(((bf16[2,256,512]{2,1,0:T(8,128)(2,1)}), bf16[2,256,8192]{2,1,0:T(8,128)(2,1)}) %all-gather.5.cloned.1.call-update) | async-done | bytes 8388624 | tf_op jit(solution)/shard_map/all_gather | solution.py:142
  309.3 14.5 %fusion = f32[512,640]{1,0:T(8,128)S(1)} fusion(bf16[512,8192]{1,0:T(8,128)(2,1)} %bitcast.80, bf16[8192,1152]{1,0:T(8,128)(2,1)} %bitcast.74), kind=kOutput, calls=%fused_computation.1 | convolution fusion | flops 5368709120 | bytes 20185088 | tf_op jit(solution)/shard_map/dot_general | solution.py:145
  324.9 0.6 fusion.35
  325.5 1.6 copy_bitcast_fusion
  327.5 2.1 collective-permute-done.8
  329.6 2.4 fusion.37
  333.2 10.2 %convolution_convert_fusion = bf16[512,8192]{1,0:T(8,128)(2,1)} fusion(bf16[8192,1152]{1,0:T(8,128)(2,1)} %bitcast.75, bf16[64,8,4,128]{3,2,1,0:T(4,128)(2,1)S(1)} %bitcast.78), kind=kOutput, calls=%fused_computation | convolution fusion | flops 4299161600 | bytes 17301504 | tf_op jit(solution)/shard_map/dot_general | solution.py:175
  343.5 104.7 %reduce-scatter.2.cloned.1.call-done = bf16[512,512]{1,0:T(8,128)(2,1)} async-done(((bf16[512,8192]{1,0:T(8,128)(2,1)}), bf16[512,512]{1,0:T(8,128)(2,1)}) %reduce-scatter.2.cloned.1.call-update) | async-done | bytes 524304 | tf_op jit(solution)/shard_map/reduce_scatter | solution.py:181
  448.1 2.0 fusion.13
  (52 shorter events, 5.0 us)
Async XLA Ops:
  6.5 202.6 %all-gather.3.cloned.1.call-start = ((), (), s32[]{:S(2)}) async-start(), calls=%async_computation.1 | async-start | bytes 20054016 | tf_op jit(solution)/shard_map/all_gather | solution.py:119
  6.5 4.5 copy-start.3
  11.0 29.7 %copy-start.1 = (s32[256,64]{0,1:T(8,128)S(1)}, s32[256,64]{0,1:T(8,128)}, u32[]{:S(2)}) copy-start(s32[256,64]{0,1:T(8,128)} %param.19) | copy-start | bytes 196612
  11.0 29.9 %copy-start.2 = (f32[256,64]{0,1:T(8,128)S(1)}, f32[256,64]{0,1:T(8,128)}, u32[]{:S(2)}) copy-start(f32[256,64]{0,1:T(8,128)} %param.20) | copy-start | bytes 196612
  11.0 298.3 %all-gather.5.cloned.1.call-start = ((), (), s32[]{:S(2)}) async-start(), calls=%async_computation.2 | async-start | bytes 8912896 | tf_op jit(solution)/shard_map/all_gather | solution.py:142
  14.1 43.9 %copy-start = (bf16[256,512]{1,0:T(8,128)(2,1)S(1)}, bf16[256,512]{1,0:T(8,128)(2,1)}, u32[]{:S(2)}) copy-start(bf16[256,512]{1,0:T(8,128)(2,1)} %param.11) | copy-start | bytes 786436
  14.1 1.6 collective-permute-start
  15.8 23.9 %collective-permute-start.1 = (bf16[2,128,512]{2,1,0:T(8,128)(2,1)S(1)}, bf16[2,128,512]{2,1,0:T(8,128)(2,1)S(1)}, u32[]{:S(2)}, u32[]{:S(2)}) collective-permute-start(bf16[2,128,512]{2,1,0:T(8,128)(2,1)S(1)} %fusion.34), channel_id=1, source_target_pairs={{0,32},{16,48},{32,0},{48,16},{64,96},{80,112},{96,64},{112,80},{1... | collective-permute-start | bytes 786440 | tf_op jit(solution)/shard_map/ppermute | solution.py:86
  39.7 10.2 %collective-permute-start.2 = (bf16[2,128,512]{2,1,0:T(8,128)(2,1)S(1)}, bf16[2,128,512]{2,1,0:T(8,128)(2,1)S(1)}, u32[]{:S(2)}, u32[]{:S(2)}) collective-permute-start(bf16[2,128,512]{2,1,0:T(8,128)(2,1)S(1)} %fusion.41), channel_id=1, source_target_pairs={{0,64},{16,80},{32,96},{48,112},{64,0},{80,16},{96,32},{112,48},{1... | collective-permute-start | bytes 786440 | tf_op jit(solution)/shard_map/ppermute | solution.py:86
  50.0 8.0 %collective-permute-start.3 = (bf16[2,128,512]{2,1,0:T(8,128)(2,1)S(1)}, bf16[2,128,512]{2,1,0:T(8,128)(2,1)S(1)}, u32[]{:S(2)}, u32[]{:S(2)}) collective-permute-start(bf16[2,128,512]{2,1,0:T(8,128)(2,1)S(1)} %add.84), channel_id=1, source_target_pairs={{0,128},{16,144},{32,160},{48,176},{64,192},{80,208},{96,224},{112... | collective-permute-start | bytes 786440 | tf_op jit(solution)/shard_map/ppermute | solution.py:86
  58.6 3.8 collective-permute-start.4
  62.4 5.1 %collective-permute-start.5 = (f32[2,256,1]{1,0,2:T(2,128)S(1)}, f32[2,256,1]{1,0,2:T(2,128)S(1)}, u32[]{:S(2)}, u32[]{:S(2)}) collective-permute-start(f32[2,256,1]{1,0,2:T(2,128)S(1)} %bitcast_add_fusion.1), channel_id=1, source_target_pairs={{0,2},{1,3},{2,0},{3,1},{4,6},{5,7},{6,4},{7,5},{8,10},{9,11},{10,... | collective-permute-start | bytes 6152 | tf_op jit(solution)/shard_map/ppermute | solution.py:70
  67.5 6.5 %collective-permute-start.6 = (f32[2,256,1]{1,0,2:T(2,128)S(1)}, f32[2,256,1]{1,0,2:T(2,128)S(1)}, u32[]{:S(2)}, u32[]{:S(2)}) collective-permute-start(f32[2,256,1]{1,0,2:T(2,128)S(1)} %add.88), channel_id=1, source_target_pairs={{0,4},{1,5},{2,6},{3,7},{4,0},{5,1},{6,2},{7,3},{8,12},{9,13},{10,... | collective-permute-start | bytes 6152 | tf_op jit(solution)/shard_map/ppermute | solution.py:70
  74.0 4.6 %collective-permute-start.7 = (f32[2,256,1]{1,0,2:T(2,128)S(1)}, f32[2,256,1]{1,0,2:T(2,128)S(1)}, u32[]{:S(2)}, u32[]{:S(2)}) collective-permute-start(f32[2,256,1]{1,0,2:T(2,128)S(1)} %add.89), channel_id=1, source_target_pairs={{0,8},{1,9},{2,10},{3,11},{4,12},{5,13},{6,14},{7,15},{8,0},{9,1},... | collective-permute-start | bytes 6152 | tf_op jit(solution)/shard_map/ppermute | solution.py:70
  209.2 238.9 %reduce-scatter.2.cloned.1.call-start = ((), (), s32[]{:S(2)}) async-start(), calls=%async_computation.3 | async-start | bytes 8912896 | tf_op jit(solution)/shard_map/reduce_scatter | solution.py:181
  324.3 5.3 %collective-permute-start.8 = (bf16[2,1,256,128]{2,3,0,1:T(8,128)(2,1)S(1)}, bf16[2,1,256,128]{2,3,0,1:T(8,128)(2,1)S(1)}, u32[]{:S(2)}, u32[]{:S(2)}) collective-permute-start(bf16[2,1,256,128]{2,3,0,1:T(8,128)(2,1)S(1)} %fusion.21), channel_id=1, source_target_pairs={{0,1},{1,0},{2,3},{3,2},{4,5},{5,4},{6,7},{7,6},{8,9},{9,8},{10,11... | collective-permute-start | bytes 393224 | tf_op jit(solution)/shard_map/ppermute | solution.py:159
Sparse Core Ops, SparseCore 0:
  11.1 197.9 all-gather.2
  210.9 98.3 all-gather.4
  343.5 104.5 reduce-scatter.1
